TPU v7x, 256 devices: a whole 4x4x8 slice. The times are simulated.
256 devices in a mesh: dp: 4 (over x), expert: 64 (over z, y, core).
Axes of the slice: x: 4, y: 4, z: 8, core: 2. Of those that a mesh axis runs over, the one named last changes fastest.
Arguments:
- tokens: bfloat16 [32768, 4096], P(('dp', 'expert')), may hold values from -6 to 6
- out_grad: bfloat16 [32768, 4096], P(('dp', 'expert')), may hold values from -0.75 to 0.75
- routes: int32 [32768, 1], P(('dp', 'expert')), may hold values from 0 to 63; in each aligned block of 128 rows (0 to 127, 128 to 255, ...) at most 3 rows name the same one
- gate_probs: bfloat16 [32768, 1], P(('dp', 'expert')), may hold values from 0.049804688 to 1
- w_gate: bfloat16 [64, 4096, 768], P('expert', None, 'dp'), may hold values from -0.09375 to 0.09375
- w_up: bfloat16 [64, 4096, 768], P('expert', None, 'dp'), may hold values from -0.09375 to 0.09375
- w_down: bfloat16 [64, 768, 4096], P('expert', 'dp'), may hold values from -0.21875 to 0.21875
Outputs:
- grad_tokens: bfloat16 [32768, 4096], P(('dp', 'expert'))
- grad_probs: bfloat16 [32768, 1], P(('dp', 'expert'))
- grad_w_gate: bfloat16 [64, 4096, 768], P('expert', None, 'dp')
- grad_w_up: bfloat16 [64, 4096, 768], P('expert', None, 'dp')
- grad_w_down: bfloat16 [64, 768, 4096], P('expert', 'dp')
Inputs may be any that keep to these rules, and one draw needn't show every extreme that they name: `routes`: the experts of one token are different. Among the 128 tokens of one device no expert is named more than 3 times, a bound that some block reaches.
All inputs are finite; a program needn't handle non-finite values.
Results may differ from a plain program's by a relative error of at most 0.018.
Values may be sent and summed in bfloat16 or wider, within the bound.
No kernel may reach another device: no remote copies, remote signals or barrier semaphores. Data moves between devices by JAX's collectives and lax.ppermute only.
A program may use at most 128 MiB of HBM per device.

v0:
```python
import jax
import jax.numpy as jnp
from jax import lax
from jax.sharding import PartitionSpec as P


def body(tokens, out_grad, routes, gate_probs, w_gate, w_up, w_down):
    expert_count = lax.axis_size("expert")
    tok_count, width = tokens.shape
    top_count = routes.shape[1]
    capacity = 3 * tok_count * top_count // (2 * expert_count)
    slot_total = expert_count * capacity
    flat_routes = routes.reshape(-1)
    one_hot = (flat_routes[:, None] == jnp.arange(expert_count, dtype=jnp.int32)[None, :]).astype(
        jnp.int32
    )
    earlier = jnp.cumsum(one_hot, axis=0) - one_hot
    slot_index = jnp.sum(earlier * one_hot, axis=1)
    destination = flat_routes * capacity + slot_index
    placing = (jnp.arange(slot_total, dtype=jnp.int32)[:, None] == destination[None, :]).astype(
        jnp.bfloat16
    )
    collect = jnp.sum(placing.reshape(slot_total, tok_count, top_count), axis=2)
    sent_in = (
        jnp.dot(collect, tokens, preferred_element_type=jnp.float32)
        .astype(jnp.bfloat16)
        .reshape(expert_count, capacity, width)
    )
    sent_dy = (
        jnp.dot(collect, out_grad, preferred_element_type=jnp.float32)
        .astype(jnp.bfloat16)
        .reshape(expert_count, capacity, width)
    )
    sent_prob = (
        jnp.dot(placing, gate_probs.reshape(-1), preferred_element_type=jnp.float32)
        .astype(jnp.bfloat16)
        .reshape(expert_count, capacity)
    )
    recv_in, recv_dy, recv_prob = (
        lax.all_to_all(sent_in, "expert", split_axis=0, concat_axis=0, tiled=True),
        lax.all_to_all(sent_dy, "expert", split_axis=0, concat_axis=0, tiled=True),
        lax.all_to_all(sent_prob, "expert", split_axis=0, concat_axis=0, tiled=True),
    )
    all_in, all_dy, all_prob = (
        lax.all_gather(recv_in, "dp", axis=0, tiled=True),
        lax.all_gather(recv_dy, "dp", axis=0, tiled=True),
        lax.all_gather(recv_prob, "dp", axis=0, tiled=True),
    )
    row_total = all_in.shape[0] * capacity
    rows_in = all_in.reshape(row_total, width)
    rows_dy = all_dy.reshape(row_total, width)
    rows_prob = all_prob.reshape(row_total)
    gate_w = w_gate[0]
    up_w = w_up[0]
    down_w = w_down[0]
    contract_last = (((1,), (1,)), ((), ()))
    contract_first = (((0,), (0,)), ((), ()))
    gate_pre = jnp.dot(rows_in, gate_w, preferred_element_type=jnp.float32)
    up_pre = jnp.dot(rows_in, up_w, preferred_element_type=jnp.float32)
    sigmoid_gate = jax.nn.sigmoid(gate_pre)
    active = gate_pre * sigmoid_gate
    hidden = (active * up_pre).astype(jnp.bfloat16)
    back_raw = lax.dot_general(rows_dy, down_w, contract_last, preferred_element_type=jnp.float32)
    weight_col = rows_prob.astype(jnp.float32)[:, None]
    scaled = (weight_col * rows_dy.astype(jnp.float32)).astype(jnp.bfloat16)
    grad_down = lax.dot_general(
        hidden, scaled, contract_first, preferred_element_type=jnp.float32
    ).astype(jnp.bfloat16)
    back_hidden = weight_col * back_raw
    grad_gate_pre = (
        back_hidden * up_pre * sigmoid_gate * (1.0 + gate_pre * (1.0 - sigmoid_gate))
    ).astype(jnp.bfloat16)
    grad_up_pre = (back_hidden * active).astype(jnp.bfloat16)
    grad_gate = lax.dot_general(
        rows_in, grad_gate_pre, contract_first, preferred_element_type=jnp.float32
    ).astype(jnp.bfloat16)
    grad_up = lax.dot_general(
        rows_in, grad_up_pre, contract_first, preferred_element_type=jnp.float32
    ).astype(jnp.bfloat16)
    row_part = lax.dot_general(
        grad_gate_pre, gate_w, contract_last, preferred_element_type=jnp.float32
    )
    row_part = row_part + lax.dot_general(
        grad_up_pre, up_w, contract_last, preferred_element_type=jnp.float32
    )
    own_rows = lax.psum_scatter(
        row_part.astype(jnp.bfloat16), "dp", scatter_dimension=0, tiled=True
    )
    outputs = jnp.dot(hidden, down_w, preferred_element_type=jnp.float32)
    own_out = lax.psum_scatter(
        outputs.astype(jnp.bfloat16), "dp", scatter_dimension=0, tiled=True
    ).astype(jnp.float32)
    own_dy = recv_dy.reshape(slot_total, width).astype(jnp.float32)
    scores = jnp.sum(own_out * own_dy, axis=1)
    back_rows, back_scores = (
        lax.all_to_all(
            own_rows.reshape(expert_count, capacity, width),
            "expert",
            split_axis=0,
            concat_axis=0,
            tiled=True,
        ),
        lax.all_to_all(
            scores.astype(jnp.bfloat16).reshape(expert_count, capacity),
            "expert",
            split_axis=0,
            concat_axis=0,
            tiled=True,
        ),
    )
    grad_tokens = lax.dot_general(
        collect,
        back_rows.reshape(slot_total, width),
        contract_first,
        preferred_element_type=jnp.float32,
    ).astype(jnp.bfloat16)
    grad_probs = (
        jnp.dot(back_scores.reshape(slot_total), placing, preferred_element_type=jnp.float32)
        .astype(jnp.bfloat16)
        .reshape(tok_count, top_count)
    )
    return (grad_tokens, grad_probs, grad_gate[None], grad_up[None], grad_down[None])


def solution(mesh):
    in_specs = (
        P(("dp", "expert"), None),
        P(("dp", "expert"), None),
        P(("dp", "expert"), None),
        P(("dp", "expert"), None),
        P("expert", None, "dp"),
        P("expert", None, "dp"),
        P("expert", "dp", None),
    )
    out_specs = (
        P(("dp", "expert"), None),
        P(("dp", "expert"), None),
        P("expert", None, "dp"),
        P("expert", None, "dp"),
        P("expert", "dp", None),
    )
    return jax.shard_map(body, mesh=mesh, in_specs=in_specs, out_specs=out_specs, check_vma=False)
```

profile of v0, /device:TPU:8, one launch (start us, length us, event | category | flops | bytes accessed | tf_op | source)
XLA Modules:
  0.0 471.2 jit_solution(15526037392462060360)
XLA Ops:
  13.9 63.3 %all_to_all.34 = bf16[64,3,4096]{2,1,0:T(4,128)(2,1)S(1)} all-to-all(bf16[64,3,4096]{2,1,0:T(4,128)(2,1)} %reshape.100), channel_id=1, replica_groups=mesh['dp'=4,'expert'=64] {'expert'}, dimensions={0} | all-to-all | bytes 3145728 | tf_op jit(solution)/shard_map/all_to_all | solution.py:41
  85.1 56.7 %all_to_all.35 = bf16[64,3,4096]{2,1,0:T(4,128)(2,1)S(1)} all-to-all(bf16[64,3,4096]{2,1,0:T(4,128)(2,1)} %reshape.102), channel_id=1, replica_groups=mesh['dp'=4,'expert'=64] {'expert'}, dimensions={0} | all-to-all | bytes 3145728 | tf_op jit(solution)/shard_map/all_to_all | solution.py:40
  144.4 13.9 %all_to_all.36 = bf16[64,1,3]{2,1,0:T(2,128)(2,1)S(1)} all-to-all(bf16[64,1,3]{2,1,0:T(2,128)(2,1)S(1)} %all_to_all.28), channel_id=1, replica_groups=mesh['dp'=4,'expert'=64] {'expert'}, dimensions={0} | all-to-all | bytes 768 | tf_op jit(solution)/shard_map/all_to_all | solution.py:42
  158.3 13.5 %all-gather = bf16[256,1,3]{2,1,0:T(2,128)(2,1)S(1)} all-gather(bf16[64,1,3]{2,1,0:T(2,128)(2,1)S(1)} %all_to_all.36), channel_id=2, replica_groups=mesh['dp'=4,'expert'=64] {'dp'}, dimensions={0}, use_global_device_ids=true | all-gather | bytes 1920 | tf_op jit(solution)/shard_map/all_gather | solution.py:47
  172.4 11.5 %copy.20 = bf16[256,3,4096]{2,1,0:T(4,128)(2,1)} copy(bf16[256,3,4096]{2,0,1:T(8,128)(2,1)} %all-gather.4.cloned.1.call-done) | data formatting | bytes 12582912 | tf_op jit(solution)/shard_map/all_gather | solution.py:46
  183.9 13.7 %reshape.101 = bf16[768,4096]{1,0:T(8,128)(2,1)} reshape(bf16[256,3,4096]{2,1,0:T(4,128)(2,1)} %copy.20) | data formatting | bytes 12582912 | tf_op jit(solution)/shard_map/reshape | solution.py:51
  197.6 19.7 %all-gather.6.cloned.1.call-done = bf16[256,3,4096]{2,0,1:T(8,128)(2,1)} async-done(((bf16[64,3,4096]{2,0,1:T(8,128)(2,1)}), bf16[256,3,4096]{2,0,1:T(8,128)(2,1)}) %all-gather.6.cloned.1.call-update) | async-done | bytes 6291472 | tf_op jit(solution)/shard_map/all_gather | solution.py:45
  217.3 11.5 %copy.22 = bf16[256,3,4096]{2,1,0:T(4,128)(2,1)} copy(bf16[256,3,4096]{2,0,1:T(8,128)(2,1)} %all-gather.6.cloned.1.call-done) | data formatting | bytes 12582912 | tf_op jit(solution)/shard_map/all_gather | solution.py:45
  228.8 14.0 %reshape.103 = bf16[768,4096]{1,0:T(8,128)(2,1)} reshape(bf16[256,3,4096]{2,1,0:T(4,128)(2,1)} %copy.22) | data formatting | bytes 12582912 | tf_op jit(solution)/shard_map/reshape | solution.py:50
  242.8 5.6 %fusion.8 = f32[768,192]{0,1:T(8,128)S(1)} fusion(bf16[768,4096]{1,0:T(8,128)(2,1)} %reshape.103, bf16[1,4096,192]{1,2,0:T(8,128)(2,1)} %param.11), kind=kOutput, calls=%fused_computation.17 | convolution fusion | flops 1207959552 | bytes 8454144 | tf_op jit(solution)/shard_map/dot_general | solution.py:58
  250.7 3.2 multiply_convert_fusion.6
  253.9 4.5 convolution_convert_fusion
  259.8 2.8 fusion.6
  262.6 4.5 add_convert_fusion
  267.2 4.6 reshape.109
  271.8 53.2 %reduce-scatter.5.cloned.1.call-done = bf16[192,4096]{1,0:T(8,128)(2,1)} async-done(((bf16[768,4096]{1,0:T(8,128)(2,1)}), bf16[192,4096]{1,0:T(8,128)(2,1)}) %reduce-scatter.5.cloned.1.call-update) | async-done | bytes 1572880 | tf_op jit(solution)/shard_map/reduce_scatter | solution.py:90
  328.6 10.9 %all-to-all-start.4 = ((bf16[64,1,3]{2,1,0:T(2,128)(2,1)}), bf16[64,1,3]{2,1,0:T(2,128)(2,1)S(1)}, u32[]{:S(2)}, u32[]{:S(2)}) async-start(bf16[64,1,3]{2,1,0:T(2,128)(2,1)} %convert_element_type.121), calls=%async_computation.6 | async-start | bytes 65536 | tf_op jit(solution)/shard_map/all_to_all | solution.py:103
  339.5 54.3 %reduce-scatter.3.cloned.1.call-done = bf16[192,4096]{1,0:T(8,128)(2,1)} async-done(((bf16[768,4096]{1,0:T(8,128)(2,1)}), bf16[192,4096]{1,0:T(8,128)(2,1)}) %reduce-scatter.3.cloned.1.call-update) | async-done | bytes 1572880 | tf_op jit(solution)/shard_map/reduce_scatter | solution.py:86
  393.8 4.1 reshape.104
  397.9 10.7 %all-to-all-start.3 = ((bf16[64,3,4096]{2,1,0:T(4,128)(2,1)}), bf16[64,3,4096]{2,1,0:T(4,128)(2,1)}, u32[]{:S(2)}, u32[]{:S(2)}) async-start(bf16[64,3,4096]{2,1,0:T(4,128)(2,1)} %reshape.104), calls=%async_computation.4 | async-start | bytes 4194304 | tf_op jit(solution)/shard_map/all_to_all | solution.py:96
  408.7 5.5 %fusion.3 = bf16[1,4096,192]{1,2,0:T(8,128)(2,1)} fusion(bf16[768,192]{0,1:T(8,128)(2,1)S(1)} %copy-done.7, bf16[768,4096]{1,0:T(8,128)(2,1)} %reshape.103), kind=kOutput, calls=%fused_computation.11 | convolution fusion | flops 1208745984 | bytes 8159232 | tf_op jit(solution)/shard_map/dot_general | solution.py:74
  414.2 5.5 %fusion.4 = bf16[1,4096,192]{1,2,0:T(8,128)(2,1)} fusion(bf16[768,192]{0,1:T(8,128)(2,1)S(1)} %copy-done.6, bf16[768,4096]{1,0:T(8,128)(2,1)} %reshape.103), kind=kOutput, calls=%fused_computation.12 | convolution fusion | flops 1208745984 | bytes 8159232 | tf_op jit(solution)/shard_map/dot_general | solution.py:77
  423.3 36.5 %all-to-all-done.3 = bf16[64,3,4096]{2,1,0:T(4,128)(2,1)} async-done(((bf16[64,3,4096]{2,1,0:T(4,128)(2,1)}), bf16[64,3,4096]{2,1,0:T(4,128)(2,1)}, u32[]{:S(2)}, u32[]{:S(2)}) %all-to-all-start.3) | async-done | bytes 1572896 | tf_op jit(solution)/shard_map/all_to_all | solution.py:96
  459.8 3.1 reshape.105
  (61 shorter events, 30.0 us)
Async XLA Ops:
  7.2 243.5 %copy-start = (bf16[1,4096,192]{1,2,0:T(8,128)(2,1)S(1)}, bf16[1,4096,192]{1,2,0:T(8,128)(2,1)}, u32[]{:S(2)}) copy-start(bf16[1,4096,192]{1,2,0:T(8,128)(2,1)} %param.12) | copy-start | bytes 4718596
  7.2 165.2 %all-gather.4.cloned.1.call-start = ((), (), s32[]{:S(2)}) async-start(), calls=%async_computation.7 | async-start | bytes 7864320 | tf_op jit(solution)/shard_map/all_gather | solution.py:46
  77.2 1.3 copy-start.1
  80.9 136.5 %all-gather.6.cloned.1.call-start = ((), (), s32[]{:S(2)}) async-start(), calls=%async_computation.8 | async-start | bytes 7864320 | tf_op jit(solution)/shard_map/all_gather | solution.py:45
  141.7 2.4 copy-start.8
  144.0 181.0 %reduce-scatter.5.cloned.1.call-start = ((), (), s32[]{:S(2)}) async-start(), calls=%async_computation.10 | async-start | bytes 7864320 | tf_op jit(solution)/shard_map/reduce_scatter | solution.py:90
  228.8 19.6 %copy-start.3 = (bf16[1,192,4096]{2,1,0:T(8,128)(2,1)S(1)}, bf16[1,192,4096]{2,1,0:T(8,128)(2,1)}, u32[]{:S(2)}) copy-start(bf16[1,192,4096]{2,1,0:T(8,128)(2,1)} %param.13) | copy-start | bytes 4718596
  242.8 5.6 %copy-start.2 = (bf16[768,4096]{1,0:T(8,128)(2,1)S(1)}, bf16[768,4096]{1,0:T(8,128)(2,1)}, u32[]{:S(2)}) copy-start(bf16[768,4096]{1,0:T(8,128)(2,1)} %reshape.101) | copy-start | bytes 18874372
  242.8 7.9 %slice-start.2 = ((s8[6291456]{0:T(1024)(128)(4,1)}), s8[4194304]{0:T(1024)(128)(4,1)S(1)}, s32[]{:S(2)}) async-start(s8[6291456]{0:T(1024)(128)(4,1)} %bitcast.55), calls=%async_computation.13 | async-start | bytes 8388608
  248.4 2.3 slice-start.3
  258.4 1.4 copy-start.4
  258.4 135.4 %reduce-scatter.3.cloned.1.call-start = ((), (), s32[]{:S(2)}) async-start(), calls=%async_computation.9 | async-start | bytes 7864320 | tf_op jit(solution)/shard_map/reduce_scatter | solution.py:86
  259.8 2.8 copy-start.5
  328.6 69.3 %all-to-all-start.4 = ((bf16[64,1,3]{2,1,0:T(2,128)(2,1)}), bf16[64,1,3]{2,1,0:T(2,128)(2,1)S(1)}, u32[]{:S(2)}, u32[]{:S(2)}) async-start(bf16[64,1,3]{2,1,0:T(2,128)(2,1)} %convert_element_type.121), calls=%async_computation.6 | async-start | bytes 65536 | tf_op jit(solution)/shard_map/all_to_all | solution.py:103
  339.5 69.2 %copy-start.7 = (bf16[768,192]{0,1:T(8,128)(2,1)S(1)}, bf16[768,192]{0,1:T(8,128)(2,1)}, u32[]{:S(2)}) copy-start(bf16[768,192]{0,1:T(8,128)(2,1)} %get-tuple-element.6) | copy-start | bytes 884740
  397.9 61.9 %all-to-all-start.3 = ((bf16[64,3,4096]{2,1,0:T(4,128)(2,1)}), bf16[64,3,4096]{2,1,0:T(4,128)(2,1)}, u32[]{:S(2)}, u32[]{:S(2)}) async-start(bf16[64,3,4096]{2,1,0:T(4,128)(2,1)} %reshape.104), calls=%async_computation.4 | async-start | bytes 4194304 | tf_op jit(solution)/shard_map/all_to_all | solution.py:96
  408.7 5.5 %copy-start.6 = (bf16[768,192]{0,1:T(8,128)(2,1)S(1)}, bf16[768,192]{0,1:T(8,128)(2,1)}, u32[]{:S(2)}) copy-start(bf16[768,192]{0,1:T(8,128)(2,1)} %get-tuple-element.7) | copy-start | bytes 884740
  408.7 11.0 %slice-start = ((s8[6291456]{0:T(1024)(128)(4,1)}), s8[4194304]{0:T(1024)(128)(4,1)S(1)}, s32[]{:S(2)}) async-start(s8[6291456]{0:T(1024)(128)(4,1)} %bitcast.53), calls=%async_computation.11 | async-start | bytes 8388608
  414.2 5.5 %slice-start.1 = ((s8[6291456]{0:T(1024)(128)(4,1)}), s8[2097152]{0:T(1024)(128)(4,1)S(1)}, s32[]{:S(2)}) async-start(s8[6291456]{0:T(1024)(128)(4,1)} %bitcast.53), calls=%async_computation.12 | async-start | bytes 4194304
Sparse Core Ops, SparseCore 0:
  81.0 64.3 all-gather.3
  147.8 69.5 all-gather.5
  258.5 66.4 reduce-scatter.4
  327.5 66.2 reduce-scatter.2
where the time goes:
time: 478 us; the launch traced here: 471 us
  waiting for transfers between devices  164 us (34%)
  blocking collectives  147 us (31%)
  local copies, waits for them, and re-layouts  75.9 us (16%)
  matrix products  42.4 us (9%)
  starting transfers between devices  21.7 us (5%)
  between operations  14.2 us (3%)
  other arithmetic  5.74 us (1%)
    all_to_all x1, blocking collectives, body(): lax.all_to_all(sent_dy, 'expert', split_axis=0, concat_axis=0, tiled=True)  63.3 us
    all_to_all x1, blocking collectives, body(): lax.all_to_all(sent_in, 'expert', split_axis=0, concat_axis=0, tiled=True)  56.7 us
    reduce_scatter x1, waiting for transfers between devices, body(): lax.psum_scatter(row_part.astype(jnp.bfloat16), 'dp', scatter_dimension=0...  54.3 us
    reduce_scatter x1, waiting for transfers between devices, body(): lax.psum_scatter(outputs.astype(jnp.bfloat16), 'dp', scatter_dimension=0,...  53.2 us
    all_to_all x1, waiting for transfers between devices, body(): lax.all_to_all(own_rows.reshape(expert_count, capacity, width), 'expert',...  36.5 us
    all_gather x1, waiting for transfers between devices, body(): lax.all_gather(recv_in, 'dp', axis=0, tiled=True)  19.7 us
    reshape x1, local copies, waits for them, and re-layouts, body(): rows_in = all_in.reshape(row_total, width)  14 us
    all_to_all x1, blocking collectives, body(): lax.all_to_all(sent_prob, 'expert', split_axis=0, concat_axis=0, tiled=True)  13.9 us
  transfers between devices with their start and end apart: 6, of which 4 were waited for; matrix products, arithmetic and copies ran while one was open for 14% of the time, Pallas kernels for 0%

commit v1 on v0

v1 whole, which is shorter than its diff:
```python
import jax
import jax.numpy as jnp
from jax import lax
from jax.sharding import PartitionSpec as P

LANES = 128


def body(tokens, out_grad, routes, gate_probs, w_gate, w_up, w_down):
    expert_count = lax.axis_size("expert")
    tok_count, width = tokens.shape
    top_count = routes.shape[1]
    capacity = 3 * tok_count * top_count // (2 * expert_count)
    slot_total = expert_count * capacity
    per_peer = capacity * width // LANES
    flat_routes = routes.reshape(-1)
    one_hot = (flat_routes[:, None] == jnp.arange(expert_count, dtype=jnp.int32)[None, :]).astype(
        jnp.int32
    )
    earlier = jnp.cumsum(one_hot, axis=0) - one_hot
    slot_index = jnp.sum(earlier * one_hot, axis=1)
    destination = flat_routes * capacity + slot_index
    placing = (jnp.arange(slot_total, dtype=jnp.int32)[:, None] == destination[None, :]).astype(
        jnp.bfloat16
    )
    collect = jnp.sum(placing.reshape(slot_total, tok_count, top_count), axis=2)
    sent_in = (
        jnp.dot(collect, tokens, preferred_element_type=jnp.float32)
        .astype(jnp.bfloat16)
        .reshape(expert_count, per_peer, LANES)
    )
    sent_dy = (
        jnp.dot(collect, out_grad, preferred_element_type=jnp.float32)
        .astype(jnp.bfloat16)
        .reshape(expert_count, per_peer, LANES)
    )
    sent_prob = (
        jnp.dot(placing, gate_probs.reshape(-1), preferred_element_type=jnp.float32)
        .astype(jnp.bfloat16)
        .reshape(expert_count, capacity)
    )
    recv_in = lax.all_to_all(sent_in, "expert", 0, 0, tiled=True).reshape(slot_total, width)
    recv_dy = lax.all_to_all(sent_dy, "expert", 0, 0, tiled=True).reshape(slot_total, width)
    recv_prob = lax.all_to_all(sent_prob, "expert", 0, 0, tiled=True).reshape(slot_total)
    dy_ext = jnp.concatenate(
        [recv_dy, jnp.broadcast_to(recv_prob[:, None], (slot_total, LANES))], axis=1
    )
    rows_in = lax.all_gather(recv_in, "dp", axis=0, tiled=True)
    rows_dy_ext = lax.all_gather(dy_ext, "dp", axis=0, tiled=True)
    rows_dy = rows_dy_ext[:, :width]
    rows_prob = rows_dy_ext[:, width]
    gate_w = w_gate[0]
    up_w = w_up[0]
    down_w = w_down[0]
    contract_last = (((1,), (1,)), ((), ()))
    contract_first = (((0,), (0,)), ((), ()))
    gate_pre = jnp.dot(rows_in, gate_w, preferred_element_type=jnp.float32)
    up_pre = jnp.dot(rows_in, up_w, preferred_element_type=jnp.float32)
    sigmoid_gate = jax.nn.sigmoid(gate_pre)
    active = gate_pre * sigmoid_gate
    hidden = (active * up_pre).astype(jnp.bfloat16)
    back_raw = lax.dot_general(rows_dy, down_w, contract_last, preferred_element_type=jnp.float32)
    score_part = jnp.sum(back_raw * hidden.astype(jnp.float32), axis=1)
    weight_col = rows_prob.astype(jnp.float32)[:, None]
    scaled = (weight_col * rows_dy.astype(jnp.float32)).astype(jnp.bfloat16)
    back_hidden = weight_col * back_raw
    grad_gate_pre = (
        back_hidden * up_pre * sigmoid_gate * (1.0 + gate_pre * (1.0 - sigmoid_gate))
    ).astype(jnp.bfloat16)
    grad_up_pre = (back_hidden * active).astype(jnp.bfloat16)
    row_part = lax.dot_general(
        grad_gate_pre, gate_w, contract_last, preferred_element_type=jnp.float32
    )
    row_part = row_part + lax.dot_general(
        grad_up_pre, up_w, contract_last, preferred_element_type=jnp.float32
    )
    row_total = row_part.shape[0]
    row_ext = jnp.concatenate(
        [row_part, jnp.broadcast_to(score_part[:, None], (row_total, LANES))], axis=1
    ).astype(jnp.bfloat16)
    own_ext = lax.psum_scatter(row_ext, "dp", scatter_dimension=0, tiled=True)
    grad_down = lax.dot_general(
        hidden, scaled, contract_first, preferred_element_type=jnp.float32
    ).astype(jnp.bfloat16)
    grad_gate = lax.dot_general(
        rows_in, grad_gate_pre, contract_first, preferred_element_type=jnp.float32
    ).astype(jnp.bfloat16)
    grad_up = lax.dot_general(
        rows_in, grad_up_pre, contract_first, preferred_element_type=jnp.float32
    ).astype(jnp.bfloat16)
    own_rows = own_ext[:, :width].reshape(expert_count, per_peer, LANES)
    own_scores = own_ext[:, width].reshape(expert_count, capacity)
    back_rows = lax.all_to_all(own_rows, "expert", 0, 0, tiled=True).reshape(slot_total, width)
    back_scores = lax.all_to_all(own_scores, "expert", 0, 0, tiled=True).reshape(slot_total)
    grad_tokens = lax.dot_general(
        collect, back_rows, contract_first, preferred_element_type=jnp.float32
    ).astype(jnp.bfloat16)
    grad_probs = (
        jnp.dot(back_scores, placing, preferred_element_type=jnp.float32)
        .astype(jnp.bfloat16)
        .reshape(tok_count, top_count)
    )
    return (grad_tokens, grad_probs, grad_gate[None], grad_up[None], grad_down[None])


def solution(mesh):
    in_specs = (
        P(("dp", "expert"), None),
        P(("dp", "expert"), None),
        P(("dp", "expert"), None),
        P(("dp", "expert"), None),
        P("expert", None, "dp"),
        P("expert", None, "dp"),
        P("expert", "dp", None),
    )
    out_specs = (
        P(("dp", "expert"), None),
        P(("dp", "expert"), None),
        P("expert", None, "dp"),
        P("expert", None, "dp"),
        P("expert", "dp", None),
    )
    return jax.shard_map(body, mesh=mesh, in_specs=in_specs, out_specs=out_specs, check_vma=False)
```

time: 478 us -> 371 us (0.78); the launches traced: 471 us -> 370 us
  blocking collectives: 147 us -> 52 us
  local copies, waits for them, and re-layouts: 75.9 us -> 17.8 us
  waiting for transfers between devices: 164 us -> 207 us
  starting transfers between devices: 21.7 us -> 27.5 us
    all_to_all x3 -> x1, blocking collectives: 134 us -> 52 us  [body(): lax.all_to_all(sent_in, 'expert', 0, 0, tiled=True)]
    all_gather x2, waiting for transfers between devices: 19.7 us -> 62 us  [the longest x1 62 us: body(): rows_dy_ext = lax.all_gather(dy_ext, 'dp', axis=0, tiled=True)]
    all_to_all x2 -> x4, waiting for transfers between devices: 36.5 us -> 76.3 us  [the longest x1 39.8 us: body(): lax.all_to_all(sent_dy, 'expert', 0, 0, tiled=True)]
    reduce_scatter x2 -> x1, waiting for transfers between devices: 108 us -> 69 us  [body(): own_ext = lax.psum_scatter(row_ext, 'dp', scatter_dimension=0, tiled=True)]
    reshape x5, local copies, waits for them, and re-layouts: 35 us -> 10.1 us  [the longest x1 3.69 us: body(): lax.all_to_all(sent_in, 'expert', 0, 0, tiled=True)]
    all_gather x2 -> x0, local copies, waits for them, and re-layouts: 23 us -> none  [the longest x1 11.5 us: body(): lax.all_gather(recv_dy, 'dp', axis=0, tiled=True)]
    all_gather x1 -> x0, blocking collectives: 13.5 us -> none  [body(): lax.all_gather(recv_prob, 'dp', axis=0, tiled=True)]
    concatenate x0 -> x2, other arithmetic: none -> 5.98 us  [the longest x1 3.25 us: body(): jnp.concatenate([row_part, jnp.broadcast_to(score_part[:, None], (row_tot...]
  transfers between devices with their start and end apart: 6 -> 7, of which waited for: 4 -> 6; matrix products, arithmetic and copies ran while one was open for 14% -> 9% of each run, Pallas kernels for 0% -> 0%
where the time goes in v1:
time: 371 us; the launch traced here: 370 us
  waiting for transfers between devices  207 us (56%)
  blocking collectives  52 us (14%)
  matrix products  41.4 us (11%)
  starting transfers between devices  27.5 us (7%)
  local copies, waits for them, and re-layouts  17.8 us (5%)
  between operations  14 us (4%)
  other arithmetic  9.76 us (3%)
    reduce_scatter x1, waiting for transfers between devices, body(): own_ext = lax.psum_scatter(row_ext, 'dp', scatter_dimension=0, tiled=True)  69 us
    all_gather x1, waiting for transfers between devices, body(): rows_dy_ext = lax.all_gather(dy_ext, 'dp', axis=0, tiled=True)  62 us
    all_to_all x1, blocking collectives, body(): lax.all_to_all(sent_in, 'expert', 0, 0, tiled=True)  52 us
    all_to_all x1, waiting for transfers between devices, body(): lax.all_to_all(sent_dy, 'expert', 0, 0, tiled=True)  39.8 us
    all_to_all x1, waiting for transfers between devices, body(): lax.all_to_all(own_rows, 'expert', 0, 0, tiled=True)  25.5 us
    all_to_all x1, starting transfers between devices, body(): lax.all_to_all(own_scores, 'expert', 0, 0, tiled=True).reshape(slot_total)  10.5 us
  transfers between devices with their start and end apart: 7, of which 6 were waited for; matrix products, arithmetic and copies ran while one was open for 9% of the time, Pallas kernels for 0%

profile of v1, /device:TPU:8, one launch (start us, length us, event | category | flops | bytes accessed | tf_op | source)
XLA Modules:
  0.0 369.8 jit_solution(16737061636005797935)
XLA Ops:
  9.8 2.9 convolution_convert_fusion.2
  12.7 2.6 reshape.82
  15.3 52.0 %all_to_all.35 = bf16[64,96,128]{2,1,0:T(8,128)(2,1)} all-to-all(bf16[64,96,128]{2,1,0:T(8,128)(2,1)S(1)} %reshape.82), channel_id=1, replica_groups=mesh['dp'=4,'expert'=64] {'expert'}, dimensions={0} | all-to-all | bytes 3145728 | tf_op jit(solution)/shard_map/all_to_all | solution.py:42
  67.3 3.7 reshape.83
  72.0 5.4 %all-to-all-start.1 = ((bf16[64,1,3]{2,1,0:T(2,128)(2,1)}), bf16[64,1,3]{2,1,0:T(2,128)(2,1)S(1)}, u32[]{:S(2)}, u32[]{:S(2)}) async-start(bf16[64,1,3]{2,1,0:T(2,128)(2,1)} %all_to_all.28), calls=%async_computation.1 | async-start | bytes 65536 | tf_op jit(solution)/shard_map/all_to_all | solution.py:44
  81.3 4.6 %all-to-all-done.1 = bf16[64,1,3]{2,1,0:T(2,128)(2,1)S(1)} async-done(((bf16[64,1,3]{2,1,0:T(2,128)(2,1)}), bf16[64,1,3]{2,1,0:T(2,128)(2,1)S(1)}, u32[]{:S(2)}, u32[]{:S(2)}) %all-to-all-start.1) | async-done | bytes 416 | tf_op jit(solution)/shard_map/all_to_all | solution.py:44
  86.0 5.6 %all-to-all-start = ((bf16[64,96,128]{2,1,0:T(8,128)(2,1)}), bf16[64,96,128]{2,1,0:T(8,128)(2,1)S(1)}, u32[]{:S(2)}, u32[]{:S(2)}) async-start(bf16[64,96,128]{2,1,0:T(8,128)(2,1)} %reshape.79), calls=%async_computation | async-start | bytes 3145728 | tf_op jit(solution)/shard_map/all_to_all | solution.py:43
  91.9 39.8 %all-to-all-done = bf16[64,96,128]{2,1,0:T(8,128)(2,1)S(1)} async-done(((bf16[64,96,128]{2,1,0:T(8,128)(2,1)}), bf16[64,96,128]{2,1,0:T(8,128)(2,1)S(1)}, u32[]{:S(2)}, u32[]{:S(2)}) %all-to-all-start) | async-done | bytes 1572896 | tf_op jit(solution)/shard_map/all_to_all | solution.py:43
  133.8 2.7 pad_maximum_fusion.1
  136.8 6.0 %fusion.11 = f32[768,192]{0,1:T(8,128)} fusion(bf16[768,4096]{1,0:T(8,128)(2,1)} %all-gather.5.cloned.1.call-done, bf16[1,4096,192]{1,2,0:T(8,128)(2,1)S(1)} %copy-done), kind=kOutput, calls=%fused_computation.20 | convolution fusion | flops 1207959552 | bytes 8454144 | tf_op jit(solution)/shard_map/dot_general | solution.py:57
  142.8 3.1 fusion.14
  145.9 62.0 %all-gather.3.cloned.1.call-done = bf16[768,4224]{1,0:T(8,128)(2,1)} async-done(((bf16[192,4224]{1,0:T(8,128)(2,1)}), bf16[768,4224]{1,0:T(8,128)(2,1)}) %all-gather.3.cloned.1.call-update) | async-done | bytes 6488080 | tf_op jit(solution)/shard_map/all_gather | solution.py:49
  208.9 6.6 %multiply_reduce_fusion = (bf16[768]{0:T(1024)(128)(2,1)S(1)}, bf16[768,192]{0,1:T(8,128)(2,1)}, bf16[768,192]{0,1:T(8,128)(2,1)S(1)}, bf16[768,192]{0,1:T(8,128)(2,1)S(1)}) fusion(f32[768,192]{0,1:T(8,128)} %fusion.14, f32[768,192]{0,1:T(8,128)} %fusion.11, f32[768]{0:T(1024)S(1)} %convert_reduce_fusion, bf16[1,192,4096]{2,1,0:T(8,128)(2,1)} %param.13, ...), kind=kOutput, calls=%fused_computation.29 | convolution fusion | flops 1210760448 | bytes 9933312 | tf_op jit(solution)/shard_map/dot_general | solution.py:62
  219.5 3.3 pad_maximum_fusion
  222.7 69.0 %reduce-scatter.2.cloned.1.call-done = bf16[192,4224]{1,0:T(8,128)(2,1)} async-done(((bf16[768,4224]{1,0:T(8,128)(2,1)}), bf16[192,4224]{1,0:T(8,128)(2,1)}) %reduce-scatter.2.cloned.1.call-update) | async-done | bytes 1622032 | tf_op jit(solution)/shard_map/reduce_scatter | solution.py:81
  293.5 10.5 %all-to-all-start.4 = ((bf16[64,1,3]{2,1,0:T(2,128)(2,1)}), bf16[64,1,3]{2,1,0:T(2,128)(2,1)S(1)}, u32[]{:S(2)}, u32[]{:S(2)}) async-start(bf16[64,1,3]{2,1,0:T(2,128)(2,1)} %all_to_all.29), calls=%async_computation.5 | async-start | bytes 65536 | tf_op jit(solution)/shard_map/all_to_all | solution.py:94
  304.1 2.1 reshape.84
  306.2 6.4 %all-to-all-done.4 = bf16[64,1,3]{2,1,0:T(2,128)(2,1)S(1)} async-done(((bf16[64,1,3]{2,1,0:T(2,128)(2,1)}), bf16[64,1,3]{2,1,0:T(2,128)(2,1)S(1)}, u32[]{:S(2)}, u32[]{:S(2)}) %all-to-all-start.4) | async-done | bytes 416 | tf_op jit(solution)/shard_map/all_to_all | solution.py:94
  312.6 5.6 %all-to-all-start.3 = ((bf16[64,96,128]{2,1,0:T(8,128)(2,1)}), bf16[64,96,128]{2,1,0:T(8,128)(2,1)S(1)}, u32[]{:S(2)}, u32[]{:S(2)}) async-start(bf16[64,96,128]{2,1,0:T(8,128)(2,1)} %reshape.84), calls=%async_computation.4 | async-start | bytes 3145728 | tf_op jit(solution)/shard_map/all_to_all | solution.py:93
  318.3 5.5 %fusion.6 = bf16[1,4096,192]{1,2,0:T(8,128)(2,1)} fusion(bf16[768,192]{0,1:T(8,128)(2,1)S(1)} %copy-done.4, bf16[768,4096]{1,0:T(8,128)(2,1)} %all-gather.5.cloned.1.call-done), kind=kOutput, calls=%fused_computation.14 | convolution fusion | flops 1208745984 | bytes 8159232 | tf_op jit(solution)/shard_map/dot_general | solution.py:85
  323.7 5.5 %fusion.7 = bf16[1,4096,192]{1,2,0:T(8,128)(2,1)} fusion(bf16[768,192]{0,1:T(8,128)(2,1)S(1)} %get-tuple-element.8, bf16[768,4096]{1,0:T(8,128)(2,1)} %all-gather.5.cloned.1.call-done), kind=kOutput, calls=%fused_computation.15 | convolution fusion | flops 1208745984 | bytes 8159232 | tf_op jit(solution)/shard_map/dot_general | solution.py:88
  329.2 2.7 fusion.8
  332.8 25.5 %all-to-all-done.3 = bf16[64,96,128]{2,1,0:T(8,128)(2,1)S(1)} async-done(((bf16[64,96,128]{2,1,0:T(8,128)(2,1)}), bf16[64,96,128]{2,1,0:T(8,128)(2,1)S(1)}, u32[]{:S(2)}, u32[]{:S(2)}) %all-to-all-start.3) | async-done | bytes 1572896 | tf_op jit(solution)/shard_map/all_to_all | solution.py:93
  360.4 2.9 convolution_convert_fusion.4
  (53 shorter events, 19.9 us)
Async XLA Ops:
  7.2 129.6 %copy-start = (bf16[1,4096,192]{1,2,0:T(8,128)(2,1)S(1)}, bf16[1,4096,192]{1,2,0:T(8,128)(2,1)}, u32[]{:S(2)}) copy-start(bf16[1,4096,192]{1,2,0:T(8,128)(2,1)} %param.11) | copy-start | bytes 4718596
  7.2 129.6 %all-gather.5.cloned.1.call-start = ((), (), s32[]{:S(2)}) async-start(), calls=%async_computation.7 | async-start | bytes 7864320 | tf_op jit(solution)/shard_map/all_gather | solution.py:48
  67.3 3.7 %copy-start.6 = (bf16[128,1]{0,1:T(2,128)(2,1)S(1)}, bf16[128,1]{0,1:T(2,128)(2,1)}, u32[]{:S(2)}) copy-start(bf16[128,1]{0,1:T(2,128)(2,1)} %param.10) | copy-start | bytes 772
  72.0 14.0 %all-to-all-start.1 = ((bf16[64,1,3]{2,1,0:T(2,128)(2,1)}), bf16[64,1,3]{2,1,0:T(2,128)(2,1)S(1)}, u32[]{:S(2)}, u32[]{:S(2)}) async-start(bf16[64,1,3]{2,1,0:T(2,128)(2,1)} %all_to_all.28), calls=%async_computation.1 | async-start | bytes 65536 | tf_op jit(solution)/shard_map/all_to_all | solution.py:44
  86.0 45.7 %all-to-all-start = ((bf16[64,96,128]{2,1,0:T(8,128)(2,1)}), bf16[64,96,128]{2,1,0:T(8,128)(2,1)S(1)}, u32[]{:S(2)}, u32[]{:S(2)}) async-start(bf16[64,96,128]{2,1,0:T(8,128)(2,1)} %reshape.79), calls=%async_computation | async-start | bytes 3145728 | tf_op jit(solution)/shard_map/all_to_all | solution.py:43
  91.6 116.2 %all-gather.3.cloned.1.call-start = ((), (), s32[]{:S(2)}) async-start(), calls=%async_computation.6 | async-start | bytes 8110080 | tf_op jit(solution)/shard_map/all_gather | solution.py:49
  136.5 6.3 %copy-start.2 = (bf16[1,4096,192]{1,2,0:T(8,128)(2,1)S(1)}, bf16[1,4096,192]{1,2,0:T(8,128)(2,1)}, u32[]{:S(2)}) copy-start(bf16[1,4096,192]{1,2,0:T(8,128)(2,1)} %param.12) | copy-start | bytes 4718596
  136.6 155.2 %reduce-scatter.2.cloned.1.call-start = ((), (), s32[]{:S(2)}) async-start(), calls=%async_computation.8 | async-start | bytes 8110080 | tf_op jit(solution)/shard_map/reduce_scatter | solution.py:81
  136.8 6.0 %copy-start.5 = (bf16[768,4096]{1,0:T(8,128)(2,1)S(1)}, bf16[768,4096]{1,0:T(8,128)(2,1)}, u32[]{:S(2)}) copy-start(bf16[768,4096]{1,0:T(8,128)(2,1)} %all-gather.5.cloned.1.call-done) | copy-start | bytes 18874372
  215.5 1.8 copy-start.3
  291.7 12.4 %slice-start = ((bf16[192,4224]{1,0:T(8,128)(2,1)}), bf16[192,4096]{1,0:T(8,128)(2,1)S(1)}, s32[]{:S(2)}) async-start(bf16[192,4224]{1,0:T(8,128)(2,1)} %reduce-scatter.2.cloned.1.call-done), calls=%async_computation.9 | async-start | bytes 3145728 | tf_op jit(solution)/shard_map/slice | solution.py:91
  293.5 19.1 %all-to-all-start.4 = ((bf16[64,1,3]{2,1,0:T(2,128)(2,1)}), bf16[64,1,3]{2,1,0:T(2,128)(2,1)S(1)}, u32[]{:S(2)}, u32[]{:S(2)}) async-start(bf16[64,1,3]{2,1,0:T(2,128)(2,1)} %all_to_all.29), calls=%async_computation.5 | async-start | bytes 65536 | tf_op jit(solution)/shard_map/all_to_all | solution.py:94
  306.2 12.0 %copy-start.4 = (bf16[768,192]{0,1:T(8,128)(2,1)S(1)}, bf16[768,192]{0,1:T(8,128)(2,1)}, u32[]{:S(2)}) copy-start(bf16[768,192]{0,1:T(8,128)(2,1)} %copy-done.3) | copy-start | bytes 884740
  312.6 45.7 %all-to-all-start.3 = ((bf16[64,96,128]{2,1,0:T(8,128)(2,1)}), bf16[64,96,128]{2,1,0:T(8,128)(2,1)S(1)}, u32[]{:S(2)}, u32[]{:S(2)}) async-start(bf16[64,96,128]{2,1,0:T(8,128)(2,1)} %reshape.84), calls=%async_computation.4 | async-start | bytes 3145728 | tf_op jit(solution)/shard_map/all_to_all | solution.py:93
  318.2 11.0 %slice-start.1 = ((s8[6488064]{0:T(1024)(128)(4,1)}), s8[4194304]{0:T(1024)(128)(4,1)S(1)}, s32[]{:S(2)}) async-start(s8[6488064]{0:T(1024)(128)(4,1)} %bitcast.47), calls=%async_computation.10 | async-start | bytes 8388608
  323.7 5.5 %slice-start.2 = ((s8[6488064]{0:T(1024)(128)(4,1)}), s8[2293760]{0:T(1024)(128)(4,1)S(1)}, s32[]{:S(2)}) async-start(s8[6488064]{0:T(1024)(128)(4,1)} %bitcast.47), calls=%async_computation.11 | async-start | bytes 4587520
  323.7 5.5 %copy-start.7 = (bf16[768,192]{0,1:T(8,128)(2,1)S(1)}, bf16[768,192]{0,1:T(8,128)(2,1)}, u32[]{:S(2)}) copy-start(bf16[768,192]{0,1:T(8,128)(2,1)} %get-tuple-element.6) | copy-start | bytes 884740
  329.2 34.0 %copy-start.1 = (bf16[1,4096,192]{1,2,0:T(8,128)(2,1)S(1)}, bf16[1,4096,192]{1,2,0:T(8,128)(2,1)}, u32[]{:S(2)}) copy-start(bf16[1,4096,192]{1,2,0:T(8,128)(2,1)} %param.11) | copy-start | bytes 4718596
Sparse Core Ops, SparseCore 0:
  71.1 64.3 all-gather.4
  137.3 70.4 all-gather.2
  222.9 68.8 reduce-scatter.1

commit v2 on v1

v2 whole, which is shorter than its diff:
```python
import jax
import jax.numpy as jnp
from jax import lax
from jax.sharding import PartitionSpec as P

LANES = 128
CHUNKS = 2


def body(tokens, out_grad, routes, gate_probs, w_gate, w_up, w_down):
    expert_count = lax.axis_size("expert")
    tok_count, width = tokens.shape
    top_count = routes.shape[1]
    capacity = 3 * tok_count * top_count // (2 * expert_count)
    slot_total = expert_count * capacity
    piece = width // CHUNKS
    per_peer = capacity * piece // LANES
    flat_routes = routes.reshape(-1)
    one_hot = (flat_routes[:, None] == jnp.arange(expert_count, dtype=jnp.int32)[None, :]).astype(
        jnp.int32
    )
    earlier = jnp.cumsum(one_hot, axis=0) - one_hot
    slot_index = jnp.sum(earlier * one_hot, axis=1)
    destination = flat_routes * capacity + slot_index
    placing = (jnp.arange(slot_total, dtype=jnp.int32)[:, None] == destination[None, :]).astype(
        jnp.bfloat16
    )
    collect = jnp.sum(placing.reshape(slot_total, tok_count, top_count), axis=2)
    contract_last = (((1,), (1,)), ((), ()))
    contract_first = (((0,), (0,)), ((), ()))

    def to_expert(rows):
        shaped = rows.reshape(expert_count, per_peer, LANES)
        return lax.all_to_all(shaped, "expert", 0, 0, tiled=True).reshape(slot_total, piece)

    def dispatch(source, c):
        part = source[:, c * piece:(c + 1) * piece]
        rows = jnp.dot(collect, part, preferred_element_type=jnp.float32).astype(jnp.bfloat16)
        return to_expert(rows)

    sent_prob = (
        jnp.dot(placing, gate_probs.reshape(-1), preferred_element_type=jnp.float32)
        .astype(jnp.bfloat16)
        .reshape(expert_count, capacity)
    )
    recv_prob = lax.all_to_all(sent_prob, "expert", 0, 0, tiled=True).reshape(slot_total)
    rows_in = []
    for c in range(CHUNKS):
        rows_in.append(lax.all_gather(dispatch(tokens, c), "dp", axis=0, tiled=True))
    rows_dy = []
    rows_prob = None
    for c in range(CHUNKS):
        recv = dispatch(out_grad, c)
        if c == 0:
            recv = jnp.concatenate(
                [recv, jnp.broadcast_to(recv_prob[:, None], (slot_total, LANES))], axis=1
            )
        gathered = lax.all_gather(recv, "dp", axis=0, tiled=True)
        if c == 0:
            rows_prob = gathered[:, piece]
            gathered = gathered[:, :piece]
        rows_dy.append(gathered)
    gate_w = w_gate[0]
    up_w = w_up[0]
    down_w = w_down[0]
    gate_pre = None
    up_pre = None
    for c in range(CHUNKS):
        g = jnp.dot(rows_in[c], gate_w[c * piece:(c + 1) * piece], preferred_element_type=jnp.float32)
        u = jnp.dot(rows_in[c], up_w[c * piece:(c + 1) * piece], preferred_element_type=jnp.float32)
        gate_pre = g if gate_pre is None else gate_pre + g
        up_pre = u if up_pre is None else up_pre + u
    sigmoid_gate = jax.nn.sigmoid(gate_pre)
    active = gate_pre * sigmoid_gate
    hidden = (active * up_pre).astype(jnp.bfloat16)
    back_raw = None
    for c in range(CHUNKS):
        b = lax.dot_general(
            rows_dy[c], down_w[:, c * piece:(c + 1) * piece], contract_last,
            preferred_element_type=jnp.float32,
        )
        back_raw = b if back_raw is None else back_raw + b
    score_part = jnp.sum(back_raw * hidden.astype(jnp.float32), axis=1)
    weight_col = rows_prob.astype(jnp.float32)[:, None]
    back_hidden = weight_col * back_raw
    grad_gate_pre = (
        back_hidden * up_pre * sigmoid_gate * (1.0 + gate_pre * (1.0 - sigmoid_gate))
    ).astype(jnp.bfloat16)
    grad_up_pre = (back_hidden * active).astype(jnp.bfloat16)
    row_total = grad_gate_pre.shape[0]
    back_rows = []
    back_scores = None
    for c in range(CHUNKS):
        part = lax.dot_general(
            grad_gate_pre, gate_w[c * piece:(c + 1) * piece], contract_last,
            preferred_element_type=jnp.float32,
        )
        part = part + lax.dot_general(
            grad_up_pre, up_w[c * piece:(c + 1) * piece], contract_last,
            preferred_element_type=jnp.float32,
        )
        if c == 0:
            part = jnp.concatenate(
                [part, jnp.broadcast_to(score_part[:, None], (row_total, LANES))], axis=1
            )
        own = lax.psum_scatter(part.astype(jnp.bfloat16), "dp", scatter_dimension=0, tiled=True)
        if c == 0:
            own_scores = own[:, piece].reshape(expert_count, capacity)
            back_scores = lax.all_to_all(own_scores, "expert", 0, 0, tiled=True).reshape(slot_total)
            own = own[:, :piece]
        back_rows.append(to_expert(own))
    grad_down = []
    grad_gate = []
    grad_up = []
    for c in range(CHUNKS):
        dy_c = rows_dy[c]
        scaled = (weight_col * dy_c.astype(jnp.float32)).astype(jnp.bfloat16)
        grad_down.append(lax.dot_general(
            hidden, scaled, contract_first, preferred_element_type=jnp.float32
        ).astype(jnp.bfloat16))
        grad_gate.append(lax.dot_general(
            rows_in[c], grad_gate_pre, contract_first, preferred_element_type=jnp.float32
        ).astype(jnp.bfloat16))
        grad_up.append(lax.dot_general(
            rows_in[c], grad_up_pre, contract_first, preferred_element_type=jnp.float32
        ).astype(jnp.bfloat16))
    grad_down = jnp.concatenate(grad_down, axis=1)
    grad_gate = jnp.concatenate(grad_gate, axis=0)
    grad_up = jnp.concatenate(grad_up, axis=0)
    grad_tokens = jnp.concatenate(
        [
            lax.dot_general(
                collect, back_rows[c], contract_first, preferred_element_type=jnp.float32
            ).astype(jnp.bfloat16)
            for c in range(CHUNKS)
        ],
        axis=1,
    )
    grad_probs = (
        jnp.dot(back_scores, placing, preferred_element_type=jnp.float32)
        .astype(jnp.bfloat16)
        .reshape(tok_count, top_count)
    )
    return (grad_tokens, grad_probs, grad_gate[None], grad_up[None], grad_down[None])


def solution(mesh):
    in_specs = (
        P(("dp", "expert"), None),
        P(("dp", "expert"), None),
        P(("dp", "expert"), None),
        P(("dp", "expert"), None),
        P("expert", None, "dp"),
        P("expert", None, "dp"),
        P("expert", "dp", None),
    )
    out_specs = (
        P(("dp", "expert"), None),
        P(("dp", "expert"), None),
        P("expert", None, "dp"),
        P("expert", None, "dp"),
        P("expert", "dp", None),
    )
    return jax.shard_map(body, mesh=mesh, in_specs=in_specs, out_specs=out_specs, check_vma=False)
```

time: 371 us -> 394 us (1.062)
  blocking collectives: 52 us -> 92.5 us
  waiting for transfers between devices: 207 us -> 171 us
  starting transfers between devices: 27.5 us -> 38.9 us
    all_to_all x1 -> x3, blocking collectives: 52 us -> 92.5 us  [to_expert(): lax.all_to_all(shaped, 'expert', 0, 0, tiled=True)]
    all_to_all x2 -> x3, waiting for transfers between devices: 65.3 us -> 47.3 us  [to_expert(): lax.all_to_all(shaped, 'expert', 0, 0, tiled=True)]
    all_gather x2 -> x4, waiting for transfers between devices: 62 us -> 48 us  [the longest x2 48 us: body(): gathered = lax.all_gather(recv, 'dp', axis=0, tiled=True)]
    all_to_all x2 -> x3, starting transfers between devices: 11.2 us -> 22.2 us  [to_expert(): lax.all_to_all(shaped, 'expert', 0, 0, tiled=True)]
    all_to_all x1, waiting for transfers between devices: 6.43 us -> 0.01 us  [body(): lax.all_to_all(own_scores, 'expert', 0, 0, tiled=True).reshape(slot_total)]
    dot_general x10 -> x20, matrix products: 38 us -> 40.8 us  [the longest x2 8.9 us: body(): lax.dot_general(rows_dy[c], down_w[:, c * piece:(c + 1) * piece], contrac...]
    reshape x6 -> x12, local copies, waits for them, and re-layouts: 14.6 us -> 13.5 us  [the longest x6 6.83 us: to_expert(): lax.all_to_all(shaped, 'expert', 0, 0, tiled=True)]
    reduce_scatter x1 -> x2, waiting for transfers between devices: 69 us -> 68.5 us  [body(): lax.psum_scatter(part.astype(jnp.bfloat16), 'dp', scatter_dimension=0, ti...]
  transfers between devices with their start and end apart: 7 -> 11, of which waited for: 6 -> 8; matrix products, arithmetic and copies ran while one was open for 9% -> 14% of each run, Pallas kernels for 0% -> 0%
where the time goes in v2:
time: 394 us; the launch traced here: 392 us
  waiting for transfers between devices  171 us (43%)
  blocking collectives  92.5 us (23%)
  matrix products  45.2 us (11%)
  starting transfers between devices  38.9 us (10%)
  local copies, waits for them, and re-layouts  19.2 us (5%)
  between operations  14.5 us (4%)
  other arithmetic  11 us (3%)
    all_to_all x3, blocking collectives, to_expert(): lax.all_to_all(shaped, 'expert', 0, 0, tiled=True)  92.5 us
    reduce_scatter x2, waiting for transfers between devices, body(): lax.psum_scatter(part.astype(jnp.bfloat16), 'dp', scatter_dimension=0, ti...  68.5 us
    all_gather x2, waiting for transfers between devices, body(): gathered = lax.all_gather(recv, 'dp', axis=0, tiled=True)  48 us
    all_to_all x3, waiting for transfers between devices, to_expert(): lax.all_to_all(shaped, 'expert', 0, 0, tiled=True)  47.3 us
    all_to_all x3, starting transfers between devices, to_expert(): lax.all_to_all(shaped, 'expert', 0, 0, tiled=True)  22.2 us
    all_to_all x1, starting transfers between devices, body(): lax.all_to_all(own_scores, 'expert', 0, 0, tiled=True).reshape(slot_total)  10.6 us
    dot_general x2, matrix products, body(): lax.dot_general(rows_dy[c], down_w[:, c * piece:(c + 1) * piece], contrac...  8.9 us
    dot_general x2, matrix products, body(): jnp.dot(rows_in[c], gate_w[c * piece:(c + 1) * piece], preferred_element_...  8.55 us
  transfers between devices with their start and end apart: 11, of which 8 were waited for; matrix products, arithmetic and copies ran while one was open for 14% of the time, Pallas kernels for 0%

profile of v2, /device:TPU:8, one launch (start us, length us, event | category | flops | bytes accessed | tf_op | source)
XLA Modules:
  0.0 392.1 jit_solution(721865889223023181)
XLA Ops:
  11.5 35.0 %all_to_all.50 = bf16[64,48,128]{2,1,0:T(8,128)(2,1)S(1)} all-to-all(bf16[64,48,128]{2,1,0:T(8,128)(2,1)S(1)} %reshape.110), channel_id=1, replica_groups=mesh['dp'=4,'expert'=64] {'expert'}, dimensions={0} | all-to-all | bytes 1572864 | tf_op jit(solution)/shard_map/all_to_all | solution.py:34
  48.6 28.7 %all_to_all.51 = bf16[64,48,128]{2,1,0:T(8,128)(2,1)S(1)} all-to-all(bf16[64,48,128]{2,1,0:T(8,128)(2,1)S(1)} %reshape.112), channel_id=1, replica_groups=mesh['dp'=4,'expert'=64] {'expert'}, dimensions={0} | all-to-all | bytes 1572864 | tf_op jit(solution)/shard_map/all_to_all | solution.py:34
  79.5 5.8 %all-to-all-start.1 = ((bf16[64,1,3]{2,1,0:T(2,128)(2,1)}), bf16[64,1,3]{2,1,0:T(2,128)(2,1)S(1)}, u32[]{:S(2)}, u32[]{:S(2)}) async-start(bf16[64,1,3]{2,1,0:T(2,128)(2,1)} %all_to_all.40), calls=%async_computation.1 | async-start | bytes 65536 | tf_op jit(solution)/shard_map/all_to_all | solution.py:46
  86.9 6.9 %all-to-all-done.1 = bf16[64,1,3]{2,1,0:T(2,128)(2,1)S(1)} async-done(((bf16[64,1,3]{2,1,0:T(2,128)(2,1)}), bf16[64,1,3]{2,1,0:T(2,128)(2,1)S(1)}, u32[]{:S(2)}, u32[]{:S(2)}) %all-to-all-start.1) | async-done | bytes 416 | tf_op jit(solution)/shard_map/all_to_all | solution.py:46
  93.8 5.5 %all-to-all-start = ((bf16[64,48,128]{2,1,0:T(8,128)(2,1)}), bf16[64,48,128]{2,1,0:T(8,128)(2,1)S(1)}, u32[]{:S(2)}, u32[]{:S(2)}) async-start(bf16[64,48,128]{2,1,0:T(8,128)(2,1)} %reshape.105), calls=%async_computation | async-start | bytes 1572864 | tf_op jit(solution)/shard_map/all_to_all | solution.py:34
  99.7 23.0 %all-to-all-done = bf16[64,48,128]{2,1,0:T(8,128)(2,1)S(1)} async-done(((bf16[64,48,128]{2,1,0:T(8,128)(2,1)}), bf16[64,48,128]{2,1,0:T(8,128)(2,1)S(1)}, u32[]{:S(2)}, u32[]{:S(2)}) %all-to-all-start) | async-done | bytes 786464 | tf_op jit(solution)/shard_map/all_to_all | solution.py:34
  126.0 28.7 %all_to_all.52 = bf16[64,48,128]{2,1,0:T(8,128)(2,1)S(1)} all-to-all(bf16[64,48,128]{2,1,0:T(8,128)(2,1)S(1)} %reshape.108), channel_id=1, replica_groups=mesh['dp'=4,'expert'=64] {'expert'}, dimensions={0} | all-to-all | bytes 1572864 | tf_op jit(solution)/shard_map/all_to_all | solution.py:34
  156.2 4.1 %fusion.18 = f32[768,192]{0,1:T(8,128)} fusion(bf16[768,2048]{1,0:T(8,128)(2,1)} %all-gather.9.cloned.1.call-done, bf16[1,4096,192]{1,2,0:T(8,128)(2,1)S(1)} %copy-done.12), kind=kOutput, calls=%fused_computation.42 | convolution fusion | flops 603979776 | bytes 4521984 | tf_op jit(solution)/shard_map/dot_general | solution.py:69
  162.4 4.5 %convolution_add_fusion = f32[768,192]{0,1:T(8,128)} fusion(f32[768,192]{0,1:T(8,128)} %fusion.18, bf16[768,2048]{1,0:T(8,128)(2,1)} %all-gather.11.cloned.1.call-done, bf16[1,4096,192]{1,2,0:T(8,128)(2,1)} %param.11), kind=kOutput, calls=%fused_computation.27 | convolution fusion | flops 604127232 | bytes 5111808 | tf_op jit(solution)/shard_map/dot_general | solution.py:69
  168.9 8.6 %all-gather.5.cloned.1.call-done = bf16[768,2176]{1,0:T(8,128)(2,1)} async-done(((bf16[192,2176]{1,0:T(8,128)(2,1)}), bf16[768,2176]{1,0:T(8,128)(2,1)}) %all-gather.5.cloned.1.call-update) | async-done | bytes 3342352 | tf_op jit(solution)/shard_map/all_gather | solution.py:58
  178.5 4.1 %fusion.5 = f32[768,192]{0,1:T(8,128)} fusion(bf16[768,2176]{1,0:T(8,128)(2,1)} %all-gather.5.cloned.1.call-done, bf16[192,4096]{1,0:T(8,128)(2,1)} %bitcast.64), kind=kOutput, calls=%fused_computation.10 | convolution fusion | flops 603979776 | bytes 4521984 | tf_op jit(solution)/shard_map/dot_general | solution.py:78
  182.6 39.4 %all-gather.7.cloned.1.call-done = bf16[768,2048]{1,0:T(8,128)(2,1)} async-done(((bf16[192,2048]{1,0:T(8,128)(2,1)}), bf16[768,2048]{1,0:T(8,128)(2,1)}) %all-gather.7.cloned.1.call-update) | async-done | bytes 3145744 | tf_op jit(solution)/shard_map/all_gather | solution.py:58
  222.0 4.8 %multiply_reduce_fusion = (bf16[768]{0:T(1024)(128)(2,1)S(1)}, bf16[768,192]{0,1:T(8,128)(2,1)}, bf16[768,192]{0,1:T(8,128)(2,1)S(1)}, bf16[768,192]{0,1:T(8,128)(2,1)S(1)}) fusion(f32[768,192]{0,1:T(8,128)} %convolution_add_fusion.1, f32[768,192]{0,1:T(8,128)} %convolution_add_fusion, f32[768]{0:T(1024)S(1)} %convert_reduce_fusion, f32[768,192]{0,1:T(8,128)} %fusion.5, ...), kind=kOutput, calls=%fused_computation.57 | convolution fusion | flops 606928128 | bytes 6590976 | tf_op jit(solution)/shard_map/dot_general | solution.py:78
  231.7 2.3 fusion.13
  234.0 2.7 add_convert_fusion
  236.6 37.7 %reduce-scatter.3.cloned.1.call-done = bf16[192,2176]{1,0:T(8,128)(2,1)} async-done(((bf16[768,2176]{1,0:T(8,128)(2,1)}), bf16[192,2176]{1,0:T(8,128)(2,1)}) %reduce-scatter.3.cloned.1.call-update) | async-done | bytes 835600 | tf_op jit(solution)/shard_map/reduce_scatter | solution.py:106
  276.1 10.6 %all-to-all-start.7 = ((bf16[64,1,3]{2,1,0:T(2,128)(2,1)}), bf16[64,1,3]{2,1,0:T(2,128)(2,1)S(1)}, u32[]{:S(2)}, u32[]{:S(2)}) async-start(bf16[64,1,3]{2,1,0:T(2,128)(2,1)} %all_to_all.41), calls=%async_computation.9 | async-start | bytes 65536 | tf_op jit(solution)/shard_map/all_to_all | solution.py:109
  286.6 30.8 %reduce-scatter.5.cloned.1.call-done = bf16[192,2048]{1,0:T(8,128)(2,1)} async-done(((bf16[768,2048]{1,0:T(8,128)(2,1)}), bf16[192,2048]{1,0:T(8,128)(2,1)}) %reduce-scatter.5.cloned.1.call-update) | async-done | bytes 786448 | tf_op jit(solution)/shard_map/reduce_scatter | solution.py:106
  319.6 10.7 %all-to-all-start.6 = ((bf16[64,48,128]{2,1,0:T(8,128)(2,1)}), bf16[64,48,128]{2,1,0:T(8,128)(2,1)}, u32[]{:S(2)}, u32[]{:S(2)}) async-start(bf16[64,48,128]{2,1,0:T(8,128)(2,1)} %reshape.116), calls=%async_computation.8 | async-start | bytes 1572864 | tf_op jit(solution)/shard_map/all_to_all | solution.py:34
  330.3 3.7 convolution_convert_fusion.3
  342.5 2.2 reshape.114
  344.8 8.6 %all-to-all-done.6 = bf16[64,48,128]{2,1,0:T(8,128)(2,1)} async-done(((bf16[64,48,128]{2,1,0:T(8,128)(2,1)}), bf16[64,48,128]{2,1,0:T(8,128)(2,1)}, u32[]{:S(2)}, u32[]{:S(2)}) %all-to-all-start.6) | async-done | bytes 786464 | tf_op jit(solution)/shard_map/all_to_all | solution.py:34
  353.4 5.9 %all-to-all-start.5 = ((bf16[64,48,128]{2,1,0:T(8,128)(2,1)}), bf16[64,48,128]{2,1,0:T(8,128)(2,1)}, u32[]{:S(2)}, u32[]{:S(2)}) async-start(bf16[64,48,128]{2,1,0:T(8,128)(2,1)} %reshape.114), calls=%async_computation.6 | async-start | bytes 1572864 | tf_op jit(solution)/shard_map/all_to_all | solution.py:34
  366.7 15.7 %all-to-all-done.5 = bf16[64,48,128]{2,1,0:T(8,128)(2,1)} async-done(((bf16[64,48,128]{2,1,0:T(8,128)(2,1)}), bf16[64,48,128]{2,1,0:T(8,128)(2,1)}, u32[]{:S(2)}, u32[]{:S(2)}) %all-to-all-start.5) | async-done | bytes 786464 | tf_op jit(solution)/shard_map/all_to_all | solution.py:34
  (118 shorter events, 47.5 us)
Async XLA Ops:
  7.2 71.4 %copy-start = (bf16[128,1]{0,1:T(2,128)(2,1)S(1)}, bf16[128,1]{0,1:T(2,128)(2,1)}, u32[]{:S(2)}) copy-start(bf16[128,1]{0,1:T(2,128)(2,1)} %param.10) | copy-start | bytes 772
  7.2 149.0 %all-gather.9.cloned.1.call-start = ((), (), s32[]{:S(2)}) async-start(), calls=%async_computation.12 | async-start | bytes 3932160 | tf_op jit(solution)/shard_map/all_gather | solution.py:49
  9.6 38.2 %copy-start.18 = (bf16[128,4096]{1,0:T(8,128)(2,1)S(1)}, bf16[128,4096]{1,0:T(8,128)(2,1)}, u32[]{:S(2)}) copy-start(bf16[128,4096]{1,0:T(8,128)(2,1)} %param.7) | copy-start | bytes 3145732
  47.8 114.6 %all-gather.11.cloned.1.call-start = ((), (), s32[]{:S(2)}) async-start(), calls=%async_computation.13 | async-start | bytes 3932160 | tf_op jit(solution)/shard_map/all_gather | solution.py:49
  48.2 37.1 %copy-start.19 = (bf16[128,4096]{1,0:T(8,128)(2,1)S(1)}, bf16[128,4096]{1,0:T(8,128)(2,1)}, u32[]{:S(2)}) copy-start(bf16[128,4096]{1,0:T(8,128)(2,1)} %param.8) | copy-start | bytes 3145732
  79.5 14.3 %all-to-all-start.1 = ((bf16[64,1,3]{2,1,0:T(2,128)(2,1)}), bf16[64,1,3]{2,1,0:T(2,128)(2,1)S(1)}, u32[]{:S(2)}, u32[]{:S(2)}) async-start(bf16[64,1,3]{2,1,0:T(2,128)(2,1)} %all_to_all.40), calls=%async_computation.1 | async-start | bytes 65536 | tf_op jit(solution)/shard_map/all_to_all | solution.py:46
  93.8 28.8 %all-to-all-start = ((bf16[64,48,128]{2,1,0:T(8,128)(2,1)}), bf16[64,48,128]{2,1,0:T(8,128)(2,1)S(1)}, u32[]{:S(2)}, u32[]{:S(2)}) async-start(bf16[64,48,128]{2,1,0:T(8,128)(2,1)} %reshape.105), calls=%async_computation | async-start | bytes 1572864 | tf_op jit(solution)/shard_map/all_to_all | solution.py:34
  99.4 78.1 %all-gather.5.cloned.1.call-start = ((), (), s32[]{:S(2)}) async-start(), calls=%async_computation.10 | async-start | bytes 4177920 | tf_op jit(solution)/shard_map/all_gather | solution.py:58
  124.1 32.2 %copy-start.12 = (bf16[1,4096,192]{1,2,0:T(8,128)(2,1)S(1)}, bf16[1,4096,192]{1,2,0:T(8,128)(2,1)}, u32[]{:S(2)}) copy-start(bf16[1,4096,192]{1,2,0:T(8,128)(2,1)} %param.11) | copy-start | bytes 4718596
  124.1 97.9 %all-gather.7.cloned.1.call-start = ((), (), s32[]{:S(2)}) async-start(), calls=%async_computation.11 | async-start | bytes 3932160 | tf_op jit(solution)/shard_map/all_gather | solution.py:58
  156.0 4.4 %copy-start.14 = (bf16[1,4096,192]{1,2,0:T(8,128)(2,1)S(1)}, bf16[1,4096,192]{1,2,0:T(8,128)(2,1)}, u32[]{:S(2)}) copy-start(bf16[1,4096,192]{1,2,0:T(8,128)(2,1)} %param.12) | copy-start | bytes 4718596
  156.0 118.4 %reduce-scatter.3.cloned.1.call-start = ((), (), s32[]{:S(2)}) async-start(), calls=%async_computation.14 | async-start | bytes 4177920 | tf_op jit(solution)/shard_map/reduce_scatter | solution.py:106
  156.2 4.1 %copy-start.3 = (bf16[768,2048]{1,0:T(8,128)(2,1)S(1)}, bf16[768,2048]{1,0:T(8,128)(2,1)}, u32[]{:S(2)}) copy-start(bf16[768,2048]{1,0:T(8,128)(2,1)} %all-gather.9.cloned.1.call-done) | copy-start | bytes 9437188
  162.4 4.5 %copy-start.2 = (bf16[768,2048]{1,0:T(8,128)(2,1)S(1)}, bf16[768,2048]{1,0:T(8,128)(2,1)}, u32[]{:S(2)}) copy-start(bf16[768,2048]{1,0:T(8,128)(2,1)} %all-gather.11.cloned.1.call-done) | copy-start | bytes 9437188
  162.4 4.5 %copy-start.15 = (bf16[1,4096,192]{1,2,0:T(8,128)(2,1)S(1)}, bf16[1,4096,192]{1,2,0:T(8,128)(2,1)}, u32[]{:S(2)}) copy-start(bf16[1,4096,192]{1,2,0:T(8,128)(2,1)} %param.12) | copy-start | bytes 4718596
  162.4 4.5 %copy-start.25 = (f32[768,192]{0,1:T(8,128)S(1)}, f32[768,192]{0,1:T(8,128)}, u32[]{:S(2)}) copy-start(f32[768,192]{0,1:T(8,128)} %fusion.23) | copy-start | bytes 1769476
  222.0 4.8 %copy-start.13 = (bf16[1,4096,192]{1,2,0:T(8,128)(2,1)S(1)}, bf16[1,4096,192]{1,2,0:T(8,128)(2,1)}, u32[]{:S(2)}) copy-start(bf16[1,4096,192]{1,2,0:T(8,128)(2,1)} %param.11) | copy-start | bytes 4718596
  231.6 85.8 %reduce-scatter.5.cloned.1.call-start = ((), (), s32[]{:S(2)}) async-start(), calls=%async_computation.15 | async-start | bytes 3932160 | tf_op jit(solution)/shard_map/reduce_scatter | solution.py:106
  276.1 43.5 %all-to-all-start.7 = ((bf16[64,1,3]{2,1,0:T(2,128)(2,1)}), bf16[64,1,3]{2,1,0:T(2,128)(2,1)S(1)}, u32[]{:S(2)}, u32[]{:S(2)}) async-start(bf16[64,1,3]{2,1,0:T(2,128)(2,1)} %all_to_all.41), calls=%async_computation.9 | async-start | bytes 65536 | tf_op jit(solution)/shard_map/all_to_all | solution.py:109
  319.6 33.8 %all-to-all-start.6 = ((bf16[64,48,128]{2,1,0:T(8,128)(2,1)}), bf16[64,48,128]{2,1,0:T(8,128)(2,1)}, u32[]{:S(2)}, u32[]{:S(2)}) async-start(bf16[64,48,128]{2,1,0:T(8,128)(2,1)} %reshape.116), calls=%async_computation.8 | async-start | bytes 1572864 | tf_op jit(solution)/shard_map/all_to_all | solution.py:34
  330.3 3.8 copy-start.4
  341.6 17.8 %copy-start.8 = (bf16[768,192]{0,1:T(8,128)(2,1)S(1)}, bf16[768,192]{0,1:T(8,128)(2,1)}, u32[]{:S(2)}) copy-start(bf16[768,192]{0,1:T(8,128)(2,1)} %copy-done.5) | copy-start | bytes 884740
  353.4 29.0 %all-to-all-start.5 = ((bf16[64,48,128]{2,1,0:T(8,128)(2,1)}), bf16[64,48,128]{2,1,0:T(8,128)(2,1)}, u32[]{:S(2)}, u32[]{:S(2)}) async-start(bf16[64,48,128]{2,1,0:T(8,128)(2,1)} %reshape.114), calls=%async_computation.6 | async-start | bytes 1572864 | tf_op jit(solution)/shard_map/all_to_all | solution.py:34
  364.9 20.4 %copy-start.1 = (bf16[128,1]{0,1:T(2,128)(2,1)S(1)}, bf16[128,1]{0,1:T(2,128)(2,1)}, u32[]{:S(2)}) copy-start(bf16[128,1]{0,1:T(2,128)(2,1)} %param.10) | copy-start | bytes 772
  (14 other events, 29.7 us)
Sparse Core Ops, SparseCore 0:
  47.9 38.5 all-gather.8
  88.9 42.2 all-gather.10
  133.6 43.8 all-gather.4
  179.7 42.2 all-gather.6
  231.7 42.6 reduce-scatter.2
  276.8 40.5 reduce-scatter.4

commit v3 on v1

--- a/solution.py
+++ b/solution.py
@@ -4,6 +4,38 @@
 from jax.sharding import PartitionSpec as P
 
 LANES = 128
+
+
+def ring_pairs(count, step):
+    return [(i, (i + step) % count) for i in range(count)]
+
+
+def ring_gather(x, axis):
+    count = lax.axis_size(axis)
+    fwd = ring_pairs(count, 1)
+    bwd = ring_pairs(count, -1)
+    half = x.shape[0] // 2
+    from_prev = lax.ppermute(x, axis, fwd)
+    from_next = lax.ppermute(x, axis, bwd)
+    far_a = lax.ppermute(from_prev[:half], axis, fwd)
+    far_b = lax.ppermute(from_next[half:], axis, bwd)
+    return jnp.concatenate([x, from_next, far_a, far_b, from_prev], axis=0)
+
+
+def ring_reduce_scatter(parts, axis):
+    count = lax.axis_size(axis)
+    fwd = ring_pairs(count, 1)
+    bwd = ring_pairs(count, -1)
+    block = parts.shape[0] // count
+    half = block // 2
+    own, to_next, far, to_prev = (parts[k * block:(k + 1) * block] for k in range(count))
+    got_a = lax.ppermute(far[:half].astype(jnp.bfloat16), axis, fwd).astype(jnp.float32)
+    got_b = lax.ppermute(far[half:].astype(jnp.bfloat16), axis, bwd).astype(jnp.float32)
+    send_next = jnp.concatenate([to_next[:half] + got_a, to_next[half:]], axis=0)
+    send_prev = jnp.concatenate([to_prev[:half], to_prev[half:] + got_b], axis=0)
+    from_prev = lax.ppermute(send_next.astype(jnp.bfloat16), axis, fwd).astype(jnp.float32)
+    from_next = lax.ppermute(send_prev.astype(jnp.bfloat16), axis, bwd).astype(jnp.float32)
+    return own + from_prev + from_next
 
 
 def body(tokens, out_grad, routes, gate_probs, w_gate, w_up, w_down):
@@ -45,8 +77,8 @@
     dy_ext = jnp.concatenate(
         [recv_dy, jnp.broadcast_to(recv_prob[:, None], (slot_total, LANES))], axis=1
     )
-    rows_in = lax.all_gather(recv_in, "dp", axis=0, tiled=True)
-    rows_dy_ext = lax.all_gather(dy_ext, "dp", axis=0, tiled=True)
+    rows_in = ring_gather(recv_in, "dp")
+    rows_dy_ext = ring_gather(dy_ext, "dp")
     rows_dy = rows_dy_ext[:, :width]
     rows_prob = rows_dy_ext[:, width]
     gate_w = w_gate[0]
@@ -77,8 +109,8 @@
     row_total = row_part.shape[0]
     row_ext = jnp.concatenate(
         [row_part, jnp.broadcast_to(score_part[:, None], (row_total, LANES))], axis=1
-    ).astype(jnp.bfloat16)
-    own_ext = lax.psum_scatter(row_ext, "dp", scatter_dimension=0, tiled=True)
+    )
+    own_ext = ring_reduce_scatter(row_ext, "dp").astype(jnp.bfloat16)
     grad_down = lax.dot_general(
         hidden, scaled, contract_first, preferred_element_type=jnp.float32
     ).astype(jnp.bfloat16)

time: 371 us -> 350 us (0.943)
  blocking collectives: 52 us -> 0 us
  starting transfers between devices: 27.5 us -> 60.5 us
  between operations: 14 us -> 1.05 us
  local copies, waits for them, and re-layouts: 17.8 us -> 27.6 us
  other arithmetic: 9.76 us -> 15.7 us
    ppermute x0 -> x12, waiting for transfers between devices: none -> 102 us  [the longest x1 30.8 us: ring_reduce_scatter(): lax.ppermute(send_prev.astype(jnp.bfloat16), axis, bwd).astype(jnp.float32)]
    reduce_scatter x1 -> x0, waiting for transfers between devices: 69 us -> none  [body(): own_ext = lax.psum_scatter(row_ext, 'dp', scatter_dimension=0, tiled=True)]
    all_gather x2 -> x0, waiting for transfers between devices: 62 us -> none  [the longest x1 62 us: body(): rows_dy_ext = lax.all_gather(dy_ext, 'dp', axis=0, tiled=True)]
    all_to_all x1 -> x0, blocking collectives: 52 us -> none  [body(): lax.all_to_all(sent_in, 'expert', 0, 0, tiled=True)]
    all_to_all x0 -> x1, waiting for transfers between devices: none -> 33.4 us  [body(): lax.all_to_all(sent_in, 'expert', 0, 0, tiled=True)]
    ppermute x0 -> x12, starting transfers between devices: none -> 20 us  [the longest x2 6.35 us: ring_gather(): far_b = lax.ppermute(from_next[half:], axis, bwd)]
    another operation x0 -> x2, other arithmetic: none -> 10.4 us
    all_to_all x1, starting transfers between devices: 5.43 us -> 12.1 us  [body(): lax.all_to_all(sent_prob, 'expert', 0, 0, tiled=True).reshape(slot_total)]
  transfers between devices with their start and end apart: 7 -> 17, of which waited for: 6 -> 11; matrix products, arithmetic and copies ran while one was open for 9% -> 13% of each run, Pallas kernels for 0% -> 0%
where the time goes in v3:
time: 350 us; the launch traced here: 349 us
  waiting for transfers between devices  206 us (59%)
  starting transfers between devices  60.5 us (17%)
  matrix products  38.5 us (11%)
  local copies, waits for them, and re-layouts  27.6 us (8%)
  other arithmetic  15.7 us (4%)
    all_to_all x1, waiting for transfers between devices, body(): lax.all_to_all(sent_dy, 'expert', 0, 0, tiled=True)  33.8 us
    all_to_all x1, waiting for transfers between devices, body(): lax.all_to_all(sent_in, 'expert', 0, 0, tiled=True)  33.4 us
    ppermute x1, waiting for transfers between devices, ring_reduce_scatter(): lax.ppermute(send_prev.astype(jnp.bfloat16), axis, bwd).astype(jnp.float32)  30.8 us
    ppermute x2, waiting for transfers between devices, ring_gather(): from_next = lax.ppermute(x, axis, bwd)  28.4 us
    all_to_all x1, waiting for transfers between devices, body(): lax.all_to_all(own_rows, 'expert', 0, 0, tiled=True)  25.4 us
    ppermute x2, waiting for transfers between devices, ring_gather(): far_a = lax.ppermute(from_prev[:half], axis, fwd)  24.1 us
    ppermute x1, waiting for transfers between devices, ring_reduce_scatter(): lax.ppermute(far[:half].astype(jnp.bfloat16), axis, fwd).astype(jnp.float32)  15.2 us
    all_to_all x1, starting transfers between devices, body(): lax.all_to_all(sent_prob, 'expert', 0, 0, tiled=True).reshape(slot_total)  12.1 us
  transfers between devices with their start and end apart: 17, of which 11 were waited for; matrix products, arithmetic and copies ran while one was open for 13% of the time, Pallas kernels for 0%

profile of v3, /device:TPU:8, one launch (start us, length us, event | category | flops | bytes accessed | tf_op | source)
XLA Modules:
  0.0 349.1 jit_solution(8591715570587444387)
XLA Ops:
  4.8 12.1 %all-to-all-start.1 = ((bf16[64,1,3]{2,1,0:T(2,128)(2,1)}), bf16[64,1,3]{2,1,0:T(2,128)(2,1)S(1)}, u32[]{:S(2)}, u32[]{:S(2)}) async-start(bf16[64,1,3]{2,1,0:T(2,128)(2,1)} %all_to_all.28), calls=%async_computation.1 | async-start | bytes 65536 | tf_op jit(solution)/shard_map/all_to_all | solution.py:76
  20.8 4.7 %all-to-all-done.1 = bf16[64,1,3]{2,1,0:T(2,128)(2,1)S(1)} async-done(((bf16[64,1,3]{2,1,0:T(2,128)(2,1)}), bf16[64,1,3]{2,1,0:T(2,128)(2,1)S(1)}, u32[]{:S(2)}, u32[]{:S(2)}) %all-to-all-start.1) | async-done | bytes 416 | tf_op jit(solution)/shard_map/all_to_all | solution.py:76
  25.5 5.6 %all-to-all-start.2 = ((bf16[64,96,128]{2,1,0:T(8,128)(2,1)}), bf16[64,96,128]{2,1,0:T(8,128)(2,1)S(1)}, u32[]{:S(2)}, u32[]{:S(2)}) async-start(bf16[64,96,128]{2,1,0:T(8,128)(2,1)} %reshape.82), calls=%async_computation.2 | async-start | bytes 3145728 | tf_op jit(solution)/shard_map/all_to_all | solution.py:74
  34.0 3.7 %reshape.79 = bf16[64,96,128]{2,1,0:T(8,128)(2,1)} reshape(bf16[192,4096]{1,0:T(8,128)(2,1)} %convolution_convert_fusion.3) | data formatting | bytes 3145728 | tf_op jit(solution)/shard_map/reshape | solution.py:67
  37.8 33.4 %all-to-all-done.2 = bf16[64,96,128]{2,1,0:T(8,128)(2,1)S(1)} async-done(((bf16[64,96,128]{2,1,0:T(8,128)(2,1)}), bf16[64,96,128]{2,1,0:T(8,128)(2,1)S(1)}, u32[]{:S(2)}, u32[]{:S(2)}) %all-to-all-start.2) | async-done | bytes 1572896 | tf_op jit(solution)/shard_map/all_to_all | solution.py:74
  71.1 5.6 %all-to-all-start = ((bf16[64,96,128]{2,1,0:T(8,128)(2,1)}), bf16[64,96,128]{2,1,0:T(8,128)(2,1)}, u32[]{:S(2)}, u32[]{:S(2)}) async-start(bf16[64,96,128]{2,1,0:T(8,128)(2,1)} %reshape.79), calls=%async_computation | async-start | bytes 3145728 | tf_op jit(solution)/shard_map/all_to_all | solution.py:75
  82.9 33.8 %all-to-all-done = bf16[64,96,128]{2,1,0:T(8,128)(2,1)} async-done(((bf16[64,96,128]{2,1,0:T(8,128)(2,1)}), bf16[64,96,128]{2,1,0:T(8,128)(2,1)}, u32[]{:S(2)}, u32[]{:S(2)}) %all-to-all-start) | async-done | bytes 1572896 | tf_op jit(solution)/shard_map/all_to_all | solution.py:75
  116.7 3.7 %reshape.80 = bf16[192,4096]{1,0:T(8,128)(2,1)} reshape(bf16[64,96,128]{2,1,0:T(8,128)(2,1)} %all-to-all-done) | data formatting | bytes 3145728 | tf_op jit(solution)/shard_map/reshape | solution.py:75
  132.4 28.4 %collective-permute-done = bf16[192,4224]{1,0:T(8,128)(2,1)S(1)} collective-permute-done((bf16[192,4224]{1,0:T(8,128)(2,1)S(1)}, bf16[192,4224]{1,0:T(8,128)(2,1)S(1)}, u32[]{:S(2)}, u32[]{:S(2)}) %collective-permute-start) | collective-permute-done | bytes 1622048 | tf_op jit(solution)/shard_map/ppermute | solution.py:19
  160.9 3.8 %collective-permute-start.3 = (bf16[96,4224]{1,0:T(8,128)(2,1)S(1)}, bf16[96,4224]{1,0:T(8,128)(2,1)S(1)}, u32[]{:S(2)}, u32[]{:S(2)}) collective-permute-start(bf16[96,4224]{1,0:T(8,128)(2,1)S(1)} %slice.74), channel_id=1, source_target_pairs={{0,192},{64,0},{128,64},{192,128},{1,193},{65,1},{129,65},{193,129... | collective-permute-start | bytes 2433032 | tf_op jit(solution)/shard_map/ppermute | solution.py:21
  165.2 16.2 %collective-permute-done.6 = bf16[96,4096]{1,0:T(8,128)(2,1)S(1)} collective-permute-done((bf16[96,4096]{1,0:T(8,128)(2,1)S(1)}, bf16[96,4096]{1,0:T(8,128)(2,1)S(1)}, u32[]{:S(2)}, u32[]{:S(2)}) %collective-permute-start.6) | collective-permute-done | bytes 786464 | tf_op jit(solution)/shard_map/ppermute | solution.py:20
  188.0 8.0 %collective-permute-done.2 = bf16[96,4224]{1,0:T(8,128)(2,1)S(1)} collective-permute-done((bf16[96,4224]{1,0:T(8,128)(2,1)S(1)}, bf16[96,4224]{1,0:T(8,128)(2,1)S(1)}, u32[]{:S(2)}, u32[]{:S(2)}) %collective-permute-start.2) | collective-permute-done | bytes 811040 | tf_op jit(solution)/shard_map/ppermute | solution.py:20
  201.4 6.4 %convolution_add_fusion = f32[768,4096]{1,0:T(8,128)} fusion(f32[768,4096]{1,0:T(8,128)S(1)} %fusion.20, bf16[768,192]{0,1:T(8,128)(2,1)S(1)} %get-tuple-element.16, bf16[1,4096,192]{1,2,0:T(8,128)(2,1)S(1)} %copy-done.3), kind=kOutput, calls=%fused_computation.9 | convolution fusion | flops 1211105280 | bytes 27033600 | tf_op jit(solution)/shard_map/dot_general | solution.py:106
  208.0 8.1 %fusion = bf16[768,4224]{1,0:T(8,128)(2,1)} fusion(f32[768,128]{1,0:T(8,128)S(1)} %broadcast_in_dim.28, f32[768,4096]{1,0:T(8,128)} %convolution_add_fusion), kind=kLoop, calls=%fused_computation.4 | loop fusion | flops 12976128 | bytes 19464192 | tf_op jit(solution)/shard_map/convert.8
  218.3 3.2 collective-permute-start.10
  221.5 15.2 %collective-permute-done.8 = bf16[96,4224]{1,0:T(8,128)(2,1)S(1)} collective-permute-done((bf16[96,4224]{1,0:T(8,128)(2,1)S(1)}, bf16[96,4224]{1,0:T(8,128)(2,1)S(1)}, u32[]{:S(2)}, u32[]{:S(2)}) %collective-permute-start.8) | collective-permute-done | bytes 811040 | tf_op jit(solution)/shard_map/ppermute | solution.py:32
  242.4 30.8 %collective-permute-done.11 = bf16[192,4224]{1,0:T(8,128)(2,1)S(1)} collective-permute-done((bf16[192,4224]{1,0:T(8,128)(2,1)S(1)}, bf16[192,4224]{1,0:T(8,128)(2,1)S(1)}, u32[]{:S(2)}, u32[]{:S(2)}) %collective-permute-start.11) | collective-permute-done | bytes 1622048 | tf_op jit(solution)/shard_map/ppermute | solution.py:37
  273.2 3.6 %collective-permute-done.9 = bf16[192,4224]{1,0:T(8,128)(2,1)S(1)} collective-permute-done((bf16[192,4224]{1,0:T(8,128)(2,1)S(1)}, bf16[192,4224]{1,0:T(8,128)(2,1)S(1)}, u32[]{:S(2)}, u32[]{:S(2)}) %collective-permute-start.9) | collective-permute-done | bytes 1622048 | tf_op jit(solution)/shard_map/ppermute | solution.py:36
  278.3 11.6 %all-to-all-start.4 = ((bf16[64,1,3]{2,1,0:T(2,128)(2,1)}), bf16[64,1,3]{2,1,0:T(2,128)(2,1)S(1)}, u32[]{:S(2)}, u32[]{:S(2)}) async-start(bf16[64,1,3]{2,1,0:T(2,128)(2,1)} %all_to_all.29), calls=%async_computation.4 | async-start | bytes 65536 | tf_op jit(solution)/shard_map/all_to_all | solution.py:126
  292.2 6.3 %all-to-all-done.4 = bf16[64,1,3]{2,1,0:T(2,128)(2,1)S(1)} async-done(((bf16[64,1,3]{2,1,0:T(2,128)(2,1)}), bf16[64,1,3]{2,1,0:T(2,128)(2,1)S(1)}, u32[]{:S(2)}, u32[]{:S(2)}) %all-to-all-start.4) | async-done | bytes 416 | tf_op jit(solution)/shard_map/all_to_all | solution.py:126
  298.5 5.6 %all-to-all-start.3 = ((bf16[64,96,128]{2,1,0:T(8,128)(2,1)}), bf16[64,96,128]{2,1,0:T(8,128)(2,1)S(1)}, u32[]{:S(2)}, u32[]{:S(2)}) async-start(bf16[64,96,128]{2,1,0:T(8,128)(2,1)} %reshape.84), calls=%async_computation.3 | async-start | bytes 3145728 | tf_op jit(solution)/shard_map/all_to_all | solution.py:125
  304.0 5.6 %fusion.7 = bf16[1,4096,192]{1,2,0:T(8,128)(2,1)} fusion(bf16[768,192]{0,1:T(8,128)(2,1)} %copy-done.6, bf16[768,4096]{1,0:T(8,128)(2,1)} %copy-done.5), kind=kOutput, calls=%fused_computation.21 | convolution fusion | flops 1208745984 | bytes 8159232 | tf_op jit(solution)/shard_map/dot_general | solution.py:117
  309.6 5.5 %fusion.8 = bf16[1,4096,192]{1,2,0:T(8,128)(2,1)} fusion(bf16[768,192]{0,1:T(8,128)(2,1)S(1)} %get-tuple-element.16, bf16[768,4096]{1,0:T(8,128)(2,1)} %copy-done.5), kind=kOutput, calls=%fused_computation.22 | convolution fusion | flops 1208745984 | bytes 8159232 | tf_op jit(solution)/shard_map/dot_general | solution.py:120
  318.7 25.4 %all-to-all-done.3 = bf16[64,96,128]{2,1,0:T(8,128)(2,1)S(1)} async-done(((bf16[64,96,128]{2,1,0:T(8,128)(2,1)}), bf16[64,96,128]{2,1,0:T(8,128)(2,1)S(1)}, u32[]{:S(2)}, u32[]{:S(2)}) %all-to-all-start.3) | async-done | bytes 1572896 | tf_op jit(solution)/shard_map/all_to_all | solution.py:125
  (95 shorter events, 61.8 us)
Async XLA Ops:
  0.6 182.4 %copy-start = (bf16[1,4096,192]{1,2,0:T(8,128)(2,1)S(1)}, bf16[1,4096,192]{1,2,0:T(8,128)(2,1)}, u32[]{:S(2)}) copy-start(bf16[1,4096,192]{1,2,0:T(8,128)(2,1)} %param.11) | copy-start | bytes 4718596
  4.8 20.7 %all-to-all-start.1 = ((bf16[64,1,3]{2,1,0:T(2,128)(2,1)}), bf16[64,1,3]{2,1,0:T(2,128)(2,1)S(1)}, u32[]{:S(2)}, u32[]{:S(2)}) async-start(bf16[64,1,3]{2,1,0:T(2,128)(2,1)} %all_to_all.28), calls=%async_computation.1 | async-start | bytes 65536 | tf_op jit(solution)/shard_map/all_to_all | solution.py:76
  25.5 45.7 %all-to-all-start.2 = ((bf16[64,96,128]{2,1,0:T(8,128)(2,1)}), bf16[64,96,128]{2,1,0:T(8,128)(2,1)S(1)}, u32[]{:S(2)}, u32[]{:S(2)}) async-start(bf16[64,96,128]{2,1,0:T(8,128)(2,1)} %reshape.82), calls=%async_computation.2 | async-start | bytes 3145728 | tf_op jit(solution)/shard_map/all_to_all | solution.py:74
  71.1 45.5 %all-to-all-start = ((bf16[64,96,128]{2,1,0:T(8,128)(2,1)}), bf16[64,96,128]{2,1,0:T(8,128)(2,1)}, u32[]{:S(2)}, u32[]{:S(2)}) async-start(bf16[64,96,128]{2,1,0:T(8,128)(2,1)} %reshape.79), calls=%async_computation | async-start | bytes 3145728 | tf_op jit(solution)/shard_map/all_to_all | solution.py:75
  79.6 45.5 %collective-permute-start.5 = (bf16[192,4096]{1,0:T(8,128)(2,1)S(1)}, bf16[192,4096]{1,0:T(8,128)(2,1)}, u32[]{:S(2)}, u32[]{:S(2)}) collective-permute-start(bf16[192,4096]{1,0:T(8,128)(2,1)S(1)} %reshape.83), channel_id=1, source_target_pairs={{0,64},{64,128},{128,192},{192,0},{1,65},{65,129},{129,193},{193,1... | collective-permute-start | bytes 4718600 | tf_op jit(solution)/shard_map/ppermute | solution.py:18
  81.1 46.0 %collective-permute-start.4 = (bf16[192,4096]{1,0:T(8,128)(2,1)S(1)}, bf16[192,4096]{1,0:T(8,128)(2,1)}, u32[]{:S(2)}, u32[]{:S(2)}) collective-permute-start(bf16[192,4096]{1,0:T(8,128)(2,1)S(1)} %reshape.83), channel_id=1, source_target_pairs={{0,192},{64,0},{128,64},{192,128},{1,193},{65,1},{129,65},{193,129... | collective-permute-start | bytes 4718600 | tf_op jit(solution)/shard_map/ppermute | solution.py:19
  122.1 38.7 %collective-permute-start = (bf16[192,4224]{1,0:T(8,128)(2,1)S(1)}, bf16[192,4224]{1,0:T(8,128)(2,1)S(1)}, u32[]{:S(2)}, u32[]{:S(2)}) collective-permute-start(bf16[192,4224]{1,0:T(8,128)(2,1)S(1)} %get-tuple-element.14), channel_id=1, source_target_pairs={{0,192},{64,0},{128,64},{192,128},{1,193},{65,1},{129,65},{193,129... | collective-permute-start | bytes 4866056 | tf_op jit(solution)/shard_map/ppermute | solution.py:19
  125.0 39.7 %collective-permute-start.1 = (bf16[192,4224]{1,0:T(8,128)(2,1)S(1)}, bf16[192,4224]{1,0:T(8,128)(2,1)S(1)}, u32[]{:S(2)}, u32[]{:S(2)}) collective-permute-start(bf16[192,4224]{1,0:T(8,128)(2,1)S(1)} %get-tuple-element.14), channel_id=1, source_target_pairs={{0,64},{64,128},{128,192},{192,0},{1,65},{65,129},{129,193},{193,1... | collective-permute-start | bytes 4866056 | tf_op jit(solution)/shard_map/ppermute | solution.py:18
  126.3 55.1 %collective-permute-start.6 = (bf16[96,4096]{1,0:T(8,128)(2,1)S(1)}, bf16[96,4096]{1,0:T(8,128)(2,1)S(1)}, u32[]{:S(2)}, u32[]{:S(2)}) collective-permute-start(bf16[96,4096]{1,0:T(8,128)(2,1)S(1)} %slice.77), channel_id=1, source_target_pairs={{0,64},{64,128},{128,192},{192,0},{1,65},{65,129},{129,193},{193,1... | collective-permute-start | bytes 2359304 | tf_op jit(solution)/shard_map/ppermute | solution.py:20
  128.3 53.1 %collective-permute-start.7 = (bf16[96,4096]{1,0:T(8,128)(2,1)S(1)}, bf16[96,4096]{1,0:T(8,128)(2,1)S(1)}, u32[]{:S(2)}, u32[]{:S(2)}) collective-permute-start(bf16[96,4096]{1,0:T(8,128)(2,1)S(1)} %slice.78), channel_id=1, source_target_pairs={{0,192},{64,0},{128,64},{192,128},{1,193},{65,1},{129,65},{193,129... | collective-permute-start | bytes 2359304 | tf_op jit(solution)/shard_map/ppermute | solution.py:21
  160.9 35.1 %collective-permute-start.3 = (bf16[96,4224]{1,0:T(8,128)(2,1)S(1)}, bf16[96,4224]{1,0:T(8,128)(2,1)S(1)}, u32[]{:S(2)}, u32[]{:S(2)}) collective-permute-start(bf16[96,4224]{1,0:T(8,128)(2,1)S(1)} %slice.74), channel_id=1, source_target_pairs={{0,192},{64,0},{128,64},{192,128},{1,193},{65,1},{129,65},{193,129... | collective-permute-start | bytes 2433032 | tf_op jit(solution)/shard_map/ppermute | solution.py:21
  164.7 31.2 %collective-permute-start.2 = (bf16[96,4224]{1,0:T(8,128)(2,1)S(1)}, bf16[96,4224]{1,0:T(8,128)(2,1)S(1)}, u32[]{:S(2)}, u32[]{:S(2)}) collective-permute-start(bf16[96,4224]{1,0:T(8,128)(2,1)S(1)} %slice.73), channel_id=1, source_target_pairs={{0,64},{64,128},{128,192},{192,0},{1,65},{65,129},{129,193},{193,1... | collective-permute-start | bytes 2433032 | tf_op jit(solution)/shard_map/ppermute | solution.py:20
  187.9 8.5 %copy-start.7 = (bf16[1,192,4096]{2,1,0:T(8,128)(2,1)S(1)}, bf16[1,192,4096]{2,1,0:T(8,128)(2,1)}, u32[]{:S(2)}) copy-start(bf16[1,192,4096]{2,1,0:T(8,128)(2,1)} %param.13) | copy-start | bytes 4718596
  218.2 18.5 %collective-permute-start.8 = (bf16[96,4224]{1,0:T(8,128)(2,1)S(1)}, bf16[96,4224]{1,0:T(8,128)(2,1)S(1)}, u32[]{:S(2)}, u32[]{:S(2)}) collective-permute-start(bf16[96,4224]{1,0:T(8,128)(2,1)S(1)} %get-tuple-element.9), channel_id=1, source_target_pairs={{0,64},{64,128},{128,192},{192,0},{1,65},{65,129},{129,193},{193,1... | collective-permute-start | bytes 2433032 | tf_op jit(solution)/shard_map/ppermute | solution.py:32
  218.3 58.5 %slice-start = ((s8[12582912]{0:T(1024)(128)(4,1)}), s8[4194304]{0:T(1024)(128)(4,1)S(1)}, s32[]{:S(2)}) async-start(s8[12582912]{0:T(1024)(128)(4,1)} %bitcast.47), calls=%async_computation.5 | async-start | bytes 8388608
  218.3 58.5 %slice-start.1 = ((s8[12582912]{0:T(1024)(128)(4,1)}), s8[4194304]{0:T(1024)(128)(4,1)S(1)}, s32[]{:S(2)}) async-start(s8[12582912]{0:T(1024)(128)(4,1)} %bitcast.47), calls=%async_computation.6 | async-start | bytes 8388608
  218.3 58.5 %slice-start.2 = ((s8[12582912]{0:T(1024)(128)(4,1)}), s8[4194304]{0:T(1024)(128)(4,1)S(1)}, s32[]{:S(2)}) async-start(s8[12582912]{0:T(1024)(128)(4,1)} %bitcast.47), calls=%async_computation.7 | async-start | bytes 8388608
  218.3 18.4 %collective-permute-start.10 = (bf16[96,4224]{1,0:T(8,128)(2,1)S(1)}, bf16[96,4224]{1,0:T(8,128)(2,1)S(1)}, u32[]{:S(2)}, u32[]{:S(2)}) collective-permute-start(bf16[96,4224]{1,0:T(8,128)(2,1)S(1)} %get-tuple-element.10), channel_id=1, source_target_pairs={{0,192},{64,0},{128,64},{192,128},{1,193},{65,1},{129,65},{193,129... | collective-permute-start | bytes 2433032 | tf_op jit(solution)/shard_map/ppermute | solution.py:33
  239.1 34.1 %collective-permute-start.11 = (bf16[192,4224]{1,0:T(8,128)(2,1)S(1)}, bf16[192,4224]{1,0:T(8,128)(2,1)S(1)}, u32[]{:S(2)}, u32[]{:S(2)}) collective-permute-start(bf16[192,4224]{1,0:T(8,128)(2,1)S(1)} %pad_maximum_fusion.3), channel_id=1, source_target_pairs={{0,192},{64,0},{128,64},{192,128},{1,193},{65,1},{129,65},{193,129... | collective-permute-start | bytes 4866056 | tf_op jit(solution)/shard_map/ppermute | solution.py:37
  242.3 34.5 %collective-permute-start.9 = (bf16[192,4224]{1,0:T(8,128)(2,1)S(1)}, bf16[192,4224]{1,0:T(8,128)(2,1)S(1)}, u32[]{:S(2)}, u32[]{:S(2)}) collective-permute-start(bf16[192,4224]{1,0:T(8,128)(2,1)S(1)} %pad_maximum_fusion.2), channel_id=1, source_target_pairs={{0,64},{64,128},{128,192},{192,0},{1,65},{65,129},{129,193},{193,1... | collective-permute-start | bytes 4866056 | tf_op jit(solution)/shard_map/ppermute | solution.py:36
  278.3 20.2 %all-to-all-start.4 = ((bf16[64,1,3]{2,1,0:T(2,128)(2,1)}), bf16[64,1,3]{2,1,0:T(2,128)(2,1)S(1)}, u32[]{:S(2)}, u32[]{:S(2)}) async-start(bf16[64,1,3]{2,1,0:T(2,128)(2,1)} %all_to_all.29), calls=%async_computation.4 | async-start | bytes 65536 | tf_op jit(solution)/shard_map/all_to_all | solution.py:126
  298.5 45.7 %all-to-all-start.3 = ((bf16[64,96,128]{2,1,0:T(8,128)(2,1)}), bf16[64,96,128]{2,1,0:T(8,128)(2,1)S(1)}, u32[]{:S(2)}, u32[]{:S(2)}) async-start(bf16[64,96,128]{2,1,0:T(8,128)(2,1)} %reshape.84), calls=%async_computation.3 | async-start | bytes 3145728 | tf_op jit(solution)/shard_map/all_to_all | solution.py:125
  304.0 11.1 %slice-start.3 = ((s8[6488064]{0:T(1024)(128)(4,1)}), s8[4194304]{0:T(1024)(128)(4,1)S(1)}, s32[]{:S(2)}) async-start(s8[6488064]{0:T(1024)(128)(4,1)} %bitcast.49), calls=%async_computation.8 | async-start | bytes 8388608
  315.1 33.9 %copy-start.1 = (bf16[1,4096,192]{1,2,0:T(8,128)(2,1)S(1)}, bf16[1,4096,192]{1,2,0:T(8,128)(2,1)}, u32[]{:S(2)}) copy-start(bf16[1,4096,192]{1,2,0:T(8,128)(2,1)} %param.11) | copy-start | bytes 4718596
  (7 other events, 27.2 us)

commit v4 on v3

--- a/solution.py
+++ b/solution.py
@@ -61,26 +61,18 @@
         .astype(jnp.bfloat16)
         .reshape(expert_count, per_peer, LANES)
     )
+    weighted = jnp.sum(
+        placing.reshape(slot_total, tok_count, top_count) * gate_probs[None, :, :], axis=2
+    )
     sent_dy = (
-        jnp.dot(collect, out_grad, preferred_element_type=jnp.float32)
+        jnp.dot(weighted, out_grad, preferred_element_type=jnp.float32)
         .astype(jnp.bfloat16)
         .reshape(expert_count, per_peer, LANES)
     )
-    sent_prob = (
-        jnp.dot(placing, gate_probs.reshape(-1), preferred_element_type=jnp.float32)
-        .astype(jnp.bfloat16)
-        .reshape(expert_count, capacity)
-    )
     recv_in = lax.all_to_all(sent_in, "expert", 0, 0, tiled=True).reshape(slot_total, width)
     recv_dy = lax.all_to_all(sent_dy, "expert", 0, 0, tiled=True).reshape(slot_total, width)
-    recv_prob = lax.all_to_all(sent_prob, "expert", 0, 0, tiled=True).reshape(slot_total)
-    dy_ext = jnp.concatenate(
-        [recv_dy, jnp.broadcast_to(recv_prob[:, None], (slot_total, LANES))], axis=1
-    )
     rows_in = ring_gather(recv_in, "dp")
-    rows_dy_ext = ring_gather(dy_ext, "dp")
-    rows_dy = rows_dy_ext[:, :width]
-    rows_prob = rows_dy_ext[:, width]
+    rows_dy = ring_gather(recv_dy, "dp")
     gate_w = w_gate[0]
     up_w = w_up[0]
     down_w = w_down[0]
@@ -91,11 +83,11 @@
     sigmoid_gate = jax.nn.sigmoid(gate_pre)
     active = gate_pre * sigmoid_gate
     hidden = (active * up_pre).astype(jnp.bfloat16)
-    back_raw = lax.dot_general(rows_dy, down_w, contract_last, preferred_element_type=jnp.float32)
-    score_part = jnp.sum(back_raw * hidden.astype(jnp.float32), axis=1)
-    weight_col = rows_prob.astype(jnp.float32)[:, None]
-    scaled = (weight_col * rows_dy.astype(jnp.float32)).astype(jnp.bfloat16)
-    back_hidden = weight_col * back_raw
+    back_hidden = lax.dot_general(
+        rows_dy, down_w, contract_last, preferred_element_type=jnp.float32
+    )
+    score_part = jnp.sum(back_hidden * hidden.astype(jnp.float32), axis=1)
+    scaled = rows_dy
     grad_gate_pre = (
         back_hidden * up_pre * sigmoid_gate * (1.0 + gate_pre * (1.0 - sigmoid_gate))
     ).astype(jnp.bfloat16)
@@ -121,14 +113,19 @@
         rows_in, grad_up_pre, contract_first, preferred_element_type=jnp.float32
     ).astype(jnp.bfloat16)
     own_rows = own_ext[:, :width].reshape(expert_count, per_peer, LANES)
-    own_scores = own_ext[:, width].reshape(expert_count, capacity)
-    back_rows = lax.all_to_all(own_rows, "expert", 0, 0, tiled=True).reshape(slot_total, width)
-    back_scores = lax.all_to_all(own_scores, "expert", 0, 0, tiled=True).reshape(slot_total)
+    own_scores = own_ext[:, width].reshape(expert_count, 1, capacity)
+    score_tile = jnp.pad(own_scores, ((0, 0), (0, 15), (0, LANES - capacity)))
+    back_ext = lax.all_to_all(
+        jnp.concatenate([own_rows, score_tile], axis=1), "expert", 0, 0, tiled=True
+    )
+    back_rows = back_ext[:, :per_peer].reshape(slot_total, width)
+    back_scores = back_ext[:, per_peer, :capacity].reshape(slot_total)
     grad_tokens = lax.dot_general(
         collect, back_rows, contract_first, preferred_element_type=jnp.float32
     ).astype(jnp.bfloat16)
+    weighted_scores = jnp.dot(back_scores, placing, preferred_element_type=jnp.float32)
     grad_probs = (
-        jnp.dot(back_scores, placing, preferred_element_type=jnp.float32)
+        (weighted_scores / gate_probs.reshape(-1).astype(jnp.float32))
         .astype(jnp.bfloat16)
         .reshape(tok_count, top_count)
     )

time: 350 us -> 333 us (0.951)
  starting transfers between devices: 60.5 us -> 49.3 us
    ppermute x2, waiting for transfers between devices: 28.4 us -> 0.01 us  [ring_gather(): from_next = lax.ppermute(x, axis, bwd)]
    ppermute x2, waiting for transfers between devices: 0.01 us -> 27.8 us  [ring_gather(): from_prev = lax.ppermute(x, axis, fwd)]
    all_to_all x3 -> x1, starting transfers between devices: 29.3 us -> 11.6 us  [body(): lax.all_to_all(jnp.concatenate([own_rows, score_tile], axis=1), 'expert',...]
    all_to_all x1, starting transfers between devices: 5.6 us -> 12.1 us  [body(): lax.all_to_all(sent_dy, 'expert', 0, 0, tiled=True)]
    all_to_all x3 -> x1, waiting for transfers between devices: 36.4 us -> 32 us  [body(): lax.all_to_all(jnp.concatenate([own_rows, score_tile], axis=1), 'expert',...]
  transfers between devices with their start and end apart: 17 -> 15, of which waited for: 11 -> 8; matrix products, arithmetic and copies ran while one was open for 13% -> 11% of each run, Pallas kernels for 0% -> 0%
where the time goes in v4:
time: 333 us; the launch traced here: 332 us
  waiting for transfers between devices  204 us (61%)
  starting transfers between devices  49.3 us (15%)
  matrix products  36.2 us (11%)
  local copies, waits for them, and re-layouts  26.2 us (8%)
  other arithmetic  15 us (5%)
    all_to_all x1, waiting for transfers between devices, body(): lax.all_to_all(sent_in, 'expert', 0, 0, tiled=True)  34.6 us
    all_to_all x1, waiting for transfers between devices, body(): lax.all_to_all(sent_dy, 'expert', 0, 0, tiled=True)  33.3 us
    all_to_all x1, waiting for transfers between devices, body(): lax.all_to_all(jnp.concatenate([own_rows, score_tile], axis=1), 'expert',...  32 us
    ppermute x1, waiting for transfers between devices, ring_reduce_scatter(): lax.ppermute(send_prev.astype(jnp.bfloat16), axis, bwd).astype(jnp.float32)  31.1 us
    ppermute x2, waiting for transfers between devices, ring_gather(): from_prev = lax.ppermute(x, axis, fwd)  27.8 us
    ppermute x2, waiting for transfers between devices, ring_gather(): far_a = lax.ppermute(from_prev[:half], axis, fwd)  25.8 us
    ppermute x1, waiting for transfers between devices, ring_reduce_scatter(): lax.ppermute(far[:half].astype(jnp.bfloat16), axis, fwd).astype(jnp.float32)  15.5 us
    all_to_all x1, starting transfers between devices, body(): lax.all_to_all(sent_dy, 'expert', 0, 0, tiled=True)  12.1 us
  transfers between devices with their start and end apart: 15, of which 8 were waited for; matrix products, arithmetic and copies ran while one was open for 11% of the time, Pallas kernels for 0%

profile of v4, /device:TPU:8, one launch (start us, length us, event | category | flops | bytes accessed | tf_op | source)
XLA Modules:
  0.0 331.7 jit_solution(17146042901190924641)
XLA Ops:
  7.1 12.1 %all-to-all-start = ((bf16[64,96,128]{2,1,0:T(8,128)(2,1)}), bf16[64,96,128]{2,1,0:T(8,128)(2,1)S(1)}, u32[]{:S(2)}, u32[]{:S(2)}) async-start(bf16[64,96,128]{2,1,0:T(8,128)(2,1)} %reshape.89), calls=%async_computation | async-start | bytes 3145728 | tf_op jit(solution)/shard_map/all_to_all | solution.py:73
  19.2 2.9 convolution_convert_fusion.3
  22.1 3.7 %reshape.91 = bf16[64,96,128]{2,1,0:T(8,128)(2,1)} reshape(bf16[192,4096]{1,0:T(8,128)(2,1)} %convolution_convert_fusion.3) | data formatting | bytes 3145728 | tf_op jit(solution)/shard_map/reshape | solution.py:62
  25.9 33.3 %all-to-all-done = bf16[64,96,128]{2,1,0:T(8,128)(2,1)S(1)} async-done(((bf16[64,96,128]{2,1,0:T(8,128)(2,1)}), bf16[64,96,128]{2,1,0:T(8,128)(2,1)S(1)}, u32[]{:S(2)}, u32[]{:S(2)}) %all-to-all-start) | async-done | bytes 1572896 | tf_op jit(solution)/shard_map/all_to_all | solution.py:73
  59.2 5.6 %all-to-all-start.1 = ((bf16[64,96,128]{2,1,0:T(8,128)(2,1)}), bf16[64,96,128]{2,1,0:T(8,128)(2,1)}, u32[]{:S(2)}, u32[]{:S(2)}) async-start(bf16[64,96,128]{2,1,0:T(8,128)(2,1)} %reshape.91), calls=%async_computation.1 | async-start | bytes 3145728 | tf_op jit(solution)/shard_map/all_to_all | solution.py:72
  70.1 34.6 %all-to-all-done.1 = bf16[64,96,128]{2,1,0:T(8,128)(2,1)} async-done(((bf16[64,96,128]{2,1,0:T(8,128)(2,1)}), bf16[64,96,128]{2,1,0:T(8,128)(2,1)}, u32[]{:S(2)}, u32[]{:S(2)}) %all-to-all-start.1) | async-done | bytes 1572896 | tf_op jit(solution)/shard_map/all_to_all | solution.py:72
  104.7 2.5 reshape.92
  115.0 3.0 collective-permute-start.3
  118.0 27.8 %collective-permute-done.5 = bf16[192,4096]{1,0:T(8,128)(2,1)S(1)} collective-permute-done((bf16[192,4096]{1,0:T(8,128)(2,1)S(1)}, bf16[192,4096]{1,0:T(8,128)(2,1)S(1)}, u32[]{:S(2)}, u32[]{:S(2)}) %collective-permute-start.5) | collective-permute-done | bytes 1572896 | tf_op jit(solution)/shard_map/ppermute | solution.py:18
  146.3 3.2 collective-permute-start.7
  151.2 25.8 %collective-permute-done.6 = bf16[96,4096]{1,0:T(8,128)(2,1)S(1)} collective-permute-done((bf16[96,4096]{1,0:T(8,128)(2,1)S(1)}, bf16[96,4096]{1,0:T(8,128)(2,1)S(1)}, u32[]{:S(2)}, u32[]{:S(2)}) %collective-permute-start.6) | collective-permute-done | bytes 786464 | tf_op jit(solution)/shard_map/ppermute | solution.py:20
  184.0 3.2 multiply_reduce_fusion
  189.1 6.4 %convolution_add_fusion = f32[768,4096]{1,0:T(8,128)} fusion(f32[768,4096]{1,0:T(8,128)S(1)} %fusion.16, bf16[768,192]{0,1:T(8,128)(2,1)S(1)} %get-tuple-element.14, bf16[1,4096,192]{1,2,0:T(8,128)(2,1)S(1)} %copy-done.2), kind=kOutput, calls=%fused_computation.8 | convolution fusion | flops 1211105280 | bytes 27033600 | tf_op jit(solution)/shard_map/dot_general | solution.py:98
  195.6 8.1 %fusion = bf16[768,4224]{1,0:T(8,128)(2,1)} fusion(f32[768,128]{1,0:T(8,128)S(1)} %broadcast_in_dim.8, f32[768,4096]{1,0:T(8,128)} %convolution_add_fusion), kind=kLoop, calls=%fused_computation.4 | loop fusion | flops 12976128 | bytes 19464192 | tf_op jit(solution)/shard_map/convert.7
  209.2 15.5 %collective-permute-done.8 = bf16[96,4224]{1,0:T(8,128)(2,1)S(1)} collective-permute-done((bf16[96,4224]{1,0:T(8,128)(2,1)S(1)}, bf16[96,4224]{1,0:T(8,128)(2,1)S(1)}, u32[]{:S(2)}, u32[]{:S(2)}) %collective-permute-start.8) | collective-permute-done | bytes 811040 | tf_op jit(solution)/shard_map/ppermute | solution.py:32
  227.0 3.1 collective-permute-start.11
  230.3 31.1 %collective-permute-done.11 = bf16[192,4224]{1,0:T(8,128)(2,1)S(1)} collective-permute-done((bf16[192,4224]{1,0:T(8,128)(2,1)S(1)}, bf16[192,4224]{1,0:T(8,128)(2,1)S(1)}, u32[]{:S(2)}, u32[]{:S(2)}) %collective-permute-start.11) | collective-permute-done | bytes 1622048 | tf_op jit(solution)/shard_map/ppermute | solution.py:37
  261.4 3.6 %collective-permute-done.9 = bf16[192,4224]{1,0:T(8,128)(2,1)S(1)} collective-permute-done((bf16[192,4224]{1,0:T(8,128)(2,1)S(1)}, bf16[192,4224]{1,0:T(8,128)(2,1)S(1)}, u32[]{:S(2)}, u32[]{:S(2)}) %collective-permute-start.9) | collective-permute-done | bytes 1622048 | tf_op jit(solution)/shard_map/ppermute | solution.py:36
  268.2 11.6 %all-to-all-start.2 = ((bf16[64,112,128]{2,1,0:T(8,128)(2,1)}), bf16[64,112,128]{2,1,0:T(8,128)(2,1)S(1)}, u32[]{:S(2)}, u32[]{:S(2)}) async-start(bf16[64,112,128]{2,1,0:T(8,128)(2,1)} %fusion.9), calls=%async_computation.2 | async-start | bytes 3670016 | tf_op jit(solution)/shard_map/all_to_all | solution.py:118
  279.9 5.5 %fusion.2 = bf16[1,4096,192]{1,2,0:T(8,128)(2,1)} fusion(bf16[768,192]{0,1:T(8,128)(2,1)S(1)} %copy-done.8, bf16[768,4096]{1,0:T(8,128)(2,1)} %copy-done.5), kind=kOutput, calls=%fused_computation.16 | convolution fusion | flops 1208745984 | bytes 8159232 | tf_op jit(solution)/shard_map/dot_general | solution.py:109
  285.4 5.5 %fusion.3 = bf16[1,4096,192]{1,2,0:T(8,128)(2,1)} fusion(bf16[768,192]{0,1:T(8,128)(2,1)S(1)} %copy-done.4, bf16[768,4096]{1,0:T(8,128)(2,1)} %copy-done.5), kind=kOutput, calls=%fused_computation.17 | convolution fusion | flops 1208745984 | bytes 8159232 | tf_op jit(solution)/shard_map/dot_general | solution.py:112
  290.9 2.6 fusion.1
  293.4 32.0 %all-to-all-done.2 = bf16[64,112,128]{2,1,0:T(8,128)(2,1)S(1)} async-done(((bf16[64,112,128]{2,1,0:T(8,128)(2,1)}), bf16[64,112,128]{2,1,0:T(8,128)(2,1)S(1)}, u32[]{:S(2)}, u32[]{:S(2)}) %all-to-all-start.2) | async-done | bytes 1835040 | tf_op jit(solution)/shard_map/all_to_all | solution.py:118
  327.7 2.5 reshape.94
  (92 shorter events, 45.3 us)
Async XLA Ops:
  0.6 176.6 %copy-start = (bf16[1,4096,192]{1,2,0:T(8,128)(2,1)S(1)}, bf16[1,4096,192]{1,2,0:T(8,128)(2,1)}, u32[]{:S(2)}) copy-start(bf16[1,4096,192]{1,2,0:T(8,128)(2,1)} %param.11) | copy-start | bytes 4718596
  7.1 52.1 %all-to-all-start = ((bf16[64,96,128]{2,1,0:T(8,128)(2,1)}), bf16[64,96,128]{2,1,0:T(8,128)(2,1)S(1)}, u32[]{:S(2)}, u32[]{:S(2)}) async-start(bf16[64,96,128]{2,1,0:T(8,128)(2,1)} %reshape.89), calls=%async_computation | async-start | bytes 3145728 | tf_op jit(solution)/shard_map/all_to_all | solution.py:73
  59.2 45.5 %all-to-all-start.1 = ((bf16[64,96,128]{2,1,0:T(8,128)(2,1)}), bf16[64,96,128]{2,1,0:T(8,128)(2,1)}, u32[]{:S(2)}, u32[]{:S(2)}) async-start(bf16[64,96,128]{2,1,0:T(8,128)(2,1)} %reshape.91), calls=%async_computation.1 | async-start | bytes 3145728 | tf_op jit(solution)/shard_map/all_to_all | solution.py:72
  66.8 45.4 %collective-permute-start.1 = (bf16[192,4096]{1,0:T(8,128)(2,1)}, bf16[192,4096]{1,0:T(8,128)(2,1)}, u32[]{:S(2)}, u32[]{:S(2)}) collective-permute-start(bf16[192,4096]{1,0:T(8,128)(2,1)} %reshape.90), channel_id=1, source_target_pairs={{0,64},{64,128},{128,192},{192,0},{1,65},{65,129},{129,193},{193,1... | collective-permute-start | bytes 4718600 | tf_op jit(solution)/shard_map/ppermute | solution.py:18
  68.3 45.5 %collective-permute-start = (bf16[192,4096]{1,0:T(8,128)(2,1)}, bf16[192,4096]{1,0:T(8,128)(2,1)}, u32[]{:S(2)}, u32[]{:S(2)}) collective-permute-start(bf16[192,4096]{1,0:T(8,128)(2,1)} %reshape.90), channel_id=1, source_target_pairs={{0,192},{64,0},{128,64},{192,128},{1,193},{65,1},{129,65},{193,129... | collective-permute-start | bytes 4718600 | tf_op jit(solution)/shard_map/ppermute | solution.py:19
  107.3 38.6 %collective-permute-start.5 = (bf16[192,4096]{1,0:T(8,128)(2,1)S(1)}, bf16[192,4096]{1,0:T(8,128)(2,1)S(1)}, u32[]{:S(2)}, u32[]{:S(2)}) collective-permute-start(bf16[192,4096]{1,0:T(8,128)(2,1)S(1)} %reshape.92), channel_id=1, source_target_pairs={{0,64},{64,128},{128,192},{192,0},{1,65},{65,129},{129,193},{193,1... | collective-permute-start | bytes 4718600 | tf_op jit(solution)/shard_map/ppermute | solution.py:18
  108.9 37.4 %collective-permute-start.4 = (bf16[192,4096]{1,0:T(8,128)(2,1)S(1)}, bf16[192,4096]{1,0:T(8,128)(2,1)S(1)}, u32[]{:S(2)}, u32[]{:S(2)}) collective-permute-start(bf16[192,4096]{1,0:T(8,128)(2,1)S(1)} %reshape.92), channel_id=1, source_target_pairs={{0,192},{64,0},{128,64},{192,128},{1,193},{65,1},{129,65},{193,129... | collective-permute-start | bytes 4718600 | tf_op jit(solution)/shard_map/ppermute | solution.py:19
  113.5 66.1 %collective-permute-start.2 = (bf16[96,4096]{1,0:T(8,128)(2,1)S(1)}, bf16[96,4096]{1,0:T(8,128)(2,1)S(1)}, u32[]{:S(2)}, u32[]{:S(2)}) collective-permute-start(bf16[96,4096]{1,0:T(8,128)(2,1)S(1)} %slice.73), channel_id=1, source_target_pairs={{0,64},{64,128},{128,192},{192,0},{1,65},{65,129},{129,193},{193,1... | collective-permute-start | bytes 2359304 | tf_op jit(solution)/shard_map/ppermute | solution.py:20
  115.0 67.1 %collective-permute-start.3 = (bf16[96,4096]{1,0:T(8,128)(2,1)S(1)}, bf16[96,4096]{1,0:T(8,128)(2,1)S(1)}, u32[]{:S(2)}, u32[]{:S(2)}) collective-permute-start(bf16[96,4096]{1,0:T(8,128)(2,1)S(1)} %slice.74), channel_id=1, source_target_pairs={{0,192},{64,0},{128,64},{192,128},{1,193},{65,1},{129,65},{193,129... | collective-permute-start | bytes 2359304 | tf_op jit(solution)/shard_map/ppermute | solution.py:21
  145.9 31.1 %collective-permute-start.6 = (bf16[96,4096]{1,0:T(8,128)(2,1)S(1)}, bf16[96,4096]{1,0:T(8,128)(2,1)S(1)}, u32[]{:S(2)}, u32[]{:S(2)}) collective-permute-start(bf16[96,4096]{1,0:T(8,128)(2,1)S(1)} %slice.75), channel_id=1, source_target_pairs={{0,64},{64,128},{128,192},{192,0},{1,65},{65,129},{129,193},{193,1... | collective-permute-start | bytes 2359304 | tf_op jit(solution)/shard_map/ppermute | solution.py:20
  146.3 30.7 %collective-permute-start.7 = (bf16[96,4096]{1,0:T(8,128)(2,1)S(1)}, bf16[96,4096]{1,0:T(8,128)(2,1)S(1)}, u32[]{:S(2)}, u32[]{:S(2)}) collective-permute-start(bf16[96,4096]{1,0:T(8,128)(2,1)S(1)} %slice.76), channel_id=1, source_target_pairs={{0,192},{64,0},{128,64},{192,128},{1,193},{65,1},{129,65},{193,129... | collective-permute-start | bytes 2359304 | tf_op jit(solution)/shard_map/ppermute | solution.py:21
  205.8 18.8 %collective-permute-start.8 = (bf16[96,4224]{1,0:T(8,128)(2,1)S(1)}, bf16[96,4224]{1,0:T(8,128)(2,1)S(1)}, u32[]{:S(2)}, u32[]{:S(2)}) collective-permute-start(bf16[96,4224]{1,0:T(8,128)(2,1)S(1)} %get-tuple-element.9), channel_id=1, source_target_pairs={{0,64},{64,128},{128,192},{192,0},{1,65},{65,129},{129,193},{193,1... | collective-permute-start | bytes 2433032 | tf_op jit(solution)/shard_map/ppermute | solution.py:32
  207.3 57.7 %slice-start = ((s8[12582912]{0:T(1024)(128)(4,1)}), s8[4194304]{0:T(1024)(128)(4,1)S(1)}, s32[]{:S(2)}) async-start(s8[12582912]{0:T(1024)(128)(4,1)} %bitcast.50), calls=%async_computation.3 | async-start | bytes 8388608
  207.3 57.7 %slice-start.1 = ((s8[12582912]{0:T(1024)(128)(4,1)}), s8[4194304]{0:T(1024)(128)(4,1)S(1)}, s32[]{:S(2)}) async-start(s8[12582912]{0:T(1024)(128)(4,1)} %bitcast.50), calls=%async_computation.4 | async-start | bytes 8388608
  207.3 57.7 %slice-start.2 = ((s8[12582912]{0:T(1024)(128)(4,1)}), s8[4194304]{0:T(1024)(128)(4,1)S(1)}, s32[]{:S(2)}) async-start(s8[12582912]{0:T(1024)(128)(4,1)} %bitcast.50), calls=%async_computation.5 | async-start | bytes 8388608
  207.3 17.3 %collective-permute-start.10 = (bf16[96,4224]{1,0:T(8,128)(2,1)S(1)}, bf16[96,4224]{1,0:T(8,128)(2,1)S(1)}, u32[]{:S(2)}, u32[]{:S(2)}) collective-permute-start(bf16[96,4224]{1,0:T(8,128)(2,1)S(1)} %get-tuple-element.10), channel_id=1, source_target_pairs={{0,192},{64,0},{128,64},{192,128},{1,193},{65,1},{129,65},{193,129... | collective-permute-start | bytes 2433032 | tf_op jit(solution)/shard_map/ppermute | solution.py:33
  227.0 34.4 %collective-permute-start.11 = (bf16[192,4224]{1,0:T(8,128)(2,1)S(1)}, bf16[192,4224]{1,0:T(8,128)(2,1)S(1)}, u32[]{:S(2)}, u32[]{:S(2)}) collective-permute-start(bf16[192,4224]{1,0:T(8,128)(2,1)S(1)} %pad_maximum_fusion.2), channel_id=1, source_target_pairs={{0,192},{64,0},{128,64},{192,128},{1,193},{65,1},{129,65},{193,129... | collective-permute-start | bytes 4866056 | tf_op jit(solution)/shard_map/ppermute | solution.py:37
  230.2 34.8 %collective-permute-start.9 = (bf16[192,4224]{1,0:T(8,128)(2,1)S(1)}, bf16[192,4224]{1,0:T(8,128)(2,1)S(1)}, u32[]{:S(2)}, u32[]{:S(2)}) collective-permute-start(bf16[192,4224]{1,0:T(8,128)(2,1)S(1)} %pad_maximum_fusion.1), channel_id=1, source_target_pairs={{0,64},{64,128},{128,192},{192,0},{1,65},{65,129},{129,193},{193,1... | collective-permute-start | bytes 4866056 | tf_op jit(solution)/shard_map/ppermute | solution.py:36
  266.8 13.0 %copy-start.8 = (bf16[768,192]{0,1:T(8,128)(2,1)S(1)}, bf16[768,192]{0,1:T(8,128)(2,1)}, u32[]{:S(2)}) copy-start(bf16[768,192]{0,1:T(8,128)(2,1)} %copy-done.7) | copy-start | bytes 884740
  268.2 57.2 %all-to-all-start.2 = ((bf16[64,112,128]{2,1,0:T(8,128)(2,1)}), bf16[64,112,128]{2,1,0:T(8,128)(2,1)S(1)}, u32[]{:S(2)}, u32[]{:S(2)}) async-start(bf16[64,112,128]{2,1,0:T(8,128)(2,1)} %fusion.9), calls=%async_computation.2 | async-start | bytes 3670016 | tf_op jit(solution)/shard_map/all_to_all | solution.py:118
  279.8 5.5 %copy-start.4 = (bf16[768,192]{0,1:T(8,128)(2,1)S(1)}, bf16[768,192]{0,1:T(8,128)(2,1)}, u32[]{:S(2)}) copy-start(bf16[768,192]{0,1:T(8,128)(2,1)} %copy-done.3) | copy-start | bytes 884740
  279.9 11.0 %slice-start.3 = ((s8[6291456]{0:T(1024)(128)(4,1)}), s8[4194304]{0:T(1024)(128)(4,1)S(1)}, s32[]{:S(2)}) async-start(s8[6291456]{0:T(1024)(128)(4,1)} %bitcast.52), calls=%async_computation.6 | async-start | bytes 8388608
  285.4 5.5 %copy-start.11 = (bf16[768,192]{0,1:T(8,128)(2,1)S(1)}, bf16[768,192]{0,1:T(8,128)(2,1)}, u32[]{:S(2)}) copy-start(bf16[768,192]{0,1:T(8,128)(2,1)} %get-tuple-element.6) | copy-start | bytes 884740
  290.9 34.9 %copy-start.9 = (bf16[128,1]{0,1:T(2,128)(2,1)S(1)}, bf16[128,1]{0,1:T(2,128)(2,1)}, u32[]{:S(2)}) copy-start(bf16[128,1]{0,1:T(2,128)(2,1)} %param.10) | copy-start | bytes 772
  (8 other events, 24.8 us)

commit v5 on v4

--- a/solution.py
+++ b/solution.py
@@ -22,19 +22,18 @@
     return jnp.concatenate([x, from_next, far_a, far_b, from_prev], axis=0)
 
 
-def ring_reduce_scatter(parts, axis):
+def ring_reduce_scatter(blocks, axis, wire):
     count = lax.axis_size(axis)
     fwd = ring_pairs(count, 1)
     bwd = ring_pairs(count, -1)
-    block = parts.shape[0] // count
-    half = block // 2
-    own, to_next, far, to_prev = (parts[k * block:(k + 1) * block] for k in range(count))
-    got_a = lax.ppermute(far[:half].astype(jnp.bfloat16), axis, fwd).astype(jnp.float32)
-    got_b = lax.ppermute(far[half:].astype(jnp.bfloat16), axis, bwd).astype(jnp.float32)
+    own, to_next, far, to_prev = blocks
+    half = own.shape[0] // 2
+    got_a = lax.ppermute(far[:half].astype(wire), axis, fwd).astype(jnp.float32)
+    got_b = lax.ppermute(far[half:].astype(wire), axis, bwd).astype(jnp.float32)
     send_next = jnp.concatenate([to_next[:half] + got_a, to_next[half:]], axis=0)
     send_prev = jnp.concatenate([to_prev[:half], to_prev[half:] + got_b], axis=0)
-    from_prev = lax.ppermute(send_next.astype(jnp.bfloat16), axis, fwd).astype(jnp.float32)
-    from_next = lax.ppermute(send_prev.astype(jnp.bfloat16), axis, bwd).astype(jnp.float32)
+    from_prev = lax.ppermute(send_next.astype(wire), axis, fwd).astype(jnp.float32)
+    from_next = lax.ppermute(send_prev.astype(wire), axis, bwd).astype(jnp.float32)
     return own + from_prev + from_next
 
 
@@ -92,17 +91,22 @@
         back_hidden * up_pre * sigmoid_gate * (1.0 + gate_pre * (1.0 - sigmoid_gate))
     ).astype(jnp.bfloat16)
     grad_up_pre = (back_hidden * active).astype(jnp.bfloat16)
-    row_part = lax.dot_general(
-        grad_gate_pre, gate_w, contract_last, preferred_element_type=jnp.float32
-    )
-    row_part = row_part + lax.dot_general(
-        grad_up_pre, up_w, contract_last, preferred_element_type=jnp.float32
-    )
-    row_total = row_part.shape[0]
-    row_ext = jnp.concatenate(
-        [row_part, jnp.broadcast_to(score_part[:, None], (row_total, LANES))], axis=1
-    )
-    own_ext = ring_reduce_scatter(row_ext, "dp").astype(jnp.bfloat16)
+    row_total = grad_gate_pre.shape[0]
+    dp_count = lax.axis_size("dp")
+    block = row_total // dp_count
+    row_blocks = []
+    for k in range(dp_count):
+        rows = slice(k * block, (k + 1) * block)
+        part = lax.dot_general(
+            grad_gate_pre[rows], gate_w, contract_last, preferred_element_type=jnp.float32
+        )
+        part = part + lax.dot_general(
+            grad_up_pre[rows], up_w, contract_last, preferred_element_type=jnp.float32
+        )
+        row_blocks.append(part)
+    own_grad = ring_reduce_scatter(row_blocks, "dp", jnp.bfloat16).astype(jnp.bfloat16)
+    score_blocks = [score_part[k * block:(k + 1) * block, None] for k in range(dp_count)]
+    own_score = ring_reduce_scatter(score_blocks, "dp", jnp.float32).astype(jnp.bfloat16)
     grad_down = lax.dot_general(
         hidden, scaled, contract_first, preferred_element_type=jnp.float32
     ).astype(jnp.bfloat16)
@@ -112,8 +116,8 @@
     grad_up = lax.dot_general(
         rows_in, grad_up_pre, contract_first, preferred_element_type=jnp.float32
     ).astype(jnp.bfloat16)
-    own_rows = own_ext[:, :width].reshape(expert_count, per_peer, LANES)
-    own_scores = own_ext[:, width].reshape(expert_count, 1, capacity)
+    own_rows = own_grad.reshape(expert_count, per_peer, LANES)
+    own_scores = own_score.reshape(expert_count, 1, capacity)
     score_tile = jnp.pad(own_scores, ((0, 0), (0, 15), (0, LANES - capacity)))
     back_ext = lax.all_to_all(
         jnp.concatenate([own_rows, score_tile], axis=1), "expert", 0, 0, tiled=True

time: 333 us -> 324 us (0.973)
  waiting for transfers between devices: 204 us -> 196 us
  starting transfers between devices: 49.3 us -> 54.8 us
  other arithmetic: 15 us -> 10.5 us
    another operation x2, other arithmetic: 10.3 us -> 0.33 us
    ppermute x4 -> x8, waiting for transfers between devices: 50.2 us -> 42.8 us  [the longest x2 30.2 us: ring_reduce_scatter(): got_a = lax.ppermute(far[:half].astype(wire), axis, fwd).astype(jnp.float32)]
    ppermute x4 -> x8, starting transfers between devices: 6.53 us -> 12 us  [the longest x2 6.19 us: ring_reduce_scatter(): got_b = lax.ppermute(far[half:].astype(wire), axis, bwd).astype(jnp.float32)]
    convert_element_type x1 -> x2, other arithmetic: 0.56 us -> 4.64 us  [the longest x1 4.62 us: body(): ring_reduce_scatter(row_blocks, 'dp', jnp.bfloat16).astype(jnp.bfloat16)]
    dot_general x2 -> x8, matrix products: 8.23 us -> 6.75 us  [the longest x4 4.23 us: body(): lax.dot_general(grad_up_pre[rows], up_w, contract_last, preferred_element...]
  transfers between devices with their start and end apart: 15 -> 19, of which waited for: 8 -> 9; matrix products, arithmetic and copies ran while one was open for 11% -> 13% of each run, Pallas kernels for 0% -> 0%
where the time goes in v5:
time: 324 us; the launch traced here: 323 us
  waiting for transfers between devices  196 us (60%)
  starting transfers between devices  54.8 us (17%)
  matrix products  34.8 us (11%)
  local copies, waits for them, and re-layouts  26 us (8%)
  other arithmetic  10.5 us (3%)
    all_to_all x1, waiting for transfers between devices, body(): lax.all_to_all(sent_in, 'expert', 0, 0, tiled=True)  34.6 us
    all_to_all x1, waiting for transfers between devices, body(): lax.all_to_all(sent_dy, 'expert', 0, 0, tiled=True)  33.3 us
    all_to_all x1, waiting for transfers between devices, body(): lax.all_to_all(jnp.concatenate([own_rows, score_tile], axis=1), 'expert',...  31.9 us
    ppermute x2, waiting for transfers between devices, ring_reduce_scatter(): got_a = lax.ppermute(far[:half].astype(wire), axis, fwd).astype(jnp.float32)  30.2 us
    ppermute x2, waiting for transfers between devices, ring_gather(): from_prev = lax.ppermute(x, axis, fwd)  27.8 us
    ppermute x2, waiting for transfers between devices, ring_gather(): far_a = lax.ppermute(from_prev[:half], axis, fwd)  25.8 us
    all_to_all x1, starting transfers between devices, body(): lax.all_to_all(sent_dy, 'expert', 0, 0, tiled=True)  12.1 us
    ppermute x2, waiting for transfers between devices, ring_reduce_scatter(): got_b = lax.ppermute(far[half:].astype(wire), axis, bwd).astype(jnp.float32)  12.1 us
  transfers between devices with their start and end apart: 19, of which 9 were waited for; matrix products, arithmetic and copies ran while one was open for 13% of the time, Pallas kernels for 0%

profile of v5, /device:TPU:8, one launch (start us, length us, event | category | flops | bytes accessed | tf_op | source)
XLA Modules:
  0.0 323.5 jit_solution(1930666028340173992)
XLA Ops:
  7.1 12.1 %all-to-all-start = ((bf16[64,96,128]{2,1,0:T(8,128)(2,1)}), bf16[64,96,128]{2,1,0:T(8,128)(2,1)S(1)}, u32[]{:S(2)}, u32[]{:S(2)}) async-start(bf16[64,96,128]{2,1,0:T(8,128)(2,1)} %reshape.97), calls=%async_computation | async-start | bytes 3145728 | tf_op jit(solution)/shard_map/all_to_all | solution.py:72
  19.2 2.9 convolution_convert_fusion.3
  22.1 3.7 %reshape.99 = bf16[64,96,128]{2,1,0:T(8,128)(2,1)} reshape(bf16[192,4096]{1,0:T(8,128)(2,1)} %convolution_convert_fusion.3) | data formatting | bytes 3145728 | tf_op jit(solution)/shard_map/reshape | solution.py:61
  25.9 33.3 %all-to-all-done = bf16[64,96,128]{2,1,0:T(8,128)(2,1)S(1)} async-done(((bf16[64,96,128]{2,1,0:T(8,128)(2,1)}), bf16[64,96,128]{2,1,0:T(8,128)(2,1)S(1)}, u32[]{:S(2)}, u32[]{:S(2)}) %all-to-all-start) | async-done | bytes 1572896 | tf_op jit(solution)/shard_map/all_to_all | solution.py:72
  59.2 5.6 %all-to-all-start.1 = ((bf16[64,96,128]{2,1,0:T(8,128)(2,1)}), bf16[64,96,128]{2,1,0:T(8,128)(2,1)}, u32[]{:S(2)}, u32[]{:S(2)}) async-start(bf16[64,96,128]{2,1,0:T(8,128)(2,1)} %reshape.99), calls=%async_computation.1 | async-start | bytes 3145728 | tf_op jit(solution)/shard_map/all_to_all | solution.py:71
  70.1 34.6 %all-to-all-done.1 = bf16[64,96,128]{2,1,0:T(8,128)(2,1)} async-done(((bf16[64,96,128]{2,1,0:T(8,128)(2,1)}), bf16[64,96,128]{2,1,0:T(8,128)(2,1)}, u32[]{:S(2)}, u32[]{:S(2)}) %all-to-all-start.1) | async-done | bytes 1572896 | tf_op jit(solution)/shard_map/all_to_all | solution.py:71
  104.7 2.5 reshape.100
  115.0 3.0 collective-permute-start.3
  118.0 27.8 %collective-permute-done.5 = bf16[192,4096]{1,0:T(8,128)(2,1)S(1)} collective-permute-done((bf16[192,4096]{1,0:T(8,128)(2,1)S(1)}, bf16[192,4096]{1,0:T(8,128)(2,1)S(1)}, u32[]{:S(2)}, u32[]{:S(2)}) %collective-permute-start.5) | collective-permute-done | bytes 1572896 | tf_op jit(solution)/shard_map/ppermute | solution.py:18
  146.3 3.2 collective-permute-start.7
  151.2 25.8 %collective-permute-done.6 = bf16[96,4096]{1,0:T(8,128)(2,1)S(1)} collective-permute-done((bf16[96,4096]{1,0:T(8,128)(2,1)S(1)}, bf16[96,4096]{1,0:T(8,128)(2,1)S(1)}, u32[]{:S(2)}, u32[]{:S(2)}) %collective-permute-start.6) | collective-permute-done | bytes 786464 | tf_op jit(solution)/shard_map/ppermute | solution.py:20
  184.1 3.1 multiply_reduce_fusion
  189.3 3.0 collective-permute-start.10
  194.6 12.1 %collective-permute-done.10 = bf16[96,4096]{1,0:T(8,128)(2,1)S(1)} collective-permute-done((bf16[96,4096]{1,0:T(8,128)(2,1)S(1)}, bf16[96,4096]{1,0:T(8,128)(2,1)S(1)}, u32[]{:S(2)}, u32[]{:S(2)}) %collective-permute-start.10) | collective-permute-done | bytes 786464 | tf_op jit(solution)/shard_map/ppermute | solution.py:32
  207.0 3.6 %collective-permute-start.11 = (bf16[192,4096]{1,0:T(8,128)(2,1)S(1)}, bf16[192,4096]{1,0:T(8,128)(2,1)}, u32[]{:S(2)}, u32[]{:S(2)}) collective-permute-start(bf16[192,4096]{1,0:T(8,128)(2,1)S(1)} %pad_maximum_fusion.1), channel_id=1, source_target_pairs={{0,192},{64,0},{128,64},{192,128},{1,193},{65,1},{129,65},{193,129... | collective-permute-start | bytes 4718600 | tf_op jit(solution)/shard_map/ppermute | solution.py:36
  212.3 3.2 collective-permute-start.14
  216.1 30.1 %collective-permute-done.12 = f32[96,1]{0,1:T(1,128)S(1)} collective-permute-done((f32[96,1]{0,1:T(1,128)S(1)}, f32[96,1]{0,1:T(1,128)S(1)}, u32[]{:S(2)}, u32[]{:S(2)}) %collective-permute-start.12) | collective-permute-done | bytes 416 | tf_op jit(solution)/shard_map/ppermute | solution.py:31
  251.5 4.6 %add_convert_fusion = bf16[192,4096]{1,0:T(8,128)(2,1)} fusion(bf16[192,4096]{1,0:T(8,128)(2,1)} %collective-permute-done.11, f32[192,4096]{1,0:T(8,128)} %convolution_add_fusion.3, bf16[192,4096]{1,0:T(8,128)(2,1)} %collective-permute-done.9), kind=kLoop, calls=%fused_computation.16 | loop fusion | flops 3932160 | bytes 7864320 | tf_op jit(solution)/shard_map/convert_element_type | solution.py:107
  256.1 2.6 reshape.101
  260.1 11.6 %all-to-all-start.2 = ((bf16[64,112,128]{2,1,0:T(8,128)(2,1)}), bf16[64,112,128]{2,1,0:T(8,128)(2,1)S(1)}, u32[]{:S(2)}, u32[]{:S(2)}) async-start(bf16[64,112,128]{2,1,0:T(8,128)(2,1)} %fusion.5), calls=%async_computation.2 | async-start | bytes 3670016 | tf_op jit(solution)/shard_map/all_to_all | solution.py:122
  271.7 5.6 %fusion.2 = bf16[1,4096,192]{1,2,0:T(8,128)(2,1)} fusion(bf16[768,192]{0,1:T(8,128)(2,1)} %copy-done.4, bf16[768,4096]{1,0:T(8,128)(2,1)} %copy-done.5), kind=kOutput, calls=%fused_computation.12 | convolution fusion | flops 1208745984 | bytes 8159232 | tf_op jit(solution)/shard_map/dot_general | solution.py:113
  277.3 5.5 %fusion.3 = bf16[1,4096,192]{1,2,0:T(8,128)(2,1)} fusion(bf16[768,192]{0,1:T(8,128)(2,1)S(1)} %copy-done.3, bf16[768,4096]{1,0:T(8,128)(2,1)} %copy-done.5), kind=kOutput, calls=%fused_computation.13 | convolution fusion | flops 1208745984 | bytes 8159232 | tf_op jit(solution)/shard_map/dot_general | solution.py:116
  285.3 31.9 %all-to-all-done.2 = bf16[64,112,128]{2,1,0:T(8,128)(2,1)S(1)} async-done(((bf16[64,112,128]{2,1,0:T(8,128)(2,1)}), bf16[64,112,128]{2,1,0:T(8,128)(2,1)S(1)}, u32[]{:S(2)}, u32[]{:S(2)}) %all-to-all-start.2) | async-done | bytes 1835040 | tf_op jit(solution)/shard_map/all_to_all | solution.py:122
  319.5 2.5 reshape.103
  (100 shorter events, 48.2 us)
Async XLA Ops:
  0.6 176.6 %copy-start = (bf16[1,4096,192]{1,2,0:T(8,128)(2,1)S(1)}, bf16[1,4096,192]{1,2,0:T(8,128)(2,1)}, u32[]{:S(2)}) copy-start(bf16[1,4096,192]{1,2,0:T(8,128)(2,1)} %param.11) | copy-start | bytes 4718596
  7.1 52.1 %all-to-all-start = ((bf16[64,96,128]{2,1,0:T(8,128)(2,1)}), bf16[64,96,128]{2,1,0:T(8,128)(2,1)S(1)}, u32[]{:S(2)}, u32[]{:S(2)}) async-start(bf16[64,96,128]{2,1,0:T(8,128)(2,1)} %reshape.97), calls=%async_computation | async-start | bytes 3145728 | tf_op jit(solution)/shard_map/all_to_all | solution.py:72
  59.2 45.5 %all-to-all-start.1 = ((bf16[64,96,128]{2,1,0:T(8,128)(2,1)}), bf16[64,96,128]{2,1,0:T(8,128)(2,1)}, u32[]{:S(2)}, u32[]{:S(2)}) async-start(bf16[64,96,128]{2,1,0:T(8,128)(2,1)} %reshape.99), calls=%async_computation.1 | async-start | bytes 3145728 | tf_op jit(solution)/shard_map/all_to_all | solution.py:71
  66.8 45.4 %collective-permute-start.1 = (bf16[192,4096]{1,0:T(8,128)(2,1)}, bf16[192,4096]{1,0:T(8,128)(2,1)}, u32[]{:S(2)}, u32[]{:S(2)}) collective-permute-start(bf16[192,4096]{1,0:T(8,128)(2,1)} %reshape.98), channel_id=1, source_target_pairs={{0,64},{64,128},{128,192},{192,0},{1,65},{65,129},{129,193},{193,1... | collective-permute-start | bytes 4718600 | tf_op jit(solution)/shard_map/ppermute | solution.py:18
  68.3 45.5 %collective-permute-start = (bf16[192,4096]{1,0:T(8,128)(2,1)}, bf16[192,4096]{1,0:T(8,128)(2,1)}, u32[]{:S(2)}, u32[]{:S(2)}) collective-permute-start(bf16[192,4096]{1,0:T(8,128)(2,1)} %reshape.98), channel_id=1, source_target_pairs={{0,192},{64,0},{128,64},{192,128},{1,193},{65,1},{129,65},{193,129... | collective-permute-start | bytes 4718600 | tf_op jit(solution)/shard_map/ppermute | solution.py:19
  107.3 38.6 %collective-permute-start.5 = (bf16[192,4096]{1,0:T(8,128)(2,1)S(1)}, bf16[192,4096]{1,0:T(8,128)(2,1)S(1)}, u32[]{:S(2)}, u32[]{:S(2)}) collective-permute-start(bf16[192,4096]{1,0:T(8,128)(2,1)S(1)} %reshape.100), channel_id=1, source_target_pairs={{0,64},{64,128},{128,192},{192,0},{1,65},{65,129},{129,193},{193,1... | collective-permute-start | bytes 4718600 | tf_op jit(solution)/shard_map/ppermute | solution.py:18
  108.9 37.4 %collective-permute-start.4 = (bf16[192,4096]{1,0:T(8,128)(2,1)S(1)}, bf16[192,4096]{1,0:T(8,128)(2,1)S(1)}, u32[]{:S(2)}, u32[]{:S(2)}) collective-permute-start(bf16[192,4096]{1,0:T(8,128)(2,1)S(1)} %reshape.100), channel_id=1, source_target_pairs={{0,192},{64,0},{128,64},{192,128},{1,193},{65,1},{129,65},{193,129... | collective-permute-start | bytes 4718600 | tf_op jit(solution)/shard_map/ppermute | solution.py:19
  113.5 66.1 %collective-permute-start.2 = (bf16[96,4096]{1,0:T(8,128)(2,1)S(1)}, bf16[96,4096]{1,0:T(8,128)(2,1)S(1)}, u32[]{:S(2)}, u32[]{:S(2)}) collective-permute-start(bf16[96,4096]{1,0:T(8,128)(2,1)S(1)} %slice.145), channel_id=1, source_target_pairs={{0,64},{64,128},{128,192},{192,0},{1,65},{65,129},{129,193},{193,1... | collective-permute-start | bytes 2359304 | tf_op jit(solution)/shard_map/ppermute | solution.py:20
  115.0 67.1 %collective-permute-start.3 = (bf16[96,4096]{1,0:T(8,128)(2,1)S(1)}, bf16[96,4096]{1,0:T(8,128)(2,1)S(1)}, u32[]{:S(2)}, u32[]{:S(2)}) collective-permute-start(bf16[96,4096]{1,0:T(8,128)(2,1)S(1)} %slice.146), channel_id=1, source_target_pairs={{0,192},{64,0},{128,64},{192,128},{1,193},{65,1},{129,65},{193,129... | collective-permute-start | bytes 2359304 | tf_op jit(solution)/shard_map/ppermute | solution.py:21
  145.9 31.1 %collective-permute-start.6 = (bf16[96,4096]{1,0:T(8,128)(2,1)S(1)}, bf16[96,4096]{1,0:T(8,128)(2,1)S(1)}, u32[]{:S(2)}, u32[]{:S(2)}) collective-permute-start(bf16[96,4096]{1,0:T(8,128)(2,1)S(1)} %slice.147), channel_id=1, source_target_pairs={{0,64},{64,128},{128,192},{192,0},{1,65},{65,129},{129,193},{193,1... | collective-permute-start | bytes 2359304 | tf_op jit(solution)/shard_map/ppermute | solution.py:20
  146.3 30.7 %collective-permute-start.7 = (bf16[96,4096]{1,0:T(8,128)(2,1)S(1)}, bf16[96,4096]{1,0:T(8,128)(2,1)S(1)}, u32[]{:S(2)}, u32[]{:S(2)}) collective-permute-start(bf16[96,4096]{1,0:T(8,128)(2,1)S(1)} %slice.148), channel_id=1, source_target_pairs={{0,192},{64,0},{128,64},{192,128},{1,193},{65,1},{129,65},{193,129... | collective-permute-start | bytes 2359304 | tf_op jit(solution)/shard_map/ppermute | solution.py:21
  187.3 28.3 %copy-start.4 = (bf16[768,192]{0,1:T(8,128)(2,1)}, bf16[768,192]{0,1:T(8,128)(2,1)S(1)}, u32[]{:S(2)}) copy-start(bf16[768,192]{0,1:T(8,128)(2,1)S(1)} %get-tuple-element.7) | copy-start | bytes 884740
  187.3 61.2 %copy-start.2 = (bf16[768,192]{0,1:T(8,128)(2,1)}, bf16[768,192]{0,1:T(8,128)(2,1)S(1)}, u32[]{:S(2)}) copy-start(bf16[768,192]{0,1:T(8,128)(2,1)S(1)} %get-tuple-element.10) | copy-start | bytes 884740
  189.3 17.3 %collective-permute-start.10 = (bf16[96,4096]{1,0:T(8,128)(2,1)S(1)}, bf16[96,4096]{1,0:T(8,128)(2,1)S(1)}, u32[]{:S(2)}, u32[]{:S(2)}) collective-permute-start(bf16[96,4096]{1,0:T(8,128)(2,1)S(1)} %get-tuple-element.9), channel_id=1, source_target_pairs={{0,192},{64,0},{128,64},{192,128},{1,193},{65,1},{129,65},{193,129... | collective-permute-start | bytes 2359304 | tf_op jit(solution)/shard_map/ppermute | solution.py:32
  193.0 17.7 %collective-permute-start.8 = (bf16[96,4096]{1,0:T(8,128)(2,1)S(1)}, bf16[96,4096]{1,0:T(8,128)(2,1)S(1)}, u32[]{:S(2)}, u32[]{:S(2)}) collective-permute-start(bf16[96,4096]{1,0:T(8,128)(2,1)S(1)} %get-tuple-element.8), channel_id=1, source_target_pairs={{0,64},{64,128},{128,192},{192,0},{1,65},{65,129},{129,193},{193,1... | collective-permute-start | bytes 2359304 | tf_op jit(solution)/shard_map/ppermute | solution.py:31
  207.0 44.4 %collective-permute-start.11 = (bf16[192,4096]{1,0:T(8,128)(2,1)S(1)}, bf16[192,4096]{1,0:T(8,128)(2,1)}, u32[]{:S(2)}, u32[]{:S(2)}) collective-permute-start(bf16[192,4096]{1,0:T(8,128)(2,1)S(1)} %pad_maximum_fusion.1), channel_id=1, source_target_pairs={{0,192},{64,0},{128,64},{192,128},{1,193},{65,1},{129,65},{193,129... | collective-permute-start | bytes 4718600 | tf_op jit(solution)/shard_map/ppermute | solution.py:36
  212.2 39.3 %collective-permute-start.9 = (bf16[192,4096]{1,0:T(8,128)(2,1)}, bf16[192,4096]{1,0:T(8,128)(2,1)}, u32[]{:S(2)}, u32[]{:S(2)}) collective-permute-start(bf16[192,4096]{1,0:T(8,128)(2,1)} %pad_maximum_fusion), channel_id=1, source_target_pairs={{0,64},{64,128},{128,192},{192,0},{1,65},{65,129},{129,193},{193,1... | collective-permute-start | bytes 4718600 | tf_op jit(solution)/shard_map/ppermute | solution.py:35
  212.3 33.9 %collective-permute-start.12 = (f32[96,1]{0,1:T(1,128)S(1)}, f32[96,1]{0,1:T(1,128)S(1)}, u32[]{:S(2)}, u32[]{:S(2)}) collective-permute-start(f32[96,1]{0,1:T(1,128)S(1)} %get-tuple-element.13), channel_id=1, source_target_pairs={{0,64},{64,128},{128,192},{192,0},{1,65},{65,129},{129,193},{193,1... | collective-permute-start | bytes 1160 | tf_op jit(solution)/shard_map/ppermute | solution.py:31
  212.3 33.9 %collective-permute-start.14 = (f32[96,1]{0,1:T(1,128)S(1)}, f32[96,1]{0,1:T(1,128)S(1)}, u32[]{:S(2)}, u32[]{:S(2)}) collective-permute-start(f32[96,1]{0,1:T(1,128)S(1)} %get-tuple-element.14), channel_id=1, source_target_pairs={{0,192},{64,0},{128,64},{192,128},{1,193},{65,1},{129,65},{193,129... | collective-permute-start | bytes 1160 | tf_op jit(solution)/shard_map/ppermute | solution.py:32
  246.4 4.4 %collective-permute-start.15 = (f32[192,1]{0,1:T(1,128)S(1)}, f32[192,1]{0,1:T(1,128)S(1)}, u32[]{:S(2)}, u32[]{:S(2)}) collective-permute-start(f32[192,1]{0,1:T(1,128)S(1)} %pad_maximum_fusion.3), channel_id=1, source_target_pairs={{0,192},{64,0},{128,64},{192,128},{1,193},{65,1},{129,65},{193,129... | collective-permute-start | bytes 2312 | tf_op jit(solution)/shard_map/ppermute | solution.py:36
  246.5 4.8 %collective-permute-start.13 = (f32[192,1]{0,1:T(1,128)S(1)}, f32[192,1]{0,1:T(1,128)S(1)}, u32[]{:S(2)}, u32[]{:S(2)}) collective-permute-start(f32[192,1]{0,1:T(1,128)S(1)} %pad_maximum_fusion.2), channel_id=1, source_target_pairs={{0,64},{64,128},{128,192},{192,0},{1,65},{65,129},{129,193},{193,1... | collective-permute-start | bytes 2312 | tf_op jit(solution)/shard_map/ppermute | solution.py:35
  260.1 57.2 %all-to-all-start.2 = ((bf16[64,112,128]{2,1,0:T(8,128)(2,1)}), bf16[64,112,128]{2,1,0:T(8,128)(2,1)S(1)}, u32[]{:S(2)}, u32[]{:S(2)}) async-start(bf16[64,112,128]{2,1,0:T(8,128)(2,1)} %fusion.5), calls=%async_computation.2 | async-start | bytes 3670016 | tf_op jit(solution)/shard_map/all_to_all | solution.py:122
  271.7 11.1 %slice-start = ((s8[6291456]{0:T(1024)(128)(4,1)}), s8[4194304]{0:T(1024)(128)(4,1)S(1)}, s32[]{:S(2)}) async-start(s8[6291456]{0:T(1024)(128)(4,1)} %bitcast.73), calls=%async_computation.3 | async-start | bytes 8388608
  282.8 34.7 %copy-start.7 = (bf16[128,1]{0,1:T(2,128)(2,1)S(1)}, bf16[128,1]{0,1:T(2,128)(2,1)}, u32[]{:S(2)}) copy-start(bf16[128,1]{0,1:T(2,128)(2,1)} %param.10) | copy-start | bytes 772
  (7 other events, 27.0 us)

commit v6 on v5

--- a/solution.py
+++ b/solution.py
@@ -71,6 +71,7 @@
     recv_in = lax.all_to_all(sent_in, "expert", 0, 0, tiled=True).reshape(slot_total, width)
     recv_dy = lax.all_to_all(sent_dy, "expert", 0, 0, tiled=True).reshape(slot_total, width)
     rows_in = ring_gather(recv_in, "dp")
+    recv_dy, rows_in = lax.optimization_barrier((recv_dy, rows_in))
     rows_dy = ring_gather(recv_dy, "dp")
     gate_w = w_gate[0]
     up_w = w_up[0]

time: 324 us -> 327 us (level)
  waiting for transfers between devices: 196 us -> 190 us
  starting transfers between devices: 54.8 us -> 60.5 us
    ppermute x2, waiting for transfers between devices: 12.1 us -> 0.33 us  [ring_reduce_scatter(): got_b = lax.ppermute(far[half:].astype(wire), axis, bwd).astype(jnp.float32)]
    all_to_all x1, starting transfers between devices: 5.6 us -> 12.2 us  [body(): lax.all_to_all(sent_in, 'expert', 0, 0, tiled=True)]
    all_to_all x1, starting transfers between devices: 12.1 us -> 5.6 us  [body(): lax.all_to_all(sent_dy, 'expert', 0, 0, tiled=True)]
    ppermute x2, waiting for transfers between devices: 30.2 us -> 35.4 us  [ring_reduce_scatter(): got_a = lax.ppermute(far[:half].astype(wire), axis, fwd).astype(jnp.float32)]
    all_to_all x1, starting transfers between devices: 11.6 us -> 15.5 us  [body(): lax.all_to_all(jnp.concatenate([own_rows, score_tile], axis=1), 'expert',...]
  transfers between devices with their start and end apart: 19 -> 19, of which waited for: 9 -> 10; matrix products, arithmetic and copies ran while one was open for 13% -> 13% of each run, Pallas kernels for 0% -> 0%
where the time goes in v6:
time: 327 us; the launch traced here: 326 us
  waiting for transfers between devices  190 us (58%)
  starting transfers between devices  60.5 us (19%)
  matrix products  36.2 us (11%)
  local copies, waits for them, and re-layouts  27.7 us (8%)
  other arithmetic  10.5 us (3%)
    ppermute x2, waiting for transfers between devices, ring_reduce_scatter(): got_a = lax.ppermute(far[:half].astype(wire), axis, fwd).astype(jnp.float32)  35.4 us
    all_to_all x1, waiting for transfers between devices, body(): lax.all_to_all(sent_dy, 'expert', 0, 0, tiled=True)  34.6 us
    all_to_all x1, waiting for transfers between devices, body(): lax.all_to_all(sent_in, 'expert', 0, 0, tiled=True)  33.3 us
    all_to_all x1, waiting for transfers between devices, body(): lax.all_to_all(jnp.concatenate([own_rows, score_tile], axis=1), 'expert',...  31.9 us
    ppermute x2, waiting for transfers between devices, ring_gather(): from_prev = lax.ppermute(x, axis, fwd)  27.1 us
    ppermute x2, waiting for transfers between devices, ring_gather(): far_a = lax.ppermute(from_prev[:half], axis, fwd)  25 us
    all_to_all x1, starting transfers between devices, body(): lax.all_to_all(jnp.concatenate([own_rows, score_tile], axis=1), 'expert',...  15.5 us
    all_to_all x1, starting transfers between devices, body(): lax.all_to_all(sent_in, 'expert', 0, 0, tiled=True)  12.2 us
  transfers between devices with their start and end apart: 19, of which 10 were waited for; matrix products, arithmetic and copies ran while one was open for 13% of the time, Pallas kernels for 0%

profile of v6, /device:TPU:8, one launch (start us, length us, event | category | flops | bytes accessed | tf_op | source)
XLA Modules:
  0.0 326.4 jit_solution(3105665278614873025)
XLA Ops:
  7.1 12.2 %all-to-all-start.1 = ((bf16[64,96,128]{2,1,0:T(8,128)(2,1)}), bf16[64,96,128]{2,1,0:T(8,128)(2,1)S(1)}, u32[]{:S(2)}, u32[]{:S(2)}) async-start(bf16[64,96,128]{2,1,0:T(8,128)(2,1)} %reshape.99), calls=%async_computation.1 | async-start | bytes 3145728 | tf_op jit(solution)/shard_map/all_to_all | solution.py:71
  19.3 2.9 convolution_convert_fusion.4
  22.2 3.7 %reshape.97 = bf16[64,96,128]{2,1,0:T(8,128)(2,1)} reshape(bf16[192,4096]{1,0:T(8,128)(2,1)} %convolution_convert_fusion.4) | data formatting | bytes 3145728 | tf_op jit(solution)/shard_map/reshape | solution.py:69
  26.0 33.3 %all-to-all-done.1 = bf16[64,96,128]{2,1,0:T(8,128)(2,1)S(1)} async-done(((bf16[64,96,128]{2,1,0:T(8,128)(2,1)}), bf16[64,96,128]{2,1,0:T(8,128)(2,1)S(1)}, u32[]{:S(2)}, u32[]{:S(2)}) %all-to-all-start.1) | async-done | bytes 1572896 | tf_op jit(solution)/shard_map/all_to_all | solution.py:71
  59.3 5.6 %all-to-all-start = ((bf16[64,96,128]{2,1,0:T(8,128)(2,1)}), bf16[64,96,128]{2,1,0:T(8,128)(2,1)}, u32[]{:S(2)}, u32[]{:S(2)}) async-start(bf16[64,96,128]{2,1,0:T(8,128)(2,1)} %reshape.97), calls=%async_computation | async-start | bytes 3145728 | tf_op jit(solution)/shard_map/all_to_all | solution.py:72
  70.2 34.6 %all-to-all-done = bf16[64,96,128]{2,1,0:T(8,128)(2,1)} async-done(((bf16[64,96,128]{2,1,0:T(8,128)(2,1)}), bf16[64,96,128]{2,1,0:T(8,128)(2,1)}, u32[]{:S(2)}, u32[]{:S(2)}) %all-to-all-start) | async-done | bytes 1572896 | tf_op jit(solution)/shard_map/all_to_all | solution.py:72
  116.2 11.5 %collective-permute-done.2 = bf16[96,4096]{1,0:T(8,128)(2,1)S(1)} collective-permute-done((bf16[96,4096]{1,0:T(8,128)(2,1)S(1)}, bf16[96,4096]{1,0:T(8,128)(2,1)S(1)}, u32[]{:S(2)}, u32[]{:S(2)}) %collective-permute-start.2) | collective-permute-done | bytes 786464 | tf_op jit(solution)/shard_map/ppermute | solution.py:20
  127.8 2.7 collective-permute-done.3
  139.9 27.1 %collective-permute-done.5 = bf16[192,4096]{1,0:T(8,128)(2,1)S(1)} collective-permute-done((bf16[192,4096]{1,0:T(8,128)(2,1)S(1)}, bf16[192,4096]{1,0:T(8,128)(2,1)S(1)}, u32[]{:S(2)}, u32[]{:S(2)}) %collective-permute-start.5) | collective-permute-done | bytes 1572896 | tf_op jit(solution)/shard_map/ppermute | solution.py:18
  170.9 13.4 %collective-permute-done.6 = bf16[96,4096]{1,0:T(8,128)(2,1)S(1)} collective-permute-done((bf16[96,4096]{1,0:T(8,128)(2,1)S(1)}, bf16[96,4096]{1,0:T(8,128)(2,1)S(1)}, u32[]{:S(2)}, u32[]{:S(2)}) %collective-permute-start.6) | collective-permute-done | bytes 786464 | tf_op jit(solution)/shard_map/ppermute | solution.py:20
  185.8 3.1 multiply_reduce_fusion
  192.6 2.8 collective-permute-start.10
  196.8 11.6 %collective-permute-done.8 = bf16[96,4096]{1,0:T(8,128)(2,1)S(1)} collective-permute-done((bf16[96,4096]{1,0:T(8,128)(2,1)S(1)}, bf16[96,4096]{1,0:T(8,128)(2,1)S(1)}, u32[]{:S(2)}, u32[]{:S(2)}) %collective-permute-start.8) | collective-permute-done | bytes 786464 | tf_op jit(solution)/shard_map/ppermute | solution.py:31
  210.2 3.2 collective-permute-start.11
  213.5 3.2 collective-permute-start.14
  217.3 23.8 %collective-permute-done.12 = f32[96,1]{0,1:T(1,128)S(1)} collective-permute-done((f32[96,1]{0,1:T(1,128)S(1)}, f32[96,1]{0,1:T(1,128)S(1)}, u32[]{:S(2)}, u32[]{:S(2)}) %collective-permute-start.12) | collective-permute-done | bytes 416 | tf_op jit(solution)/shard_map/ppermute | solution.py:31
  247.9 4.6 %add_convert_fusion = bf16[192,4096]{1,0:T(8,128)(2,1)} fusion(bf16[192,4096]{1,0:T(8,128)(2,1)} %collective-permute-done.11, f32[192,4096]{1,0:T(8,128)} %convolution_add_fusion.3, bf16[192,4096]{1,0:T(8,128)(2,1)} %collective-permute-done.9), kind=kLoop, calls=%fused_computation.16 | loop fusion | flops 3932160 | bytes 7864320 | tf_op jit(solution)/shard_map/convert_element_type | solution.py:108
  252.6 2.6 reshape.101
  256.5 15.5 %all-to-all-start.2 = ((bf16[64,112,128]{2,1,0:T(8,128)(2,1)}), bf16[64,112,128]{2,1,0:T(8,128)(2,1)S(1)}, u32[]{:S(2)}, u32[]{:S(2)}) async-start(bf16[64,112,128]{2,1,0:T(8,128)(2,1)} %fusion.5), calls=%async_computation.2 | async-start | bytes 3670016 | tf_op jit(solution)/shard_map/all_to_all | solution.py:123
  272.1 5.6 %fusion.3 = bf16[1,4096,192]{1,2,0:T(8,128)(2,1)} fusion(bf16[768,192]{0,1:T(8,128)(2,1)} %copy-done.2, bf16[768,4096]{1,0:T(8,128)(2,1)} %copy-done.5), kind=kOutput, calls=%fused_computation.13 | convolution fusion | flops 1208745984 | bytes 8159232 | tf_op jit(solution)/shard_map/dot_general | solution.py:117
  277.6 5.5 %fusion.2 = bf16[1,4096,192]{1,2,0:T(8,128)(2,1)} fusion(bf16[768,192]{0,1:T(8,128)(2,1)S(1)} %copy-done.4, bf16[768,4096]{1,0:T(8,128)(2,1)} %copy-done.5), kind=kOutput, calls=%fused_computation.12 | convolution fusion | flops 1208745984 | bytes 8159232 | tf_op jit(solution)/shard_map/dot_general | solution.py:114
  285.7 31.9 %all-to-all-done.2 = bf16[64,112,128]{2,1,0:T(8,128)(2,1)S(1)} async-done(((bf16[64,112,128]{2,1,0:T(8,128)(2,1)}), bf16[64,112,128]{2,1,0:T(8,128)(2,1)S(1)}, u32[]{:S(2)}, u32[]{:S(2)}) %all-to-all-start.2) | async-done | bytes 1835040 | tf_op jit(solution)/shard_map/all_to_all | solution.py:123
  318.9 3.7 %reshape.103 = bf16[192,4096]{1,0:T(8,128)(2,1)} reshape(bf16[64,96,128]{2,1,0:T(8,128)(2,1)} %slice.163) | data formatting | bytes 3145728 | tf_op jit(solution)/shard_map/reshape | solution.py:126
  322.6 2.9 convolution_convert_fusion.5
  (100 shorter events, 58.1 us)
Async XLA Ops:
  0.6 134.8 %copy-start = (bf16[1,4096,192]{1,2,0:T(8,128)(2,1)S(1)}, bf16[1,4096,192]{1,2,0:T(8,128)(2,1)}, u32[]{:S(2)}) copy-start(bf16[1,4096,192]{1,2,0:T(8,128)(2,1)} %param.11) | copy-start | bytes 4718596
  7.1 12.2 %copy-start.7 = (bf16[128,1]{0,1:T(2,128)(2,1)S(1)}, bf16[128,1]{0,1:T(2,128)(2,1)}, u32[]{:S(2)}) copy-start(bf16[128,1]{0,1:T(2,128)(2,1)} %param.10) | copy-start | bytes 772
  7.1 52.2 %all-to-all-start.1 = ((bf16[64,96,128]{2,1,0:T(8,128)(2,1)}), bf16[64,96,128]{2,1,0:T(8,128)(2,1)S(1)}, u32[]{:S(2)}, u32[]{:S(2)}) async-start(bf16[64,96,128]{2,1,0:T(8,128)(2,1)} %reshape.99), calls=%async_computation.1 | async-start | bytes 3145728 | tf_op jit(solution)/shard_map/all_to_all | solution.py:71
  59.3 45.5 %all-to-all-start = ((bf16[64,96,128]{2,1,0:T(8,128)(2,1)}), bf16[64,96,128]{2,1,0:T(8,128)(2,1)}, u32[]{:S(2)}, u32[]{:S(2)}) async-start(bf16[64,96,128]{2,1,0:T(8,128)(2,1)} %reshape.97), calls=%async_computation | async-start | bytes 3145728 | tf_op jit(solution)/shard_map/all_to_all | solution.py:72
  67.0 40.4 %collective-permute-start.1 = (bf16[192,4096]{1,0:T(8,128)(2,1)}, bf16[192,4096]{1,0:T(8,128)(2,1)}, u32[]{:S(2)}, u32[]{:S(2)}) collective-permute-start(bf16[192,4096]{1,0:T(8,128)(2,1)} %reshape.100), channel_id=1, source_target_pairs={{0,64},{64,128},{128,192},{192,0},{1,65},{65,129},{129,193},{193,1... | collective-permute-start | bytes 4718600 | tf_op jit(solution)/shard_map/ppermute | solution.py:18
  68.5 43.2 %collective-permute-start = (bf16[192,4096]{1,0:T(8,128)(2,1)}, bf16[192,4096]{1,0:T(8,128)(2,1)}, u32[]{:S(2)}, u32[]{:S(2)}) collective-permute-start(bf16[192,4096]{1,0:T(8,128)(2,1)} %reshape.100), channel_id=1, source_target_pairs={{0,192},{64,0},{128,64},{192,128},{1,193},{65,1},{129,65},{193,129... | collective-permute-start | bytes 4718600 | tf_op jit(solution)/shard_map/ppermute | solution.py:19
  108.6 19.2 %collective-permute-start.2 = (bf16[96,4096]{1,0:T(8,128)(2,1)S(1)}, bf16[96,4096]{1,0:T(8,128)(2,1)S(1)}, u32[]{:S(2)}, u32[]{:S(2)}) collective-permute-start(bf16[96,4096]{1,0:T(8,128)(2,1)S(1)} %slice.145), channel_id=1, source_target_pairs={{0,64},{64,128},{128,192},{192,0},{1,65},{65,129},{129,193},{193,1... | collective-permute-start | bytes 2359304 | tf_op jit(solution)/shard_map/ppermute | solution.py:20
  112.9 17.7 %collective-permute-start.3 = (bf16[96,4096]{1,0:T(8,128)(2,1)S(1)}, bf16[96,4096]{1,0:T(8,128)(2,1)S(1)}, u32[]{:S(2)}, u32[]{:S(2)}) collective-permute-start(bf16[96,4096]{1,0:T(8,128)(2,1)S(1)} %slice.146), channel_id=1, source_target_pairs={{0,192},{64,0},{128,64},{192,128},{1,193},{65,1},{129,65},{193,129... | collective-permute-start | bytes 2359304 | tf_op jit(solution)/shard_map/ppermute | solution.py:21
  132.2 34.9 %collective-permute-start.5 = (bf16[192,4096]{1,0:T(8,128)(2,1)S(1)}, bf16[192,4096]{1,0:T(8,128)(2,1)S(1)}, u32[]{:S(2)}, u32[]{:S(2)}) collective-permute-start(bf16[192,4096]{1,0:T(8,128)(2,1)S(1)} %reshape.98), channel_id=1, source_target_pairs={{0,64},{64,128},{128,192},{192,0},{1,65},{65,129},{129,193},{193,1... | collective-permute-start | bytes 4718600 | tf_op jit(solution)/shard_map/ppermute | solution.py:18
  133.7 34.7 %collective-permute-start.4 = (bf16[192,4096]{1,0:T(8,128)(2,1)S(1)}, bf16[192,4096]{1,0:T(8,128)(2,1)S(1)}, u32[]{:S(2)}, u32[]{:S(2)}) collective-permute-start(bf16[192,4096]{1,0:T(8,128)(2,1)S(1)} %reshape.98), channel_id=1, source_target_pairs={{0,192},{64,0},{128,64},{192,128},{1,193},{65,1},{129,65},{193,129... | collective-permute-start | bytes 4718600 | tf_op jit(solution)/shard_map/ppermute | solution.py:19
  167.1 17.2 %collective-permute-start.6 = (bf16[96,4096]{1,0:T(8,128)(2,1)S(1)}, bf16[96,4096]{1,0:T(8,128)(2,1)S(1)}, u32[]{:S(2)}, u32[]{:S(2)}) collective-permute-start(bf16[96,4096]{1,0:T(8,128)(2,1)S(1)} %slice.147), channel_id=1, source_target_pairs={{0,64},{64,128},{128,192},{192,0},{1,65},{65,129},{129,193},{193,1... | collective-permute-start | bytes 2359304 | tf_op jit(solution)/shard_map/ppermute | solution.py:20
  168.5 15.8 %collective-permute-start.7 = (bf16[96,4096]{1,0:T(8,128)(2,1)S(1)}, bf16[96,4096]{1,0:T(8,128)(2,1)S(1)}, u32[]{:S(2)}, u32[]{:S(2)}) collective-permute-start(bf16[96,4096]{1,0:T(8,128)(2,1)S(1)} %slice.148), channel_id=1, source_target_pairs={{0,192},{64,0},{128,64},{192,128},{1,193},{65,1},{129,65},{193,129... | collective-permute-start | bytes 2359304 | tf_op jit(solution)/shard_map/ppermute | solution.py:21
  189.0 27.8 %copy-start.3 = (bf16[768,192]{0,1:T(8,128)(2,1)}, bf16[768,192]{0,1:T(8,128)(2,1)S(1)}, u32[]{:S(2)}) copy-start(bf16[768,192]{0,1:T(8,128)(2,1)S(1)} %get-tuple-element.11) | copy-start | bytes 884740
  189.0 56.5 %copy-start.2 = (bf16[768,192]{0,1:T(8,128)(2,1)}, bf16[768,192]{0,1:T(8,128)(2,1)S(1)}, u32[]{:S(2)}) copy-start(bf16[768,192]{0,1:T(8,128)(2,1)S(1)} %get-tuple-element.14) | copy-start | bytes 884740
  191.0 17.4 %collective-permute-start.8 = (bf16[96,4096]{1,0:T(8,128)(2,1)S(1)}, bf16[96,4096]{1,0:T(8,128)(2,1)S(1)}, u32[]{:S(2)}, u32[]{:S(2)}) collective-permute-start(bf16[96,4096]{1,0:T(8,128)(2,1)S(1)} %get-tuple-element.12), channel_id=1, source_target_pairs={{0,64},{64,128},{128,192},{192,0},{1,65},{65,129},{129,193},{193,1... | collective-permute-start | bytes 2359304 | tf_op jit(solution)/shard_map/ppermute | solution.py:31
  192.6 16.2 %collective-permute-start.10 = (bf16[96,4096]{1,0:T(8,128)(2,1)S(1)}, bf16[96,4096]{1,0:T(8,128)(2,1)S(1)}, u32[]{:S(2)}, u32[]{:S(2)}) collective-permute-start(bf16[96,4096]{1,0:T(8,128)(2,1)S(1)} %get-tuple-element.13), channel_id=1, source_target_pairs={{0,192},{64,0},{128,64},{192,128},{1,193},{65,1},{129,65},{193,129... | collective-permute-start | bytes 2359304 | tf_op jit(solution)/shard_map/ppermute | solution.py:32
  208.7 39.2 %collective-permute-start.9 = (bf16[192,4096]{1,0:T(8,128)(2,1)S(1)}, bf16[192,4096]{1,0:T(8,128)(2,1)}, u32[]{:S(2)}, u32[]{:S(2)}) collective-permute-start(bf16[192,4096]{1,0:T(8,128)(2,1)S(1)} %pad_maximum_fusion), channel_id=1, source_target_pairs={{0,64},{64,128},{128,192},{192,0},{1,65},{65,129},{129,193},{193,1... | collective-permute-start | bytes 4718600 | tf_op jit(solution)/shard_map/ppermute | solution.py:35
  210.2 37.7 %collective-permute-start.11 = (bf16[192,4096]{1,0:T(8,128)(2,1)}, bf16[192,4096]{1,0:T(8,128)(2,1)}, u32[]{:S(2)}, u32[]{:S(2)}) collective-permute-start(bf16[192,4096]{1,0:T(8,128)(2,1)} %pad_maximum_fusion.1), channel_id=1, source_target_pairs={{0,192},{64,0},{128,64},{192,128},{1,193},{65,1},{129,65},{193,129... | collective-permute-start | bytes 4718600 | tf_op jit(solution)/shard_map/ppermute | solution.py:36
  213.5 27.6 %collective-permute-start.12 = (f32[96,1]{0,1:T(1,128)S(1)}, f32[96,1]{0,1:T(1,128)S(1)}, u32[]{:S(2)}, u32[]{:S(2)}) collective-permute-start(f32[96,1]{0,1:T(1,128)S(1)} %get-tuple-element.17), channel_id=1, source_target_pairs={{0,64},{64,128},{128,192},{192,0},{1,65},{65,129},{129,193},{193,1... | collective-permute-start | bytes 1160 | tf_op jit(solution)/shard_map/ppermute | solution.py:31
  213.5 28.0 %collective-permute-start.14 = (f32[96,1]{0,1:T(1,128)S(1)}, f32[96,1]{0,1:T(1,128)S(1)}, u32[]{:S(2)}, u32[]{:S(2)}) collective-permute-start(f32[96,1]{0,1:T(1,128)S(1)} %get-tuple-element.18), channel_id=1, source_target_pairs={{0,192},{64,0},{128,64},{192,128},{1,193},{65,1},{129,65},{193,129... | collective-permute-start | bytes 1160 | tf_op jit(solution)/shard_map/ppermute | solution.py:32
  241.6 6.1 %collective-permute-start.13 = (f32[192,1]{0,1:T(1,128)S(1)}, f32[192,1]{0,1:T(1,128)S(1)}, u32[]{:S(2)}, u32[]{:S(2)}) collective-permute-start(f32[192,1]{0,1:T(1,128)S(1)} %pad_maximum_fusion.2), channel_id=1, source_target_pairs={{0,64},{64,128},{128,192},{192,0},{1,65},{65,129},{129,193},{193,1... | collective-permute-start | bytes 2312 | tf_op jit(solution)/shard_map/ppermute | solution.py:35
  243.5 4.2 %collective-permute-start.15 = (f32[192,1]{0,1:T(1,128)S(1)}, f32[192,1]{0,1:T(1,128)S(1)}, u32[]{:S(2)}, u32[]{:S(2)}) collective-permute-start(f32[192,1]{0,1:T(1,128)S(1)} %pad_maximum_fusion.3), channel_id=1, source_target_pairs={{0,192},{64,0},{128,64},{192,128},{1,193},{65,1},{129,65},{193,129... | collective-permute-start | bytes 2312 | tf_op jit(solution)/shard_map/ppermute | solution.py:36
  256.5 61.1 %all-to-all-start.2 = ((bf16[64,112,128]{2,1,0:T(8,128)(2,1)}), bf16[64,112,128]{2,1,0:T(8,128)(2,1)S(1)}, u32[]{:S(2)}, u32[]{:S(2)}) async-start(bf16[64,112,128]{2,1,0:T(8,128)(2,1)} %fusion.5), calls=%async_computation.2 | async-start | bytes 3670016 | tf_op jit(solution)/shard_map/all_to_all | solution.py:123
  272.0 11.1 %slice-start = ((s8[6291456]{0:T(1024)(128)(4,1)}), s8[4194304]{0:T(1024)(128)(4,1)S(1)}, s32[]{:S(2)}) async-start(s8[6291456]{0:T(1024)(128)(4,1)} %bitcast.73), calls=%async_computation.3 | async-start | bytes 8388608
  (7 other events, 32.3 us)

commit v7 on v5

--- a/solution.py
+++ b/solution.py
@@ -106,7 +106,10 @@
         row_blocks.append(part)
     own_grad = ring_reduce_scatter(row_blocks, "dp", jnp.bfloat16).astype(jnp.bfloat16)
     score_blocks = [score_part[k * block:(k + 1) * block, None] for k in range(dp_count)]
-    own_score = ring_reduce_scatter(score_blocks, "dp", jnp.float32).astype(jnp.bfloat16)
+    own_score = score_blocks[0]
+    for k in range(1, dp_count):
+        own_score = own_score + lax.ppermute(score_blocks[k], "dp", ring_pairs(dp_count, k))
+    own_score = own_score.astype(jnp.bfloat16)
     grad_down = lax.dot_general(
         hidden, scaled, contract_first, preferred_element_type=jnp.float32
     ).astype(jnp.bfloat16)

time: 324 us -> 319 us (0.985)
  waiting for transfers between devices: 196 us -> 192 us
    ppermute x2 -> x1, waiting for transfers between devices: 30.2 us -> 0.13 us  [ring_reduce_scatter(): got_a = lax.ppermute(far[:half].astype(wire), axis, fwd).astype(jnp.float32)]
    ppermute x0 -> x3, waiting for transfers between devices: none -> 26.3 us  [body(): lax.ppermute(score_blocks[k], 'dp', ring_pairs(dp_count, k))]
    ppermute x0 -> x3, starting transfers between devices: none -> 4.79 us  [body(): lax.ppermute(score_blocks[k], 'dp', ring_pairs(dp_count, k))]
    ppermute x2 -> x1, waiting for transfers between devices: 12.1 us -> 12.1 us  [ring_reduce_scatter(): got_b = lax.ppermute(far[half:].astype(wire), axis, bwd).astype(jnp.float32)]
  transfers between devices with their start and end apart: 19 -> 18, of which waited for: 9 -> 9; matrix products, arithmetic and copies ran while one was open for 13% -> 13% of each run, Pallas kernels for 0% -> 0%
where the time goes in v7:
time: 319 us; the launch traced here: 318 us
  waiting for transfers between devices  192 us (60%)
  starting transfers between devices  54.3 us (17%)
  matrix products  34.8 us (11%)
  local copies, waits for them, and re-layouts  26 us (8%)
  other arithmetic  10.3 us (3%)
    all_to_all x1, waiting for transfers between devices, body(): lax.all_to_all(sent_in, 'expert', 0, 0, tiled=True)  34.6 us
    all_to_all x1, waiting for transfers between devices, body(): lax.all_to_all(sent_dy, 'expert', 0, 0, tiled=True)  33.3 us
    all_to_all x1, waiting for transfers between devices, body(): lax.all_to_all(jnp.concatenate([own_rows, score_tile], axis=1), 'expert',...  31.9 us
    ppermute x2, waiting for transfers between devices, ring_gather(): from_prev = lax.ppermute(x, axis, fwd)  27.8 us
    ppermute x3, waiting for transfers between devices, body(): lax.ppermute(score_blocks[k], 'dp', ring_pairs(dp_count, k))  26.3 us
    ppermute x2, waiting for transfers between devices, ring_gather(): far_a = lax.ppermute(from_prev[:half], axis, fwd)  25.8 us
    all_to_all x1, starting transfers between devices, body(): lax.all_to_all(sent_dy, 'expert', 0, 0, tiled=True)  12.1 us
    ppermute x1, waiting for transfers between devices, ring_reduce_scatter(): got_b = lax.ppermute(far[half:].astype(wire), axis, bwd).astype(jnp.float32)  12.1 us
  transfers between devices with their start and end apart: 18, of which 9 were waited for; matrix products, arithmetic and copies ran while one was open for 13% of the time, Pallas kernels for 0%

profile of v7, /device:TPU:8, one launch (start us, length us, event | category | flops | bytes accessed | tf_op | source)
XLA Modules:
  0.0 318.5 jit_solution(9613614538012844195)
XLA Ops:
  7.1 12.1 %all-to-all-start = ((bf16[64,96,128]{2,1,0:T(8,128)(2,1)}), bf16[64,96,128]{2,1,0:T(8,128)(2,1)S(1)}, u32[]{:S(2)}, u32[]{:S(2)}) async-start(bf16[64,96,128]{2,1,0:T(8,128)(2,1)} %reshape.91), calls=%async_computation | async-start | bytes 3145728 | tf_op jit(solution)/shard_map/all_to_all | solution.py:72
  19.2 2.9 convolution_convert_fusion.3
  22.1 3.7 %reshape.93 = bf16[64,96,128]{2,1,0:T(8,128)(2,1)} reshape(bf16[192,4096]{1,0:T(8,128)(2,1)} %convolution_convert_fusion.3) | data formatting | bytes 3145728 | tf_op jit(solution)/shard_map/reshape | solution.py:61
  25.9 33.3 %all-to-all-done = bf16[64,96,128]{2,1,0:T(8,128)(2,1)S(1)} async-done(((bf16[64,96,128]{2,1,0:T(8,128)(2,1)}), bf16[64,96,128]{2,1,0:T(8,128)(2,1)S(1)}, u32[]{:S(2)}, u32[]{:S(2)}) %all-to-all-start) | async-done | bytes 1572896 | tf_op jit(solution)/shard_map/all_to_all | solution.py:72
  59.2 5.6 %all-to-all-start.1 = ((bf16[64,96,128]{2,1,0:T(8,128)(2,1)}), bf16[64,96,128]{2,1,0:T(8,128)(2,1)}, u32[]{:S(2)}, u32[]{:S(2)}) async-start(bf16[64,96,128]{2,1,0:T(8,128)(2,1)} %reshape.93), calls=%async_computation.1 | async-start | bytes 3145728 | tf_op jit(solution)/shard_map/all_to_all | solution.py:71
  70.1 34.6 %all-to-all-done.1 = bf16[64,96,128]{2,1,0:T(8,128)(2,1)} async-done(((bf16[64,96,128]{2,1,0:T(8,128)(2,1)}), bf16[64,96,128]{2,1,0:T(8,128)(2,1)}, u32[]{:S(2)}, u32[]{:S(2)}) %all-to-all-start.1) | async-done | bytes 1572896 | tf_op jit(solution)/shard_map/all_to_all | solution.py:71
  104.7 2.5 reshape.94
  115.0 3.0 collective-permute-start.3
  118.0 27.8 %collective-permute-done.5 = bf16[192,4096]{1,0:T(8,128)(2,1)S(1)} collective-permute-done((bf16[192,4096]{1,0:T(8,128)(2,1)S(1)}, bf16[192,4096]{1,0:T(8,128)(2,1)S(1)}, u32[]{:S(2)}, u32[]{:S(2)}) %collective-permute-start.5) | collective-permute-done | bytes 1572896 | tf_op jit(solution)/shard_map/ppermute | solution.py:18
  146.3 3.2 %collective-permute-start.7 = (bf16[96,4096]{1,0:T(8,128)(2,1)S(1)}, bf16[96,4096]{1,0:T(8,128)(2,1)S(1)}, u32[]{:S(2)}, u32[]{:S(2)}) collective-permute-start(bf16[96,4096]{1,0:T(8,128)(2,1)S(1)} %slice.103), channel_id=1, source_target_pairs={{0,192},{64,0},{128,64},{192,128},{1,193},{65,1},{129,65},{193,129... | collective-permute-start | bytes 2359304 | tf_op jit(solution)/shard_map/ppermute | solution.py:21
  151.2 25.8 %collective-permute-done.6 = bf16[96,4096]{1,0:T(8,128)(2,1)S(1)} collective-permute-done((bf16[96,4096]{1,0:T(8,128)(2,1)S(1)}, bf16[96,4096]{1,0:T(8,128)(2,1)S(1)}, u32[]{:S(2)}, u32[]{:S(2)}) %collective-permute-start.6) | collective-permute-done | bytes 786464 | tf_op jit(solution)/shard_map/ppermute | solution.py:20
  184.1 3.1 multiply_reduce_fusion
  189.3 3.0 collective-permute-start.10
  194.6 12.1 %collective-permute-done.10 = bf16[96,4096]{1,0:T(8,128)(2,1)S(1)} collective-permute-done((bf16[96,4096]{1,0:T(8,128)(2,1)S(1)}, bf16[96,4096]{1,0:T(8,128)(2,1)S(1)}, u32[]{:S(2)}, u32[]{:S(2)}) %collective-permute-start.10) | collective-permute-done | bytes 786464 | tf_op jit(solution)/shard_map/ppermute | solution.py:32
  207.0 3.6 %collective-permute-start.11 = (bf16[192,4096]{1,0:T(8,128)(2,1)S(1)}, bf16[192,4096]{1,0:T(8,128)(2,1)}, u32[]{:S(2)}, u32[]{:S(2)}) collective-permute-start(bf16[192,4096]{1,0:T(8,128)(2,1)S(1)} %pad_maximum_fusion.1), channel_id=1, source_target_pairs={{0,192},{64,0},{128,64},{192,128},{1,193},{65,1},{129,65},{193,129... | collective-permute-start | bytes 4718600 | tf_op jit(solution)/shard_map/ppermute | solution.py:36
  212.3 3.2 %collective-permute-start.14 = (f32[192,1]{0,1:T(1,128)S(1)}, f32[192,1]{0,1:T(1,128)S(1)}, u32[]{:S(2)}, u32[]{:S(2)}) collective-permute-start(f32[192,1]{0,1:T(1,128)S(1)} %bitcast.71), channel_id=1, source_target_pairs={{0,192},{64,0},{128,64},{192,128},{1,193},{65,1},{129,65},{193,129... | collective-permute-start | bytes 2312 | tf_op jit(solution)/shard_map/ppermute | solution.py:111
  219.9 21.0 %collective-permute-done.14 = f32[192,1]{0,1:T(1,128)S(1)} collective-permute-done((f32[192,1]{0,1:T(1,128)S(1)}, f32[192,1]{0,1:T(1,128)S(1)}, u32[]{:S(2)}, u32[]{:S(2)}) %collective-permute-start.14) | collective-permute-done | bytes 800 | tf_op jit(solution)/shard_map/ppermute | solution.py:111
  241.0 5.2 %collective-permute-done.12 = f32[192,1]{0,1:T(1,128)S(1)} collective-permute-done((f32[192,1]{0,1:T(1,128)S(1)}, f32[192,1]{0,1:T(1,128)S(1)}, u32[]{:S(2)}, u32[]{:S(2)}) %collective-permute-start.12) | collective-permute-done | bytes 800 | tf_op jit(solution)/shard_map/ppermute | solution.py:111
  246.4 4.6 %add_convert_fusion = bf16[192,4096]{1,0:T(8,128)(2,1)} fusion(bf16[192,4096]{1,0:T(8,128)(2,1)} %collective-permute-done.11, f32[192,4096]{1,0:T(8,128)} %convolution_add_fusion.3, bf16[192,4096]{1,0:T(8,128)(2,1)} %collective-permute-done.9), kind=kLoop, calls=%fused_computation.16 | loop fusion | flops 3932160 | bytes 7864320 | tf_op jit(solution)/shard_map/convert_element_type | solution.py:107
  251.0 2.6 reshape.95
  255.0 11.6 %all-to-all-start.2 = ((bf16[64,112,128]{2,1,0:T(8,128)(2,1)}), bf16[64,112,128]{2,1,0:T(8,128)(2,1)S(1)}, u32[]{:S(2)}, u32[]{:S(2)}) async-start(bf16[64,112,128]{2,1,0:T(8,128)(2,1)} %fusion.5), calls=%async_computation.2 | async-start | bytes 3670016 | tf_op jit(solution)/shard_map/all_to_all | solution.py:125
  266.6 5.6 %fusion.2 = bf16[1,4096,192]{1,2,0:T(8,128)(2,1)} fusion(bf16[768,192]{0,1:T(8,128)(2,1)} %copy-done.4, bf16[768,4096]{1,0:T(8,128)(2,1)} %copy-done.5), kind=kOutput, calls=%fused_computation.12 | convolution fusion | flops 1208745984 | bytes 8159232 | tf_op jit(solution)/shard_map/dot_general | solution.py:116
  272.2 5.5 %fusion.3 = bf16[1,4096,192]{1,2,0:T(8,128)(2,1)} fusion(bf16[768,192]{0,1:T(8,128)(2,1)S(1)} %copy-done.3, bf16[768,4096]{1,0:T(8,128)(2,1)} %copy-done.5), kind=kOutput, calls=%fused_computation.13 | convolution fusion | flops 1208745984 | bytes 8159232 | tf_op jit(solution)/shard_map/dot_general | solution.py:119
  280.3 31.9 %all-to-all-done.2 = bf16[64,112,128]{2,1,0:T(8,128)(2,1)S(1)} async-done(((bf16[64,112,128]{2,1,0:T(8,128)(2,1)}), bf16[64,112,128]{2,1,0:T(8,128)(2,1)S(1)}, u32[]{:S(2)}, u32[]{:S(2)}) %all-to-all-start.2) | async-done | bytes 1835040 | tf_op jit(solution)/shard_map/all_to_all | solution.py:125
  (94 shorter events, 49.4 us)
Async XLA Ops:
  0.6 176.6 %copy-start = (bf16[1,4096,192]{1,2,0:T(8,128)(2,1)S(1)}, bf16[1,4096,192]{1,2,0:T(8,128)(2,1)}, u32[]{:S(2)}) copy-start(bf16[1,4096,192]{1,2,0:T(8,128)(2,1)} %param.11) | copy-start | bytes 4718596
  7.1 52.1 %all-to-all-start = ((bf16[64,96,128]{2,1,0:T(8,128)(2,1)}), bf16[64,96,128]{2,1,0:T(8,128)(2,1)S(1)}, u32[]{:S(2)}, u32[]{:S(2)}) async-start(bf16[64,96,128]{2,1,0:T(8,128)(2,1)} %reshape.91), calls=%async_computation | async-start | bytes 3145728 | tf_op jit(solution)/shard_map/all_to_all | solution.py:72
  59.2 45.5 %all-to-all-start.1 = ((bf16[64,96,128]{2,1,0:T(8,128)(2,1)}), bf16[64,96,128]{2,1,0:T(8,128)(2,1)}, u32[]{:S(2)}, u32[]{:S(2)}) async-start(bf16[64,96,128]{2,1,0:T(8,128)(2,1)} %reshape.93), calls=%async_computation.1 | async-start | bytes 3145728 | tf_op jit(solution)/shard_map/all_to_all | solution.py:71
  66.8 45.4 %collective-permute-start.1 = (bf16[192,4096]{1,0:T(8,128)(2,1)}, bf16[192,4096]{1,0:T(8,128)(2,1)}, u32[]{:S(2)}, u32[]{:S(2)}) collective-permute-start(bf16[192,4096]{1,0:T(8,128)(2,1)} %reshape.92), channel_id=1, source_target_pairs={{0,64},{64,128},{128,192},{192,0},{1,65},{65,129},{129,193},{193,1... | collective-permute-start | bytes 4718600 | tf_op jit(solution)/shard_map/ppermute | solution.py:18
  68.3 45.5 %collective-permute-start = (bf16[192,4096]{1,0:T(8,128)(2,1)}, bf16[192,4096]{1,0:T(8,128)(2,1)}, u32[]{:S(2)}, u32[]{:S(2)}) collective-permute-start(bf16[192,4096]{1,0:T(8,128)(2,1)} %reshape.92), channel_id=1, source_target_pairs={{0,192},{64,0},{128,64},{192,128},{1,193},{65,1},{129,65},{193,129... | collective-permute-start | bytes 4718600 | tf_op jit(solution)/shard_map/ppermute | solution.py:19
  107.3 38.6 %collective-permute-start.5 = (bf16[192,4096]{1,0:T(8,128)(2,1)S(1)}, bf16[192,4096]{1,0:T(8,128)(2,1)S(1)}, u32[]{:S(2)}, u32[]{:S(2)}) collective-permute-start(bf16[192,4096]{1,0:T(8,128)(2,1)S(1)} %reshape.94), channel_id=1, source_target_pairs={{0,64},{64,128},{128,192},{192,0},{1,65},{65,129},{129,193},{193,1... | collective-permute-start | bytes 4718600 | tf_op jit(solution)/shard_map/ppermute | solution.py:18
  108.9 37.4 %collective-permute-start.4 = (bf16[192,4096]{1,0:T(8,128)(2,1)S(1)}, bf16[192,4096]{1,0:T(8,128)(2,1)S(1)}, u32[]{:S(2)}, u32[]{:S(2)}) collective-permute-start(bf16[192,4096]{1,0:T(8,128)(2,1)S(1)} %reshape.94), channel_id=1, source_target_pairs={{0,192},{64,0},{128,64},{192,128},{1,193},{65,1},{129,65},{193,129... | collective-permute-start | bytes 4718600 | tf_op jit(solution)/shard_map/ppermute | solution.py:19
  113.5 66.1 %collective-permute-start.2 = (bf16[96,4096]{1,0:T(8,128)(2,1)S(1)}, bf16[96,4096]{1,0:T(8,128)(2,1)S(1)}, u32[]{:S(2)}, u32[]{:S(2)}) collective-permute-start(bf16[96,4096]{1,0:T(8,128)(2,1)S(1)} %slice.100), channel_id=1, source_target_pairs={{0,64},{64,128},{128,192},{192,0},{1,65},{65,129},{129,193},{193,1... | collective-permute-start | bytes 2359304 | tf_op jit(solution)/shard_map/ppermute | solution.py:20
  115.0 67.1 %collective-permute-start.3 = (bf16[96,4096]{1,0:T(8,128)(2,1)S(1)}, bf16[96,4096]{1,0:T(8,128)(2,1)S(1)}, u32[]{:S(2)}, u32[]{:S(2)}) collective-permute-start(bf16[96,4096]{1,0:T(8,128)(2,1)S(1)} %slice.101), channel_id=1, source_target_pairs={{0,192},{64,0},{128,64},{192,128},{1,193},{65,1},{129,65},{193,129... | collective-permute-start | bytes 2359304 | tf_op jit(solution)/shard_map/ppermute | solution.py:21
  145.9 31.1 %collective-permute-start.6 = (bf16[96,4096]{1,0:T(8,128)(2,1)S(1)}, bf16[96,4096]{1,0:T(8,128)(2,1)S(1)}, u32[]{:S(2)}, u32[]{:S(2)}) collective-permute-start(bf16[96,4096]{1,0:T(8,128)(2,1)S(1)} %slice.102), channel_id=1, source_target_pairs={{0,64},{64,128},{128,192},{192,0},{1,65},{65,129},{129,193},{193,1... | collective-permute-start | bytes 2359304 | tf_op jit(solution)/shard_map/ppermute | solution.py:20
  146.3 30.7 %collective-permute-start.7 = (bf16[96,4096]{1,0:T(8,128)(2,1)S(1)}, bf16[96,4096]{1,0:T(8,128)(2,1)S(1)}, u32[]{:S(2)}, u32[]{:S(2)}) collective-permute-start(bf16[96,4096]{1,0:T(8,128)(2,1)S(1)} %slice.103), channel_id=1, source_target_pairs={{0,192},{64,0},{128,64},{192,128},{1,193},{65,1},{129,65},{193,129... | collective-permute-start | bytes 2359304 | tf_op jit(solution)/shard_map/ppermute | solution.py:21
  187.3 29.8 %copy-start.4 = (bf16[768,192]{0,1:T(8,128)(2,1)}, bf16[768,192]{0,1:T(8,128)(2,1)S(1)}, u32[]{:S(2)}) copy-start(bf16[768,192]{0,1:T(8,128)(2,1)S(1)} %get-tuple-element.7) | copy-start | bytes 884740
  187.3 30.4 %copy-start.2 = (bf16[768,192]{0,1:T(8,128)(2,1)}, bf16[768,192]{0,1:T(8,128)(2,1)S(1)}, u32[]{:S(2)}) copy-start(bf16[768,192]{0,1:T(8,128)(2,1)S(1)} %get-tuple-element.10) | copy-start | bytes 884740
  189.3 17.3 %collective-permute-start.10 = (bf16[96,4096]{1,0:T(8,128)(2,1)S(1)}, bf16[96,4096]{1,0:T(8,128)(2,1)S(1)}, u32[]{:S(2)}, u32[]{:S(2)}) collective-permute-start(bf16[96,4096]{1,0:T(8,128)(2,1)S(1)} %get-tuple-element.9), channel_id=1, source_target_pairs={{0,192},{64,0},{128,64},{192,128},{1,193},{65,1},{129,65},{193,129... | collective-permute-start | bytes 2359304 | tf_op jit(solution)/shard_map/ppermute | solution.py:32
  193.0 17.7 %collective-permute-start.8 = (bf16[96,4096]{1,0:T(8,128)(2,1)S(1)}, bf16[96,4096]{1,0:T(8,128)(2,1)S(1)}, u32[]{:S(2)}, u32[]{:S(2)}) collective-permute-start(bf16[96,4096]{1,0:T(8,128)(2,1)S(1)} %get-tuple-element.8), channel_id=1, source_target_pairs={{0,64},{64,128},{128,192},{192,0},{1,65},{65,129},{129,193},{193,1... | collective-permute-start | bytes 2359304 | tf_op jit(solution)/shard_map/ppermute | solution.py:31
  207.0 39.4 %collective-permute-start.11 = (bf16[192,4096]{1,0:T(8,128)(2,1)S(1)}, bf16[192,4096]{1,0:T(8,128)(2,1)}, u32[]{:S(2)}, u32[]{:S(2)}) collective-permute-start(bf16[192,4096]{1,0:T(8,128)(2,1)S(1)} %pad_maximum_fusion.1), channel_id=1, source_target_pairs={{0,192},{64,0},{128,64},{192,128},{1,193},{65,1},{129,65},{193,129... | collective-permute-start | bytes 4718600 | tf_op jit(solution)/shard_map/ppermute | solution.py:36
  212.2 34.2 %collective-permute-start.9 = (bf16[192,4096]{1,0:T(8,128)(2,1)}, bf16[192,4096]{1,0:T(8,128)(2,1)}, u32[]{:S(2)}, u32[]{:S(2)}) collective-permute-start(bf16[192,4096]{1,0:T(8,128)(2,1)} %pad_maximum_fusion), channel_id=1, source_target_pairs={{0,64},{64,128},{128,192},{192,0},{1,65},{65,129},{129,193},{193,1... | collective-permute-start | bytes 4718600 | tf_op jit(solution)/shard_map/ppermute | solution.py:35
  212.3 28.7 %collective-permute-start.14 = (f32[192,1]{0,1:T(1,128)S(1)}, f32[192,1]{0,1:T(1,128)S(1)}, u32[]{:S(2)}, u32[]{:S(2)}) collective-permute-start(f32[192,1]{0,1:T(1,128)S(1)} %bitcast.71), channel_id=1, source_target_pairs={{0,192},{64,0},{128,64},{192,128},{1,193},{65,1},{129,65},{193,129... | collective-permute-start | bytes 2312 | tf_op jit(solution)/shard_map/ppermute | solution.py:111
  215.5 30.7 %collective-permute-start.12 = (f32[192,1]{0,1:T(1,128)S(1)}, f32[192,1]{0,1:T(1,128)S(1)}, u32[]{:S(2)}, u32[]{:S(2)}) collective-permute-start(f32[192,1]{0,1:T(1,128)S(1)} %bitcast.70), channel_id=1, source_target_pairs={{0,64},{64,128},{128,192},{192,0},{1,65},{65,129},{129,193},{193,1... | collective-permute-start | bytes 2312 | tf_op jit(solution)/shard_map/ppermute | solution.py:111
  215.5 30.7 %collective-permute-start.13 = (f32[192,1]{0,1:T(1,128)S(1)}, f32[192,1]{0,1:T(1,128)S(1)}, u32[]{:S(2)}, u32[]{:S(2)}) collective-permute-start(f32[192,1]{0,1:T(1,128)S(1)} %bitcast.69), channel_id=1, source_target_pairs={{0,128},{64,192},{128,0},{192,64},{1,129},{65,193},{129,1},{193,65... | collective-permute-start | bytes 2312 | tf_op jit(solution)/shard_map/ppermute | solution.py:111
  255.0 57.2 %all-to-all-start.2 = ((bf16[64,112,128]{2,1,0:T(8,128)(2,1)}), bf16[64,112,128]{2,1,0:T(8,128)(2,1)S(1)}, u32[]{:S(2)}, u32[]{:S(2)}) async-start(bf16[64,112,128]{2,1,0:T(8,128)(2,1)} %fusion.5), calls=%async_computation.2 | async-start | bytes 3670016 | tf_op jit(solution)/shard_map/all_to_all | solution.py:125
  266.6 5.6 %copy-start.3 = (bf16[768,192]{0,1:T(8,128)(2,1)S(1)}, bf16[768,192]{0,1:T(8,128)(2,1)}, u32[]{:S(2)}) copy-start(bf16[768,192]{0,1:T(8,128)(2,1)} %copy-done.2) | copy-start | bytes 884740
  266.6 11.1 %slice-start = ((s8[6291456]{0:T(1024)(128)(4,1)}), s8[4194304]{0:T(1024)(128)(4,1)S(1)}, s32[]{:S(2)}) async-start(s8[6291456]{0:T(1024)(128)(4,1)} %bitcast.64), calls=%async_computation.3 | async-start | bytes 8388608
  277.8 34.7 %copy-start.7 = (bf16[128,1]{0,1:T(2,128)(2,1)S(1)}, bf16[128,1]{0,1:T(2,128)(2,1)}, u32[]{:S(2)}) copy-start(bf16[128,1]{0,1:T(2,128)(2,1)} %param.10) | copy-start | bytes 772
  (6 other events, 21.4 us)

commit v8 on v7

--- a/solution.py
+++ b/solution.py
@@ -8,6 +8,18 @@
 
 def ring_pairs(count, step):
     return [(i, (i + step) % count) for i in range(count)]
+
+
+def ring_gather_blocks(x, axis):
+    count = lax.axis_size(axis)
+    fwd = ring_pairs(count, 1)
+    bwd = ring_pairs(count, -1)
+    half = x.shape[0] // 2
+    from_prev = lax.ppermute(x, axis, fwd)
+    from_next = lax.ppermute(x, axis, bwd)
+    far_a = lax.ppermute(from_prev[:half], axis, fwd)
+    far_b = lax.ppermute(from_next[half:], axis, bwd)
+    return [x, from_next, jnp.concatenate([far_a, far_b], axis=0), from_prev]
 
 
 def ring_gather(x, axis):
@@ -70,15 +82,20 @@
     )
     recv_in = lax.all_to_all(sent_in, "expert", 0, 0, tiled=True).reshape(slot_total, width)
     recv_dy = lax.all_to_all(sent_dy, "expert", 0, 0, tiled=True).reshape(slot_total, width)
-    rows_in = ring_gather(recv_in, "dp")
+    in_blocks = ring_gather_blocks(recv_in, "dp")
+    rows_in = jnp.concatenate(in_blocks, axis=0)
     rows_dy = ring_gather(recv_dy, "dp")
     gate_w = w_gate[0]
     up_w = w_up[0]
     down_w = w_down[0]
     contract_last = (((1,), (1,)), ((), ()))
     contract_first = (((0,), (0,)), ((), ()))
-    gate_pre = jnp.dot(rows_in, gate_w, preferred_element_type=jnp.float32)
-    up_pre = jnp.dot(rows_in, up_w, preferred_element_type=jnp.float32)
+    gate_pre = jnp.concatenate(
+        [jnp.dot(b, gate_w, preferred_element_type=jnp.float32) for b in in_blocks], axis=0
+    )
+    up_pre = jnp.concatenate(
+        [jnp.dot(b, up_w, preferred_element_type=jnp.float32) for b in in_blocks], axis=0
+    )
     sigmoid_gate = jax.nn.sigmoid(gate_pre)
     active = gate_pre * sigmoid_gate
     hidden = (active * up_pre).astype(jnp.bfloat16)

time: 319 us -> 320 us (level)
  local copies, waits for them, and re-layouts: 26 us -> 30.4 us
    ppermute x0 -> x4, waiting for transfers between devices: none -> 49.5 us  [the longest x1 26.4 us: ring_gather_blocks(): from_prev = lax.ppermute(x, axis, fwd)]
    ppermute x2 -> x1, waiting for transfers between devices: 27.8 us -> 0.01 us  [ring_gather(): from_prev = lax.ppermute(x, axis, fwd)]
    ppermute x2 -> x1, waiting for transfers between devices: 25.8 us -> 0.01 us  [ring_gather(): far_a = lax.ppermute(from_prev[:half], axis, fwd)]
    ppermute x0 -> x4, starting transfers between devices: none -> 6.89 us  [the longest x1 3.21 us: ring_gather_blocks(): far_b = lax.ppermute(from_next[half:], axis, bwd)]
    ppermute x2 -> x1, starting transfers between devices: 6.25 us -> 3.04 us  [ring_gather(): far_b = lax.ppermute(from_next[half:], axis, bwd)]
where the time goes in v8:
time: 320 us; the launch traced here: 319 us
  waiting for transfers between devices  190 us (59%)
  starting transfers between devices  54.4 us (17%)
  matrix products  32.6 us (10%)
  local copies, waits for them, and re-layouts  30.4 us (10%)
  other arithmetic  10.5 us (3%)
    all_to_all x1, waiting for transfers between devices, body(): lax.all_to_all(sent_in, 'expert', 0, 0, tiled=True)  34.6 us
    all_to_all x1, waiting for transfers between devices, body(): lax.all_to_all(jnp.concatenate([own_rows, score_tile], axis=1), 'expert',...  33.5 us
    all_to_all x1, waiting for transfers between devices, body(): lax.all_to_all(sent_dy, 'expert', 0, 0, tiled=True)  33.3 us
    ppermute x1, waiting for transfers between devices, ring_gather_blocks(): from_prev = lax.ppermute(x, axis, fwd)  26.4 us
    ppermute x3, waiting for transfers between devices, body(): lax.ppermute(score_blocks[k], 'dp', ring_pairs(dp_count, k))  26.3 us
    ppermute x1, waiting for transfers between devices, ring_gather_blocks(): far_a = lax.ppermute(from_prev[:half], axis, fwd)  23.1 us
    ppermute x1, waiting for transfers between devices, ring_reduce_scatter(): got_b = lax.ppermute(far[half:].astype(wire), axis, bwd).astype(jnp.float32)  12.2 us
    all_to_all x1, starting transfers between devices, body(): lax.all_to_all(sent_dy, 'expert', 0, 0, tiled=True)  12.1 us
  transfers between devices with their start and end apart: 18, of which 9 were waited for; matrix products, arithmetic and copies ran while one was open for 13% of the time, Pallas kernels for 0%

profile of v8, /device:TPU:8, one launch (start us, length us, event | category | flops | bytes accessed | tf_op | source)
XLA Modules:
  0.0 318.7 jit_solution(16224685282154825927)
XLA Ops:
  7.1 12.1 %all-to-all-start = ((bf16[64,96,128]{2,1,0:T(8,128)(2,1)}), bf16[64,96,128]{2,1,0:T(8,128)(2,1)S(1)}, u32[]{:S(2)}, u32[]{:S(2)}) async-start(bf16[64,96,128]{2,1,0:T(8,128)(2,1)} %reshape.91), calls=%async_computation | async-start | bytes 3145728 | tf_op jit(solution)/shard_map/all_to_all | solution.py:84
  19.2 2.9 convolution_convert_fusion.3
  22.1 3.7 %reshape.93 = bf16[64,96,128]{2,1,0:T(8,128)(2,1)} reshape(bf16[192,4096]{1,0:T(8,128)(2,1)} %convolution_convert_fusion.3) | data formatting | bytes 3145728 | tf_op jit(solution)/shard_map/reshape | solution.py:73
  25.9 33.3 %all-to-all-done = bf16[64,96,128]{2,1,0:T(8,128)(2,1)S(1)} async-done(((bf16[64,96,128]{2,1,0:T(8,128)(2,1)}), bf16[64,96,128]{2,1,0:T(8,128)(2,1)S(1)}, u32[]{:S(2)}, u32[]{:S(2)}) %all-to-all-start) | async-done | bytes 1572896 | tf_op jit(solution)/shard_map/all_to_all | solution.py:84
  59.2 5.6 %all-to-all-start.1 = ((bf16[64,96,128]{2,1,0:T(8,128)(2,1)}), bf16[64,96,128]{2,1,0:T(8,128)(2,1)}, u32[]{:S(2)}, u32[]{:S(2)}) async-start(bf16[64,96,128]{2,1,0:T(8,128)(2,1)} %reshape.93), calls=%async_computation.1 | async-start | bytes 3145728 | tf_op jit(solution)/shard_map/all_to_all | solution.py:83
  70.1 34.6 %all-to-all-done.1 = bf16[64,96,128]{2,1,0:T(8,128)(2,1)} async-done(((bf16[64,96,128]{2,1,0:T(8,128)(2,1)}), bf16[64,96,128]{2,1,0:T(8,128)(2,1)}, u32[]{:S(2)}, u32[]{:S(2)}) %all-to-all-start.1) | async-done | bytes 1572896 | tf_op jit(solution)/shard_map/all_to_all | solution.py:83
  116.4 3.0 collective-permute-start.3
  119.4 26.4 %collective-permute-done.5 = bf16[192,4096]{1,0:T(8,128)(2,1)S(1)} collective-permute-done((bf16[192,4096]{1,0:T(8,128)(2,1)S(1)}, bf16[192,4096]{1,0:T(8,128)(2,1)S(1)}, u32[]{:S(2)}, u32[]{:S(2)}) %collective-permute-start.5) | collective-permute-done | bytes 1572896 | tf_op jit(solution)/shard_map/ppermute | solution.py:18
  146.3 3.2 %collective-permute-start.7 = (bf16[96,4096]{1,0:T(8,128)(2,1)S(1)}, bf16[96,4096]{1,0:T(8,128)(2,1)S(1)}, u32[]{:S(2)}, u32[]{:S(2)}) collective-permute-start(bf16[96,4096]{1,0:T(8,128)(2,1)S(1)} %slice.103), channel_id=1, source_target_pairs={{0,192},{64,0},{128,64},{192,128},{1,193},{65,1},{129,65},{193,129... | collective-permute-start | bytes 2359304 | tf_op jit(solution)/shard_map/ppermute | solution.py:21
  153.9 23.1 %collective-permute-done.6 = bf16[96,4096]{1,0:T(8,128)(2,1)S(1)} collective-permute-done((bf16[96,4096]{1,0:T(8,128)(2,1)S(1)}, bf16[96,4096]{1,0:T(8,128)(2,1)S(1)}, u32[]{:S(2)}, u32[]{:S(2)}) %collective-permute-start.6) | collective-permute-done | bytes 786464 | tf_op jit(solution)/shard_map/ppermute | solution.py:20
  181.8 3.0 multiply_reduce_fusion
  187.0 2.9 collective-permute-start.10
  192.3 12.2 %collective-permute-done.10 = bf16[96,4096]{1,0:T(8,128)(2,1)S(1)} collective-permute-done((bf16[96,4096]{1,0:T(8,128)(2,1)S(1)}, bf16[96,4096]{1,0:T(8,128)(2,1)S(1)}, u32[]{:S(2)}, u32[]{:S(2)}) %collective-permute-start.10) | collective-permute-done | bytes 786464 | tf_op jit(solution)/shard_map/ppermute | solution.py:44
  204.7 3.5 %collective-permute-start.11 = (bf16[192,4096]{1,0:T(8,128)(2,1)S(1)}, bf16[192,4096]{1,0:T(8,128)(2,1)}, u32[]{:S(2)}, u32[]{:S(2)}) collective-permute-start(bf16[192,4096]{1,0:T(8,128)(2,1)S(1)} %pad_maximum_fusion.1), channel_id=1, source_target_pairs={{0,192},{64,0},{128,64},{192,128},{1,193},{65,1},{129,65},{193,129... | collective-permute-start | bytes 4718600 | tf_op jit(solution)/shard_map/ppermute | solution.py:48
  209.9 3.2 %collective-permute-start.14 = (f32[192,1]{0,1:T(1,128)S(1)}, f32[192,1]{0,1:T(1,128)S(1)}, u32[]{:S(2)}, u32[]{:S(2)}) collective-permute-start(f32[192,1]{0,1:T(1,128)S(1)} %bitcast.89), channel_id=1, source_target_pairs={{0,192},{64,0},{128,64},{192,128},{1,193},{65,1},{129,65},{193,129... | collective-permute-start | bytes 2312 | tf_op jit(solution)/shard_map/ppermute | solution.py:128
  217.6 21.0 %collective-permute-done.14 = f32[192,1]{0,1:T(1,128)S(1)} collective-permute-done((f32[192,1]{0,1:T(1,128)S(1)}, f32[192,1]{0,1:T(1,128)S(1)}, u32[]{:S(2)}, u32[]{:S(2)}) %collective-permute-start.14) | collective-permute-done | bytes 800 | tf_op jit(solution)/shard_map/ppermute | solution.py:128
  238.6 5.3 %collective-permute-done.12 = f32[192,1]{0,1:T(1,128)S(1)} collective-permute-done((f32[192,1]{0,1:T(1,128)S(1)}, f32[192,1]{0,1:T(1,128)S(1)}, u32[]{:S(2)}, u32[]{:S(2)}) %collective-permute-start.12) | collective-permute-done | bytes 800 | tf_op jit(solution)/shard_map/ppermute | solution.py:128
  244.1 4.6 %add_convert_fusion = bf16[192,4096]{1,0:T(8,128)(2,1)} fusion(bf16[192,4096]{1,0:T(8,128)(2,1)} %collective-permute-done.11, f32[192,4096]{1,0:T(8,128)} %convolution_add_fusion.3, bf16[192,4096]{1,0:T(8,128)(2,1)} %collective-permute-done.9), kind=kLoop, calls=%fused_computation.16 | loop fusion | flops 3932160 | bytes 7864320 | tf_op jit(solution)/shard_map/convert_element_type | solution.py:124
  248.7 2.6 reshape.95
  252.7 11.9 %all-to-all-start.2 = ((bf16[64,112,128]{2,1,0:T(8,128)(2,1)}), bf16[64,112,128]{2,1,0:T(8,128)(2,1)}, u32[]{:S(2)}, u32[]{:S(2)}) async-start(bf16[64,112,128]{2,1,0:T(8,128)(2,1)} %fusion.5), calls=%async_computation.2 | async-start | bytes 3670016 | tf_op jit(solution)/shard_map/all_to_all | solution.py:142
  265.9 5.5 %fusion.3 = bf16[1,4096,192]{1,2,0:T(8,128)(2,1)} fusion(bf16[768,192]{0,1:T(8,128)(2,1)S(1)} %multiply_convert_fusion.1, bf16[768,4096]{1,0:T(8,128)(2,1)} %constant_dynamic-update-slice_fusion.7), kind=kOutput, calls=%fused_computation.13 | convolution fusion | flops 1208745984 | bytes 8159232 | tf_op jit(solution)/shard_map/dot_general | solution.py:136
  271.4 2.6 fusion.2
  276.6 33.5 %all-to-all-done.2 = bf16[64,112,128]{2,1,0:T(8,128)(2,1)} async-done(((bf16[64,112,128]{2,1,0:T(8,128)(2,1)}), bf16[64,112,128]{2,1,0:T(8,128)(2,1)}, u32[]{:S(2)}, u32[]{:S(2)}) %all-to-all-start.2) | async-done | bytes 1835040 | tf_op jit(solution)/shard_map/all_to_all | solution.py:142
  312.0 2.7 slice.118
  (105 shorter events, 55.0 us)
Async XLA Ops:
  0.6 110.0 %copy-start = (bf16[1,4096,192]{1,2,0:T(8,128)(2,1)S(1)}, bf16[1,4096,192]{1,2,0:T(8,128)(2,1)}, u32[]{:S(2)}) copy-start(bf16[1,4096,192]{1,2,0:T(8,128)(2,1)} %param.11) | copy-start | bytes 4718596
  7.1 52.1 %all-to-all-start = ((bf16[64,96,128]{2,1,0:T(8,128)(2,1)}), bf16[64,96,128]{2,1,0:T(8,128)(2,1)S(1)}, u32[]{:S(2)}, u32[]{:S(2)}) async-start(bf16[64,96,128]{2,1,0:T(8,128)(2,1)} %reshape.91), calls=%async_computation | async-start | bytes 3145728 | tf_op jit(solution)/shard_map/all_to_all | solution.py:84
  59.2 45.5 %all-to-all-start.1 = ((bf16[64,96,128]{2,1,0:T(8,128)(2,1)}), bf16[64,96,128]{2,1,0:T(8,128)(2,1)}, u32[]{:S(2)}, u32[]{:S(2)}) async-start(bf16[64,96,128]{2,1,0:T(8,128)(2,1)} %reshape.93), calls=%async_computation.1 | async-start | bytes 3145728 | tf_op jit(solution)/shard_map/all_to_all | solution.py:83
  66.8 46.8 %collective-permute-start.1 = (bf16[192,4096]{1,0:T(8,128)(2,1)}, bf16[192,4096]{1,0:T(8,128)(2,1)}, u32[]{:S(2)}, u32[]{:S(2)}) collective-permute-start(bf16[192,4096]{1,0:T(8,128)(2,1)} %reshape.92), channel_id=1, source_target_pairs={{0,64},{64,128},{128,192},{192,0},{1,65},{65,129},{129,193},{193,1... | collective-permute-start | bytes 4718600 | tf_op jit(solution)/shard_map/ppermute | solution.py:30
  68.3 46.9 %collective-permute-start = (bf16[192,4096]{1,0:T(8,128)(2,1)}, bf16[192,4096]{1,0:T(8,128)(2,1)}, u32[]{:S(2)}, u32[]{:S(2)}) collective-permute-start(bf16[192,4096]{1,0:T(8,128)(2,1)} %reshape.92), channel_id=1, source_target_pairs={{0,192},{64,0},{128,64},{192,128},{1,193},{65,1},{129,65},{193,129... | collective-permute-start | bytes 4718600 | tf_op jit(solution)/shard_map/ppermute | solution.py:31
  107.3 38.6 %collective-permute-start.5 = (bf16[192,4096]{1,0:T(8,128)(2,1)S(1)}, bf16[192,4096]{1,0:T(8,128)(2,1)S(1)}, u32[]{:S(2)}, u32[]{:S(2)}) collective-permute-start(bf16[192,4096]{1,0:T(8,128)(2,1)S(1)} %reshape.94), channel_id=1, source_target_pairs={{0,64},{64,128},{128,192},{192,0},{1,65},{65,129},{129,193},{193,1... | collective-permute-start | bytes 4718600 | tf_op jit(solution)/shard_map/ppermute | solution.py:18
  108.9 37.4 %collective-permute-start.4 = (bf16[192,4096]{1,0:T(8,128)(2,1)S(1)}, bf16[192,4096]{1,0:T(8,128)(2,1)S(1)}, u32[]{:S(2)}, u32[]{:S(2)}) collective-permute-start(bf16[192,4096]{1,0:T(8,128)(2,1)S(1)} %reshape.94), channel_id=1, source_target_pairs={{0,192},{64,0},{128,64},{192,128},{1,193},{65,1},{129,65},{193,129... | collective-permute-start | bytes 4718600 | tf_op jit(solution)/shard_map/ppermute | solution.py:19
  114.9 63.8 %collective-permute-start.2 = (bf16[96,4096]{1,0:T(8,128)(2,1)S(1)}, bf16[96,4096]{1,0:T(8,128)(2,1)S(1)}, u32[]{:S(2)}, u32[]{:S(2)}) collective-permute-start(bf16[96,4096]{1,0:T(8,128)(2,1)S(1)} %slice.100), channel_id=1, source_target_pairs={{0,64},{64,128},{128,192},{192,0},{1,65},{65,129},{129,193},{193,1... | collective-permute-start | bytes 2359304 | tf_op jit(solution)/shard_map/ppermute | solution.py:32
  116.4 62.3 %collective-permute-start.3 = (bf16[96,4096]{1,0:T(8,128)(2,1)S(1)}, bf16[96,4096]{1,0:T(8,128)(2,1)S(1)}, u32[]{:S(2)}, u32[]{:S(2)}) collective-permute-start(bf16[96,4096]{1,0:T(8,128)(2,1)S(1)} %slice.101), channel_id=1, source_target_pairs={{0,192},{64,0},{128,64},{192,128},{1,193},{65,1},{129,65},{193,129... | collective-permute-start | bytes 2359304 | tf_op jit(solution)/shard_map/ppermute | solution.py:33
  145.9 31.1 %collective-permute-start.6 = (bf16[96,4096]{1,0:T(8,128)(2,1)S(1)}, bf16[96,4096]{1,0:T(8,128)(2,1)S(1)}, u32[]{:S(2)}, u32[]{:S(2)}) collective-permute-start(bf16[96,4096]{1,0:T(8,128)(2,1)S(1)} %slice.102), channel_id=1, source_target_pairs={{0,64},{64,128},{128,192},{192,0},{1,65},{65,129},{129,193},{193,1... | collective-permute-start | bytes 2359304 | tf_op jit(solution)/shard_map/ppermute | solution.py:20
  146.3 30.8 %collective-permute-start.7 = (bf16[96,4096]{1,0:T(8,128)(2,1)S(1)}, bf16[96,4096]{1,0:T(8,128)(2,1)S(1)}, u32[]{:S(2)}, u32[]{:S(2)}) collective-permute-start(bf16[96,4096]{1,0:T(8,128)(2,1)S(1)} %slice.103), channel_id=1, source_target_pairs={{0,192},{64,0},{128,64},{192,128},{1,193},{65,1},{129,65},{193,129... | collective-permute-start | bytes 2359304 | tf_op jit(solution)/shard_map/ppermute | solution.py:21
  184.8 29.9 %copy-start.4 = (bf16[768,192]{0,1:T(8,128)(2,1)}, bf16[768,192]{0,1:T(8,128)(2,1)S(1)}, u32[]{:S(2)}) copy-start(bf16[768,192]{0,1:T(8,128)(2,1)S(1)} %get-tuple-element.7) | copy-start | bytes 884740
  187.0 17.4 %collective-permute-start.10 = (bf16[96,4096]{1,0:T(8,128)(2,1)S(1)}, bf16[96,4096]{1,0:T(8,128)(2,1)S(1)}, u32[]{:S(2)}, u32[]{:S(2)}) collective-permute-start(bf16[96,4096]{1,0:T(8,128)(2,1)S(1)} %get-tuple-element.9), channel_id=1, source_target_pairs={{0,192},{64,0},{128,64},{192,128},{1,193},{65,1},{129,65},{193,129... | collective-permute-start | bytes 2359304 | tf_op jit(solution)/shard_map/ppermute | solution.py:44
  190.7 17.7 %collective-permute-start.8 = (bf16[96,4096]{1,0:T(8,128)(2,1)S(1)}, bf16[96,4096]{1,0:T(8,128)(2,1)S(1)}, u32[]{:S(2)}, u32[]{:S(2)}) collective-permute-start(bf16[96,4096]{1,0:T(8,128)(2,1)S(1)} %get-tuple-element.8), channel_id=1, source_target_pairs={{0,64},{64,128},{128,192},{192,0},{1,65},{65,129},{129,193},{193,1... | collective-permute-start | bytes 2359304 | tf_op jit(solution)/shard_map/ppermute | solution.py:43
  204.7 39.3 %collective-permute-start.11 = (bf16[192,4096]{1,0:T(8,128)(2,1)S(1)}, bf16[192,4096]{1,0:T(8,128)(2,1)}, u32[]{:S(2)}, u32[]{:S(2)}) collective-permute-start(bf16[192,4096]{1,0:T(8,128)(2,1)S(1)} %pad_maximum_fusion.1), channel_id=1, source_target_pairs={{0,192},{64,0},{128,64},{192,128},{1,193},{65,1},{129,65},{193,129... | collective-permute-start | bytes 4718600 | tf_op jit(solution)/shard_map/ppermute | solution.py:48
  209.9 34.2 %collective-permute-start.9 = (bf16[192,4096]{1,0:T(8,128)(2,1)}, bf16[192,4096]{1,0:T(8,128)(2,1)}, u32[]{:S(2)}, u32[]{:S(2)}) collective-permute-start(bf16[192,4096]{1,0:T(8,128)(2,1)} %pad_maximum_fusion), channel_id=1, source_target_pairs={{0,64},{64,128},{128,192},{192,0},{1,65},{65,129},{129,193},{193,1... | collective-permute-start | bytes 4718600 | tf_op jit(solution)/shard_map/ppermute | solution.py:47
  209.9 28.6 %collective-permute-start.14 = (f32[192,1]{0,1:T(1,128)S(1)}, f32[192,1]{0,1:T(1,128)S(1)}, u32[]{:S(2)}, u32[]{:S(2)}) collective-permute-start(f32[192,1]{0,1:T(1,128)S(1)} %bitcast.89), channel_id=1, source_target_pairs={{0,192},{64,0},{128,64},{192,128},{1,193},{65,1},{129,65},{193,129... | collective-permute-start | bytes 2312 | tf_op jit(solution)/shard_map/ppermute | solution.py:128
  213.2 30.7 %collective-permute-start.12 = (f32[192,1]{0,1:T(1,128)S(1)}, f32[192,1]{0,1:T(1,128)S(1)}, u32[]{:S(2)}, u32[]{:S(2)}) collective-permute-start(f32[192,1]{0,1:T(1,128)S(1)} %bitcast.88), channel_id=1, source_target_pairs={{0,64},{64,128},{128,192},{192,0},{1,65},{65,129},{129,193},{193,1... | collective-permute-start | bytes 2312 | tf_op jit(solution)/shard_map/ppermute | solution.py:128
  213.2 30.7 %collective-permute-start.13 = (f32[192,1]{0,1:T(1,128)S(1)}, f32[192,1]{0,1:T(1,128)S(1)}, u32[]{:S(2)}, u32[]{:S(2)}) collective-permute-start(f32[192,1]{0,1:T(1,128)S(1)} %bitcast.87), channel_id=1, source_target_pairs={{0,128},{64,192},{128,0},{192,64},{1,129},{65,193},{129,1},{193,65... | collective-permute-start | bytes 2312 | tf_op jit(solution)/shard_map/ppermute | solution.py:128
  252.7 11.9 %copy-start.3 = (bf16[192,4096]{1,0:T(8,128)(2,1)S(1)}, bf16[192,4096]{1,0:T(8,128)(2,1)}, u32[]{:S(2)}) copy-start(bf16[192,4096]{1,0:T(8,128)(2,1)} %copy-done.2) | copy-start | bytes 4718596
  252.7 57.5 %all-to-all-start.2 = ((bf16[64,112,128]{2,1,0:T(8,128)(2,1)}), bf16[64,112,128]{2,1,0:T(8,128)(2,1)}, u32[]{:S(2)}, u32[]{:S(2)}) async-start(bf16[64,112,128]{2,1,0:T(8,128)(2,1)} %fusion.5), calls=%async_computation.2 | async-start | bytes 3670016 | tf_op jit(solution)/shard_map/all_to_all | solution.py:142
  265.9 5.5 %copy-start.7 = (bf16[768,4096]{1,0:T(8,128)(2,1)S(1)}, bf16[768,4096]{1,0:T(8,128)(2,1)}, u32[]{:S(2)}) copy-start(bf16[768,4096]{1,0:T(8,128)(2,1)} %constant_dynamic-update-slice_fusion.7) | copy-start | bytes 18874372
  265.9 8.1 %slice-start = ((s8[6291456]{0:T(1024)(128)(4,1)}), s8[4194304]{0:T(1024)(128)(4,1)S(1)}, s32[]{:S(2)}) async-start(s8[6291456]{0:T(1024)(128)(4,1)} %bitcast.82), calls=%async_computation.3 | async-start | bytes 8388608
  274.0 37.3 %copy-start.9 = (bf16[128,1]{0,1:T(2,128)(2,1)S(1)}, bf16[128,1]{0,1:T(2,128)(2,1)}, u32[]{:S(2)}) copy-start(bf16[128,1]{0,1:T(2,128)(2,1)} %param.10) | copy-start | bytes 772
  (8 other events, 26.6 us)
